TPU v7x, 32 devices: a whole 2x2x4 slice. The times are simulated.
32 devices in a mesh: seq: 16 (over z, y, core), heads: 2 (over x).
Axes of the slice: x: 2, y: 2, z: 4, core: 2. Of those that a mesh axis runs over, the one named last changes fastest.
Arguments:
- residual_in: bfloat16 [2048, 3072], P('seq', 'heads'), may hold values from -24 to 24
- self_queries: bfloat16 [2048, 3072], P('seq', 'heads'), may hold values from -170 to 170
- self_keys_values: bfloat16 [2048, 2048], P('seq', 'heads'), may hold values from -5 to 5
- self_out_weight: bfloat16 [3072, 3072], P('seq', 'heads'), may hold values from -0.109375 to 0.109375
- gain_query: float32 [3072], replicated, may hold values from 0.1 to 1.9
- gain_keyvalue: float32 [3072], replicated, may hold values from 0.1 to 1.9
- cross_weight: bfloat16 [3072, 5120], P(None, 'heads')
Outputs:
- hidden: bfloat16 [2048, 3072], P('seq', 'heads')
- cross_attention: bfloat16 [2048, 3072], P('seq', 'heads')
All inputs are finite; a program needn't handle non-finite values.
Results may differ from a plain program's by a relative error of at most 0.02.
Values may be sent and summed in bfloat16 or wider, within the bound.
No kernel may reach another device: no remote copies, remote signals or barrier semaphores. Data moves between devices by JAX's collectives and lax.ppermute only.
A program may use at most 128 MiB of HBM per device.

v0:
```python
import math

import jax
import jax.numpy as jnp
from jax import lax
from jax.sharding import PartitionSpec as P

HD = 128
QPK = 3
WINDOW = 2048


def from_behind(value, axis, steps):
    count = lax.axis_size(axis)
    leading, last = (max(0, -steps), min(count, count - steps))
    return lax.ppermute(value, axis, [(source, source + steps) for source in range(leading, last)])


def attend_piece(state, block_q, query_pos, piece, first_row):
    key_pos = jnp.arange(piece.shape[0], dtype=jnp.int32)
    score_scale = 1.0 / math.sqrt(HD)

    def update(inner):
        old_max, old_sum, old_acc = inner
        blk_scores = (
            jnp.einsum(
                "ngqd,sgd->gqns",
                block_q,
                piece[:, :, 0],
                precision=lax.Precision.HIGHEST,
                preferred_element_type=jnp.float32,
            )
            * score_scale
        )
        allowed = key_pos[None, :] <= query_pos[:, None]
        blk_scores = jnp.where(allowed, blk_scores, -1e30)
        new_max = jnp.maximum(old_max, jnp.max(blk_scores, axis=-1))
        blk_weights = jnp.where(allowed, jnp.exp(blk_scores - new_max[..., None]), 0.0)
        new_sum = jnp.sum(blk_weights, axis=-1)
        new_acc = jnp.einsum(
            "gqns,sgd->gqnd",
            blk_weights,
            piece[:, :, 1],
            precision=lax.Precision.HIGHEST,
            preferred_element_type=jnp.float32,
        )
        return (new_max, new_sum, new_acc)

    def unchanged(inner):
        return inner

    return lax.cond(first_row <= jnp.max(query_pos), update, unchanged, state)


def body(
    residual_in,
    self_queries,
    self_keys_values,
    self_out_weight,
    gain_query,
    gain_keyvalue,
    cross_weight,
):
    tok_rows = residual_in.shape[0]
    groups = self_keys_values.shape[1] // (2 * HD)
    seq_place = lax.axis_index("seq")
    score_scale = 1.0 / math.sqrt(HD)
    window_span = (WINDOW + tok_rows - 2) // tok_rows
    earlier_blocks = []
    for distance in range(window_span, 0, -1):
        earlier_blocks.append(from_behind(self_keys_values, "seq", distance))
    key_window = jnp.concatenate(earlier_blocks + [self_keys_values], axis=0)
    window_rows = key_window.shape[0]
    paired = key_window.reshape(window_rows, groups, 2, HD)
    queries = self_queries.reshape(tok_rows, groups, QPK, HD)
    scores = (
        jnp.einsum("tgqd,sgd->gqts", queries, paired[:, :, 0], preferred_element_type=jnp.float32)
        * score_scale
    )
    query_pos = seq_place * tok_rows + jnp.arange(tok_rows, dtype=jnp.int32)
    key_pos = (
        seq_place * tok_rows - (window_rows - tok_rows) + jnp.arange(window_rows, dtype=jnp.int32)
    )
    allowed = (
        (key_pos[None, :] <= query_pos[:, None])
        & (key_pos[None, :] > query_pos[:, None] - WINDOW)
        & (key_pos[None, :] >= 0)
    )
    masked = jnp.where(allowed, scores, -jnp.inf)
    row_top = jnp.max(masked, axis=-1, keepdims=True)
    weights = jnp.where(allowed, jnp.exp(masked - row_top), 0.0)
    totals = jnp.sum(weights, axis=-1)
    weighted = jnp.einsum(
        "gqts,sgd->tgqd",
        weights.astype(jnp.bfloat16),
        paired[:, :, 1],
        preferred_element_type=jnp.float32,
    )
    attended = (
        (weighted / jnp.transpose(totals, (2, 0, 1))[..., None])
        .astype(jnp.bfloat16)
        .reshape(tok_rows, groups * QPK * HD)
    )
    out_weight = lax.all_gather(self_out_weight, "seq", axis=0, tiled=True)
    projected = jnp.dot(
        lax.all_gather(attended, "heads", axis=1, tiled=True),
        out_weight,
        preferred_element_type=jnp.float32,
    )
    hidden = (residual_in.astype(jnp.float32) + projected).astype(jnp.bfloat16)
    full_rows = lax.all_gather(hidden, "heads", axis=1, tiled=True)
    widened = full_rows.astype(jnp.float32)
    inverse = lax.rsqrt(jnp.mean(widened * widened, axis=-1, keepdims=True) + 1e-06)
    normed_q = (widened * inverse * gain_query).astype(jnp.bfloat16)
    normed_kv = (widened * inverse * gain_keyvalue).astype(jnp.bfloat16)
    col_layout = cross_weight.reshape(cross_weight.shape[0], groups, QPK + 2, HD)
    cross_q = jnp.einsum(
        "td,dgjh->tgjh", normed_q, col_layout[:, :, :QPK], preferred_element_type=jnp.float32
    )
    shared = jnp.einsum(
        "td,dgjh->tgjh", normed_kv, col_layout[:, :, QPK:], preferred_element_type=jnp.float32
    )
    query_sets = [(cross_q, seq_place * tok_rows + jnp.arange(tok_rows, dtype=jnp.int32))]
    initial = tuple(
        (
            (
                jnp.full((groups, QPK, block_q.shape[0]), -1e30, jnp.float32),
                jnp.zeros((groups, QPK, block_q.shape[0]), jnp.float32),
                jnp.zeros((groups, QPK, block_q.shape[0], HD), jnp.float32),
            )
            for block_q, positions in query_sets
        )
    )

    def fold_keys(carried, piece, first_row):
        return tuple(
            (
                attend_piece(state, block_q, positions, piece, first_row)
                for state, (block_q, positions) in zip(carried, query_sets)
            )
        )

    results = fold_keys(
        initial,
        lax.all_gather(shared.astype(jnp.bfloat16), "seq", axis=0, tiled=True).astype(jnp.float32),
        jnp.int32(0),
    )
    finished = []
    for state in results:
        row_count = state[2].shape[2]
        normalized = state[2] / state[1][..., None]
        finished.append(
            jnp.transpose(normalized, (2, 0, 1, 3))
            .reshape(row_count, groups * QPK * HD)
            .astype(jnp.bfloat16)
        )
    cross_attention = finished[0]
    return (hidden, cross_attention)


def solution(mesh):
    return jax.shard_map(
        body,
        mesh=mesh,
        in_specs=(
            P("seq", "heads"),
            P("seq", "heads"),
            P("seq", "heads"),
            P("seq", "heads"),
            P(),
            P(),
            P(None, "heads"),
        ),
        out_specs=(P("seq", "heads"), P("seq", "heads")),
        check_vma=False,
    )
```

profile of v0, /device:TPU:0, one launch (start us, length us, event | category | flops | bytes accessed | tf_op | source)
XLA Modules:
  0.0 314.3 jit_solution(15116221736737763680)
XLA Ops:
  7.2 0.0 all-gather.3.cloned.1.call-start
  7.2 0.7 all-gather.3.cloned.1.call-update
  7.9 0.0 all-gather.5.cloned.1.call-start
  7.9 1.1 copy.16
  9.1 2.4 collective-permute-start.15
  11.5 4.4 %collective-permute-start.14 = (bf16[128,1024]{0,1:T(8,128)(2,1)S(1)}, bf16[128,1024]{0,1:T(8,128)(2,1)S(1)}, u32[]{:S(2)}, u32[]{:S(2)}) collective-permute-start(bf16[128,1024]{0,1:T(8,128)(2,1)S(1)} %copy.16), channel_id=1, source_target_pairs={{0,4},{2,6},{4,8},{6,10},{8,12},{10,14},{12,16},{14,18},{16,20},{1... | collective-permute-start | bytes 786440 | tf_op jit(solution)/shard_map/ppermute | solution.py:16
  15.9 4.3 %collective-permute-start.2 = (bf16[128,1024]{0,1:T(8,128)(2,1)S(1)}, bf16[128,1024]{0,1:T(8,128)(2,1)S(1)}, u32[]{:S(2)}, u32[]{:S(2)}) collective-permute-start(bf16[128,1024]{0,1:T(8,128)(2,1)S(1)} %copy.16), channel_id=1, source_target_pairs={{0,28},{2,30},{1,29},{3,31}} | collective-permute-start | bytes 786440 | tf_op jit(solution)/shard_map/ppermute | solution.py:16
  20.3 1.3 collective-permute-start.1
  21.6 0.7 collective-permute-start
  22.3 1.5 and_and_fusion
  23.9 1.2 copy.35
  25.1 20.7 %copy.38 = bf16[3072,2560]{0,1:T(8,128)(2,1)} copy(bf16[3072,2560]{1,0:T(8,128)(2,1)} %param.15) | data formatting | bytes 31457280 | tf_op args[6]
  45.8 1.3 collective-permute-start.3
  47.1 1.3 collective-permute-start.4
  48.4 0.1 constant_dynamic-update-slice_fusion.15
  48.5 1.3 collective-permute-start.5
  49.8 0.1 constant_dynamic-update-slice_fusion.14
  49.9 3.9 %collective-permute-done.3 = bf16[128,1024]{0,1:T(8,128)(2,1)S(1)} collective-permute-done((bf16[128,1024]{0,1:T(8,128)(2,1)S(1)}, bf16[128,1024]{0,1:T(8,128)(2,1)S(1)}, u32[]{:S(2)}, u32[]{:S(2)}) %collective-permute-start.3) | collective-permute-done | bytes 262176 | tf_op jit(solution)/shard_map/ppermute | solution.py:16
  53.8 1.3 collective-permute-start.6
  55.1 0.1 constant_dynamic-update-slice_fusion.13
  55.2 8.6 %collective-permute-done.4 = bf16[128,1024]{0,1:T(8,128)(2,1)S(1)} collective-permute-done((bf16[128,1024]{0,1:T(8,128)(2,1)S(1)}, bf16[128,1024]{0,1:T(8,128)(2,1)S(1)}, u32[]{:S(2)}, u32[]{:S(2)}) %collective-permute-start.4) | collective-permute-done | bytes 262176 | tf_op jit(solution)/shard_map/ppermute | solution.py:16
  63.8 1.3 collective-permute-start.7
  65.1 0.1 constant_dynamic-update-slice_fusion.12
  65.1 9.9 %collective-permute-done.5 = bf16[128,1024]{0,1:T(8,128)(2,1)S(1)} collective-permute-done((bf16[128,1024]{0,1:T(8,128)(2,1)S(1)}, bf16[128,1024]{0,1:T(8,128)(2,1)S(1)}, u32[]{:S(2)}, u32[]{:S(2)}) %collective-permute-start.5) | collective-permute-done | bytes 262176 | tf_op jit(solution)/shard_map/ppermute | solution.py:16
  75.0 1.3 collective-permute-start.8
  76.3 0.1 constant_dynamic-update-slice_fusion.11
  76.4 9.9 %collective-permute-done.6 = bf16[128,1024]{0,1:T(8,128)(2,1)S(1)} collective-permute-done((bf16[128,1024]{0,1:T(8,128)(2,1)S(1)}, bf16[128,1024]{0,1:T(8,128)(2,1)S(1)}, u32[]{:S(2)}, u32[]{:S(2)}) %collective-permute-start.6) | collective-permute-done | bytes 262176 | tf_op jit(solution)/shard_map/ppermute | solution.py:16
  86.2 21.6 %collective-permute-start.9 = (bf16[128,1024]{0,1:T(8,128)(2,1)S(1)}, bf16[128,1024]{0,1:T(8,128)(2,1)S(1)}, u32[]{:S(2)}, u32[]{:S(2)}) collective-permute-start(bf16[128,1024]{0,1:T(8,128)(2,1)S(1)} %copy.16), channel_id=1, source_target_pairs={{0,14},{2,16},{4,18},{6,20},{8,22},{10,24},{12,26},{14,28},{16,30}... | collective-permute-start | bytes 786440 | tf_op jit(solution)/shard_map/ppermute | solution.py:16
  107.8 0.1 constant_dynamic-update-slice_fusion.10
  107.9 1.3 collective-permute-start.10
  109.2 0.1 constant_dynamic-update-slice_fusion.9
  109.3 30.0 %collective-permute-start.11 = (bf16[128,1024]{0,1:T(8,128)(2,1)S(1)}, bf16[128,1024]{0,1:T(8,128)(2,1)S(1)}, u32[]{:S(2)}, u32[]{:S(2)}) collective-permute-start(bf16[128,1024]{0,1:T(8,128)(2,1)S(1)} %copy.16), channel_id=1, source_target_pairs={{0,10},{2,12},{4,14},{6,16},{8,18},{10,20},{12,22},{14,24},{16,26}... | collective-permute-start | bytes 786440 | tf_op jit(solution)/shard_map/ppermute | solution.py:16
  139.3 0.1 constant_dynamic-update-slice_fusion.8
  139.4 13.3 %collective-permute-start.12 = (bf16[128,1024]{0,1:T(8,128)(2,1)S(1)}, bf16[128,1024]{0,1:T(8,128)(2,1)S(1)}, u32[]{:S(2)}, u32[]{:S(2)}) collective-permute-start(bf16[128,1024]{0,1:T(8,128)(2,1)S(1)} %copy.16), channel_id=1, source_target_pairs={{0,8},{2,10},{4,12},{6,14},{8,16},{10,18},{12,20},{14,22},{16,24},... | collective-permute-start | bytes 786440 | tf_op jit(solution)/shard_map/ppermute | solution.py:16
  152.8 0.1 constant_dynamic-update-slice_fusion.7
  152.8 2.8 collective-permute-start.13
  155.6 0.1 constant_dynamic-update-slice_fusion.6
  155.7 0.1 constant_dynamic-update-slice_fusion.5
  155.8 0.8 collective-permute-done.12
  156.6 0.1 constant_dynamic-update-slice_fusion.4
  156.7 2.6 collective-permute-done.13
  159.3 0.1 constant_dynamic-update-slice_fusion.3
  159.4 0.1 constant_dynamic-update-slice_fusion.2
  159.5 0.1 constant_dynamic-update-slice_fusion.1
  159.5 0.1 constant_dynamic-update-slice_fusion
  159.6 2.0 copy-done.3
  161.7 6.7 %fusion.58 = f32[4,3,128]{2,1,0:T(4,128)S(1)} fusion(pred[128,2176]{0,1:T(8,128)(4,1)S(1)} %and_and_fusion, bf16[128,4,3,128]{0,3,2,1:T(8,128)(2,1)S(1)} %bitcast.99, bf16[2176,4,2,128]{0,3,2,1:T(8,128)(2,1)} %bitcast.102), kind=kOutput, calls=%fused_computation.83 | convolution fusion | flops 872351872 | bytes 3184640 | tf_op jit(solution)/shard_map/sub | solution.py:91
  168.3 8.2 %fusion.36 = bf16[128,4,3,128]{0,3,2,1:T(8,128)(2,1)S(1)} fusion(bf16[2176,4,2,128]{0,3,2,1:T(8,128)(2,1)} %bitcast.103, f32[128,4,3]{0,2,1:T(4,128)S(1)} %bitcast.104, pred[128,2176]{0,1:T(8,128)(4,1)S(1)} %and_and_fusion, bf16[128,4,3,128]{0,3,2,1:T(8,128)(2,1)S(1)} %bitcast.100), kind=kOutput, calls=%fused_computation.45 | convolution fusion | flops 1728384640 | bytes 5808128 | tf_op jit(solution)/shard_map/gqts,sgd->tgqd/dot_general | solution.py:93
  176.6 11.1 %all_gather.12 = bf16[128,3072]{0,1:T(8,128)(2,1)S(1)} all-gather(bf16[128,1536]{0,1:T(8,128)(2,1)S(1)} %bitcast.101), channel_id=1, replica_groups=mesh['seq'=16,'heads'=2] {'heads'}, dimensions={1}, use_global_device_ids=true | all-gather | bytes 1179648 | tf_op jit(solution)/shard_map/all_gather | solution.py:106
  187.7 5.1 %fusion.23 = bf16[128,1536]{1,0:T(8,128)(2,1)S(1)} fusion(bf16[128,3072]{0,1:T(8,128)(2,1)S(1)} %all_gather.12, bf16[3072,1536]{1,0:T(8,128)(2,1)} %all-gather.3.cloned.1.call-done, bf16[128,1536]{1,0:T(8,128)(2,1)S(1)} %copy-done.2), kind=kOutput, calls=%fused_computation.32 | convolution fusion | flops 1208549376 | bytes 11010048 | tf_op jit(solution)/shard_map/dot_general | solution.py:105
  192.9 12.5 %all_gather.14 = bf16[128,3072]{1,0:T(8,128)(2,1)S(1)} all-gather(bf16[128,1536]{1,0:T(8,128)(2,1)S(1)} %fusion.23), channel_id=1, replica_groups=mesh['seq'=16,'heads'=2] {'heads'}, dimensions={1}, use_global_device_ids=true | all-gather | bytes 1179648 | tf_op jit(solution)/shard_map/all_gather | solution.py:111
  205.4 0.2 fusion.29
  205.7 5.7 %fusion.39 = bf16[128,4,2,128]{3,0,2,1:T(8,128)(2,1)} fusion(bf16[3072,4,5,128]{0,3,2,1:T(8,128)(2,1)} %bitcast.96, bf16[128,3072]{1,0:T(8,128)(2,1)S(1)} %all_gather.14, f32[3072]{0:T(1024)S(1)} %copy-done.4, f32[128]{0:T(128)S(1)} %add_rsqrt_fusion), kind=kOutput, calls=%fused_computation.46 | convolution fusion | flops 807010304 | bytes 7352832 | tf_op jit(solution)/shard_map/td,dgjh->tgjh/dot_general | solution.py:120
  211.4 0.7 fusion.57
  212.7 5.8 %fusion.14 = f32[128,4,3,128]{3,0,2,1:T(8,128)S(1)} fusion(bf16[3072,4,5,128]{0,3,2,1:T(8,128)(2,1)} %bitcast.97, bf16[128,3072]{1,0:T(8,128)(2,1)S(1)} %all_gather.14, f32[3072]{0:T(1024)S(1)} %copy-done.5, f32[128]{0:T(128)S(1)} %add_rsqrt_fusion), kind=kOutput, calls=%fused_computation.22 | convolution fusion | flops 1209532416 | bytes 11022848 | tf_op jit(solution)/shard_map/td,dgjh->tgjh/dot_general | solution.py:117
  218.5 48.3 %all-gather.5.cloned.1.call-done = bf16[2048,4,2,128]{3,0,2,1:T(8,128)(2,1)} async-done(((bf16[128,4,2,128]{3,0,2,1:T(8,128)(2,1)}), bf16[2048,4,2,128]{3,0,2,1:T(8,128)(2,1)}) %all-gather.5.cloned.1.call-update) | async-done | bytes 4194320 | tf_op jit(solution)/shard_map/all_gather | solution.py:145
  266.7 2.7 convert_element_type.47
  269.5 36.9 %conditional.1 = (f32[4,3,128]{2,1,0:T(4,128)S(1)}, f32[4,3,128,128]{2,3,1,0:T(8,128)S(1)}) conditional(s32[]{:T(128)} %convert_element_type.43, () %tuple.16, (s32[2048]{0:T(1024)S(1)}, s32[128]{0:T(128)S(1)}, f32[2048,4,2,128]{3,0,2,1:T(8,128)S(1)}, f32[128,4,3,128]{3,0,2,1:T(8,128)S(1)}) %tuple.17), branch_computations={%region_4.5_spmd, %region_5.8_spmd} | conditional | flops 9701685248 | bytes 82358832 | solution.py:52
  269.5 0.3 broadcast_compare_fusion
  269.9 14.3 %fusion = (f32[4,3,128]{2,1,0:T(4,128)S(1)}, f32[4,2048,128,3]{2,1,3,0:T(8,128)}) fusion(pred[128,2048]{0,1:T(8,128)(4,1)S(1)} %broadcast_compare_fusion, f32[128,4,3,128]{3,0,2,1:T(8,128)S(1)} %get-tuple-element.11, f32[2048,4,2,128]{3,0,2,1:T(8,128)S(1)} %get-tuple-element.24), kind=kOutput, calls=%fused_computation.2 | convolution fusion | flops 4841273856 | bytes 17831936 | tf_op jit(solution)/shard_map/cond/branch_1_fun/ngqd,sgd->gqns/dot_general | solution.py:26
  284.2 15.7 %fusion.1 = f32[4,3,128,128]{2,3,1,0:T(8,128)S(1)} fusion(f32[4,2048,128,3]{2,1,3,0:T(8,128)} %get-tuple-element.30, f32[4,3,128]{2,1,0:T(4,128)S(1)} %broadcast_maximum_fusion, pred[128,2048]{0,1:T(8,128)(4,1)S(1)} %broadcast_compare_fusion, f32[2048,4,2,128]{3,0,2,1:T(8,128)} %copy-done), kind=kOutput, calls=%fused_computation.3 | convolution fusion | flops 4844421120 | bytes 17831936 | tf_op jit(solution)/shard_map/cond | solution.py:52
  299.9 6.5 %fusion.2 = f32[4,3,128]{2,1,0:T(4,128)S(1)} fusion(f32[4,2048,128,3]{2,1,3,0:T(8,128)} %get-tuple-element.30, f32[4,3,128]{2,1,0:T(4,128)S(1)} %broadcast_maximum_fusion, pred[128,2048]{0,1:T(8,128)(4,1)S(1)} %broadcast_compare_fusion), kind=kLoop, calls=%fused_computation.4 | loop fusion | flops 15727104 | bytes 12857344 | tf_op jit(solution)/shard_map/cond/branch_1_fun/reduce_sum | solution.py:39
  306.4 0.1 divide_convert_fusion
  306.5 0.9 copy.43
  (30 shorter events, 0.2 us)
Async XLA Ops:
  7.2 180.6 %all-gather.3.cloned.1.call-start = ((), (), s32[]{:S(2)}) async-start(), calls=%async_computation | async-start | bytes 10027008 | tf_op jit(solution)/shard_map/all_gather | solution.py:104
  7.9 258.9 %all-gather.5.cloned.1.call-start = ((), (), s32[]{:S(2)}) async-start(), calls=%async_computation.1 | async-start | bytes 4456448 | tf_op jit(solution)/shard_map/all_gather | solution.py:145
  9.1 150.4 %collective-permute-start.15 = (bf16[128,1024]{0,1:T(8,128)(2,1)S(1)}, bf16[128,1024]{0,1:T(8,128)(2,1)S(1)}, u32[]{:S(2)}, u32[]{:S(2)}) collective-permute-start(bf16[128,1024]{0,1:T(8,128)(2,1)S(1)} %copy.16), channel_id=1, source_target_pairs={{0,2},{2,4},{4,6},{6,8},{8,10},{10,12},{12,14},{14,16},{16,18},{18... | collective-permute-start | bytes 786440 | tf_op jit(solution)/shard_map/ppermute | solution.py:16
  11.5 147.9 %collective-permute-start.14 = (bf16[128,1024]{0,1:T(8,128)(2,1)S(1)}, bf16[128,1024]{0,1:T(8,128)(2,1)S(1)}, u32[]{:S(2)}, u32[]{:S(2)}) collective-permute-start(bf16[128,1024]{0,1:T(8,128)(2,1)S(1)} %copy.16), channel_id=1, source_target_pairs={{0,4},{2,6},{4,8},{6,10},{8,12},{10,14},{12,16},{14,18},{16,20},{1... | collective-permute-start | bytes 786440 | tf_op jit(solution)/shard_map/ppermute | solution.py:16
  15.9 32.6 %collective-permute-start.2 = (bf16[128,1024]{0,1:T(8,128)(2,1)S(1)}, bf16[128,1024]{0,1:T(8,128)(2,1)S(1)}, u32[]{:S(2)}, u32[]{:S(2)}) collective-permute-start(bf16[128,1024]{0,1:T(8,128)(2,1)S(1)} %copy.16), channel_id=1, source_target_pairs={{0,28},{2,30},{1,29},{3,31}} | collective-permute-start | bytes 786440 | tf_op jit(solution)/shard_map/ppermute | solution.py:16
  20.3 26.9 %collective-permute-start.1 = (bf16[128,1024]{0,1:T(8,128)(2,1)S(1)}, bf16[128,1024]{0,1:T(8,128)(2,1)S(1)}, u32[]{:S(2)}, u32[]{:S(2)}) collective-permute-start(bf16[128,1024]{0,1:T(8,128)(2,1)S(1)} %copy.16), channel_id=1, source_target_pairs={{0,30},{1,31}} | collective-permute-start | bytes 786440 | tf_op jit(solution)/shard_map/ppermute | solution.py:16
  21.6 24.2 %collective-permute-start = (bf16[128,1024]{0,1:T(8,128)(2,1)S(1)}, bf16[128,1024]{0,1:T(8,128)(2,1)S(1)}, u32[]{:S(2)}, u32[]{:S(2)}) collective-permute-start(bf16[128,1024]{0,1:T(8,128)(2,1)S(1)} %copy.16), channel_id=1, source_target_pairs={} | collective-permute-start | bytes 786440 | tf_op jit(solution)/shard_map/ppermute | solution.py:16
  45.8 8.0 %collective-permute-start.3 = (bf16[128,1024]{0,1:T(8,128)(2,1)S(1)}, bf16[128,1024]{0,1:T(8,128)(2,1)S(1)}, u32[]{:S(2)}, u32[]{:S(2)}) collective-permute-start(bf16[128,1024]{0,1:T(8,128)(2,1)S(1)} %copy.16), channel_id=1, source_target_pairs={{0,26},{2,28},{4,30},{1,27},{3,29},{5,31}} | collective-permute-start | bytes 786440 | tf_op jit(solution)/shard_map/ppermute | solution.py:16
  47.1 16.7 %collective-permute-start.4 = (bf16[128,1024]{0,1:T(8,128)(2,1)S(1)}, bf16[128,1024]{0,1:T(8,128)(2,1)S(1)}, u32[]{:S(2)}, u32[]{:S(2)}) collective-permute-start(bf16[128,1024]{0,1:T(8,128)(2,1)S(1)} %copy.16), channel_id=1, source_target_pairs={{0,24},{2,26},{4,28},{6,30},{1,25},{3,27},{5,29},{7,31}} | collective-permute-start | bytes 786440 | tf_op jit(solution)/shard_map/ppermute | solution.py:16
  48.5 26.5 %collective-permute-start.5 = (bf16[128,1024]{0,1:T(8,128)(2,1)S(1)}, bf16[128,1024]{0,1:T(8,128)(2,1)S(1)}, u32[]{:S(2)}, u32[]{:S(2)}) collective-permute-start(bf16[128,1024]{0,1:T(8,128)(2,1)S(1)} %copy.16), channel_id=1, source_target_pairs={{0,22},{2,24},{4,26},{6,28},{8,30},{1,23},{3,25},{5,27},{7,29},{9,... | collective-permute-start | bytes 786440 | tf_op jit(solution)/shard_map/ppermute | solution.py:16
  53.8 32.5 %collective-permute-start.6 = (bf16[128,1024]{0,1:T(8,128)(2,1)S(1)}, bf16[128,1024]{0,1:T(8,128)(2,1)S(1)}, u32[]{:S(2)}, u32[]{:S(2)}) collective-permute-start(bf16[128,1024]{0,1:T(8,128)(2,1)S(1)} %copy.16), channel_id=1, source_target_pairs={{0,20},{2,22},{4,24},{6,26},{8,28},{10,30},{1,21},{3,23},{5,25},{7... | collective-permute-start | bytes 786440 | tf_op jit(solution)/shard_map/ppermute | solution.py:16
  63.8 44.1 %collective-permute-start.7 = (bf16[128,1024]{0,1:T(8,128)(2,1)S(1)}, bf16[128,1024]{0,1:T(8,128)(2,1)S(1)}, u32[]{:S(2)}, u32[]{:S(2)}) collective-permute-start(bf16[128,1024]{0,1:T(8,128)(2,1)S(1)} %copy.16), channel_id=1, source_target_pairs={{0,18},{2,20},{4,22},{6,24},{8,26},{10,28},{12,30},{1,19},{3,21},{... | collective-permute-start | bytes 786440 | tf_op jit(solution)/shard_map/ppermute | solution.py:16
  75.0 34.3 %collective-permute-start.8 = (bf16[128,1024]{0,1:T(8,128)(2,1)S(1)}, bf16[128,1024]{0,1:T(8,128)(2,1)S(1)}, u32[]{:S(2)}, u32[]{:S(2)}) collective-permute-start(bf16[128,1024]{0,1:T(8,128)(2,1)S(1)} %copy.16), channel_id=1, source_target_pairs={{0,16},{2,18},{4,20},{6,22},{8,24},{10,26},{12,28},{14,30},{1,17},... | collective-permute-start | bytes 786440 | tf_op jit(solution)/shard_map/ppermute | solution.py:16
  86.2 53.2 %collective-permute-start.9 = (bf16[128,1024]{0,1:T(8,128)(2,1)S(1)}, bf16[128,1024]{0,1:T(8,128)(2,1)S(1)}, u32[]{:S(2)}, u32[]{:S(2)}) collective-permute-start(bf16[128,1024]{0,1:T(8,128)(2,1)S(1)} %copy.16), channel_id=1, source_target_pairs={{0,14},{2,16},{4,18},{6,20},{8,22},{10,24},{12,26},{14,28},{16,30}... | collective-permute-start | bytes 786440 | tf_op jit(solution)/shard_map/ppermute | solution.py:16
  107.9 44.9 %collective-permute-start.10 = (bf16[128,1024]{0,1:T(8,128)(2,1)S(1)}, bf16[128,1024]{0,1:T(8,128)(2,1)S(1)}, u32[]{:S(2)}, u32[]{:S(2)}) collective-permute-start(bf16[128,1024]{0,1:T(8,128)(2,1)S(1)} %copy.16), channel_id=1, source_target_pairs={{0,12},{2,14},{4,16},{6,18},{8,20},{10,22},{12,24},{14,26},{16,28}... | collective-permute-start | bytes 786440 | tf_op jit(solution)/shard_map/ppermute | solution.py:16
  109.3 46.4 %collective-permute-start.11 = (bf16[128,1024]{0,1:T(8,128)(2,1)S(1)}, bf16[128,1024]{0,1:T(8,128)(2,1)S(1)}, u32[]{:S(2)}, u32[]{:S(2)}) collective-permute-start(bf16[128,1024]{0,1:T(8,128)(2,1)S(1)} %copy.16), channel_id=1, source_target_pairs={{0,10},{2,12},{4,14},{6,16},{8,18},{10,20},{12,22},{14,24},{16,26}... | collective-permute-start | bytes 786440 | tf_op jit(solution)/shard_map/ppermute | solution.py:16
  139.4 17.2 %collective-permute-start.12 = (bf16[128,1024]{0,1:T(8,128)(2,1)S(1)}, bf16[128,1024]{0,1:T(8,128)(2,1)S(1)}, u32[]{:S(2)}, u32[]{:S(2)}) collective-permute-start(bf16[128,1024]{0,1:T(8,128)(2,1)S(1)} %copy.16), channel_id=1, source_target_pairs={{0,8},{2,10},{4,12},{6,14},{8,16},{10,18},{12,20},{14,22},{16,24},... | collective-permute-start | bytes 786440 | tf_op jit(solution)/shard_map/ppermute | solution.py:16
  152.8 6.4 %collective-permute-start.13 = (bf16[128,1024]{0,1:T(8,128)(2,1)S(1)}, bf16[128,1024]{0,1:T(8,128)(2,1)S(1)}, u32[]{:S(2)}, u32[]{:S(2)}) collective-permute-start(bf16[128,1024]{0,1:T(8,128)(2,1)S(1)} %copy.16), channel_id=1, source_target_pairs={{0,6},{2,8},{4,10},{6,12},{8,14},{10,16},{12,18},{14,20},{16,22},{... | collective-permute-start | bytes 786440 | tf_op jit(solution)/shard_map/ppermute | solution.py:16
  159.6 2.1 copy-start.3
  168.3 19.4 %copy-start.2 = (bf16[128,1536]{1,0:T(8,128)(2,1)S(1)}, bf16[128,1536]{1,0:T(8,128)(2,1)}, u32[]{:S(2)}) copy-start(bf16[128,1536]{1,0:T(8,128)(2,1)} %param.9) | copy-start | bytes 1179652
  187.7 17.9 %copy-start.4 = (f32[3072]{0:T(1024)S(1)}, f32[3072]{0:T(1024)}, u32[]{:S(2)}) copy-start(f32[3072]{0:T(1024)} %param.14) | copy-start | bytes 36868
  192.8 18.5 %copy-start.1 = (bf16[128,1536]{1,0:T(8,128)(2,1)}, bf16[128,1536]{1,0:T(8,128)(2,1)S(1)}, u32[]{:S(2)}) copy-start(bf16[128,1536]{1,0:T(8,128)(2,1)S(1)} %fusion.23) | copy-start | bytes 1179652
  205.6 7.1 %copy-start.5 = (f32[3072]{0:T(1024)S(1)}, f32[3072]{0:T(1024)}, u32[]{:S(2)}) copy-start(f32[3072]{0:T(1024)} %param.13) | copy-start | bytes 36868
  269.5 14.7 %copy-start = (f32[2048,4,2,128]{3,0,2,1:T(8,128)}, f32[2048,4,2,128]{3,0,2,1:T(8,128)S(1)}, u32[]{:S(2)}) copy-start(f32[2048,4,2,128]{3,0,2,1:T(8,128)S(1)} %get-tuple-element.24) | copy-start | bytes 25165828 | tf_op jit(solution)/shard_map/cond
Sparse Core Ops, SparseCore 0:
  10.3 116.7 all-gather.2
  211.5 55.1 all-gather.4
where the time goes:
time: 315 us; the launch traced here: 314 us
  starting transfers between devices  90 us (29%)
  waiting for transfers between devices  84.7 us (27%)
  matrix products  61.5 us (20%)
  local copies, waits for them, and re-layouts  27.1 us (9%)
  blocking collectives  23.7 us (8%)
  between operations  15.1 us (5%)
  other arithmetic  12.2 us (4%)
    ppermute x16, starting transfers between devices, from_behind(): lax.ppermute(value, axis, [(source, source + steps) for source in range(l...  89.9 us
    all_gather x1, waiting for transfers between devices, body(): lax.all_gather(shared.astype(jnp.bfloat16), 'seq', axis=0, tiled=True)  48.3 us
    ppermute x16, waiting for transfers between devices, from_behind(): lax.ppermute(value, axis, [(source, source + steps) for source in range(l...  35.7 us
    unnamed x30, local copies, waits for them, and re-layouts  27 us
    cond x1, matrix products, attend_piece(): return lax.cond(first_row <= jnp.max(query_pos), update, unchanged, state)  15.7 us
    dot_general x1, matrix products, update(): jnp.einsum('ngqd,sgd->gqns', block_q, piece[:, :, 0], precision=lax.Preci...  14.3 us
    all_gather x1, blocking collectives, body(): full_rows = lax.all_gather(hidden, 'heads', axis=1, tiled=True)  12.5 us
    all_gather x1, blocking collectives, body(): lax.all_gather(attended, 'heads', axis=1, tiled=True)  11.1 us
  transfers between devices with their start and end apart: 18, of which 7 were waited for; matrix products, arithmetic and copies ran while one was open for 15% of the time, Pallas kernels for 0%

commit v1 on v0

v1 whole, which is shorter than its diff:
```python
import functools
import math

import jax
import jax.numpy as jnp
from jax import lax
from jax.experimental import pallas as pl
from jax.experimental.pallas import tpu as pltpu
from jax.sharding import PartitionSpec as P

HD = 128
QPK = 3
WINDOW = 2048


def _split(x):
    high = x.astype(jnp.bfloat16)
    low = (x - high.astype(jnp.float32)).astype(jnp.bfloat16)
    return high, low


def _attend_kernel(pos_ref, q_ref, kv_ref, o_ref, *, window, exact):
    rows = q_ref.shape[0]
    keys = kv_ref.shape[0]
    first = pos_ref[0]
    query_pos = first + lax.broadcasted_iota(jnp.int32, (rows, keys), 0)
    key_pos = lax.broadcasted_iota(jnp.int32, (rows, keys), 1)
    allowed = key_pos <= query_pos
    if window is not None:
        allowed = allowed & (key_pos > query_pos - window)
    key = kv_ref[:, :HD]
    value = kv_ref[:, HD:]
    score_scale = 1.0 / math.sqrt(HD)
    contract = (((1,), (1,)), ((), ()))
    for head in range(q_ref.shape[1] // HD):
        query = q_ref[:, head * HD:(head + 1) * HD]
        if exact:
            q_hi, q_lo = _split(query.astype(jnp.float32))
            scores = lax.dot_general(q_hi, key, contract, preferred_element_type=jnp.float32)
            scores = scores + lax.dot_general(q_lo, key, contract, preferred_element_type=jnp.float32)
        else:
            scores = lax.dot_general(query, key, contract, preferred_element_type=jnp.float32)
        scores = scores * score_scale
        masked = jnp.where(allowed, scores, -jnp.inf)
        row_top = jnp.max(masked, axis=-1, keepdims=True)
        weights = jnp.where(allowed, jnp.exp(masked - row_top), 0.0)
        totals = jnp.sum(weights, axis=-1, keepdims=True)
        if exact:
            w_hi, w_lo = _split(weights)
            acc = jnp.dot(w_hi, value, preferred_element_type=jnp.float32)
            acc = acc + jnp.dot(w_lo, value, preferred_element_type=jnp.float32)
        else:
            acc = jnp.dot(weights.astype(jnp.bfloat16), value, preferred_element_type=jnp.float32)
        o_ref[:, head * HD:(head + 1) * HD] = (acc / totals).astype(o_ref.dtype)


def attend(first_pos, queries, pairs, window, exact):
    rows, qcols = queries.shape
    keys, kvcols = pairs.shape
    groups = kvcols // (2 * HD)
    qblock = qcols // groups
    kernel = functools.partial(_attend_kernel, window=window, exact=exact)
    return pl.pallas_call(
        kernel,
        out_shape=jax.ShapeDtypeStruct((rows, qcols), jnp.bfloat16),
        grid_spec=pltpu.PrefetchScalarGridSpec(
            num_scalar_prefetch=1,
            grid=(groups,),
            in_specs=[
                pl.BlockSpec((rows, qblock), lambda g, pos: (0, g)),
                pl.BlockSpec((keys, 2 * HD), lambda g, pos: (0, g)),
            ],
            out_specs=pl.BlockSpec((rows, qblock), lambda g, pos: (0, g)),
        ),
    )(first_pos, queries, pairs)


def make_body(heads_count):
    def gather_heads(x):
        if heads_count == 2:
            other = lax.ppermute(x, "heads", [(0, 1), (1, 0)])
            first = lax.axis_index("heads") == 0
            low = jnp.where(first, x, other)
            high = jnp.where(first, other, x)
            return jnp.concatenate([low, high], axis=1)
        return lax.all_gather(x, "heads", axis=1, tiled=True)

    def body(
        residual_in,
        self_queries,
        self_keys_values,
        self_out_weight,
        gain_query,
        gain_keyvalue,
        cross_weight,
    ):
        tok_rows = residual_in.shape[0]
        groups = self_keys_values.shape[1] // (2 * HD)
        seq_place = lax.axis_index("seq")
        first_pos = (seq_place * tok_rows).astype(jnp.int32).reshape(1)

        key_window = lax.all_gather(self_keys_values, "seq", axis=0, tiled=True)
        attended = attend(first_pos, self_queries, key_window, WINDOW, False)

        out_weight = lax.all_gather(self_out_weight, "seq", axis=0, tiled=True)
        projected = jnp.dot(
            gather_heads(attended), out_weight, preferred_element_type=jnp.float32
        )
        hidden = (residual_in.astype(jnp.float32) + projected).astype(jnp.bfloat16)
        full_rows = gather_heads(hidden)
        widened = full_rows.astype(jnp.float32)
        inverse = lax.rsqrt(jnp.mean(widened * widened, axis=-1, keepdims=True) + 1e-06)
        normed_q = (widened * inverse * gain_query).astype(jnp.bfloat16)
        normed_kv = (widened * inverse * gain_keyvalue).astype(jnp.bfloat16)
        both = jnp.dot(
            jnp.concatenate([normed_q, normed_kv], axis=0),
            cross_weight,
            preferred_element_type=jnp.float32,
        ).reshape(2 * tok_rows, groups, QPK + 2, HD)
        cross_q = both[:tok_rows, :, :QPK].reshape(tok_rows, groups * QPK * HD)
        shared = both[tok_rows:, :, QPK:].reshape(tok_rows, groups * 2 * HD)
        shared_all = lax.all_gather(shared.astype(jnp.bfloat16), "seq", axis=0, tiled=True)
        cross_attention = attend(first_pos, cross_q, shared_all, None, True)
        return (hidden, cross_attention)

    return body


def solution(mesh):
    return jax.shard_map(
        make_body(mesh.shape["heads"]),
        mesh=mesh,
        in_specs=(
            P("seq", "heads"),
            P("seq", "heads"),
            P("seq", "heads"),
            P("seq", "heads"),
            P(),
            P(),
            P(None, "heads"),
        ),
        out_specs=(P("seq", "heads"), P("seq", "heads")),
        check_vma=False,
    )
```

time: 315 us -> 246 us (0.78)
  waiting for transfers between devices: 84.7 us -> 180 us
  starting transfers between devices: 90 us -> 3.13 us
  matrix products: 61.5 us -> 16.3 us
  Pallas kernels: 0 us -> 25.6 us
  blocking collectives: 23.7 us -> 0 us
  local copies, waits for them, and re-layouts: 27.1 us -> 4.35 us
  other arithmetic: 12.2 us -> 1.73 us
    ppermute x16 -> x2, starting transfers between devices: 89.9 us -> 3.01 us  [gather_heads(): other = lax.ppermute(x, 'heads', [(0, 1), (1, 0)])]
    all_gather x1, waiting for transfers between devices: 0.01 us -> 58 us  [body(): out_weight = lax.all_gather(self_out_weight, 'seq', axis=0, tiled=True)]
    all_gather x0 -> x1, waiting for transfers between devices: none -> 54.6 us  [body(): key_window = lax.all_gather(self_keys_values, 'seq', axis=0, tiled=True)]
    unnamed x30 -> x8, local copies, waits for them, and re-layouts: 27 us -> 0.02 us
    pallas_call x0 -> x2, Pallas kernels: none -> 25.6 us  [attend(): pl.pallas_call(kernel, out_shape=jax.ShapeDtypeStruct((rows, qcols), jnp....]
    all_gather x2 -> x0, blocking collectives: 23.7 us -> none  [the longest x1 12.5 us: body(): full_rows = lax.all_gather(hidden, 'heads', axis=1, tiled=True)]
    dot_general x5 -> x2, matrix products: 39.1 us -> 16.3 us  [the longest x1 11.2 us: body(): jnp.dot(jnp.concatenate([normed_q, normed_kv], axis=0), cross_weight, pre...]
    ppermute x16 -> x2, waiting for transfers between devices: 35.7 us -> 19.8 us  [gather_heads(): other = lax.ppermute(x, 'heads', [(0, 1), (1, 0)])]
  transfers between devices with their start and end apart: 18 -> 5, of which waited for: 7 -> 5; matrix products, arithmetic and copies ran while one was open for 15% -> 1% of each run, Pallas kernels for 0% -> 5%
where the time goes in v1:
time: 246 us; the launch traced here: 245 us
  waiting for transfers between devices  180 us (73%)
  Pallas kernels  25.6 us (10%)
  matrix products  16.3 us (7%)
  between operations  13.8 us (6%)
  local copies, waits for them, and re-layouts  4.35 us (2%)
  starting transfers between devices  3.13 us (1%)
    all_gather x1, waiting for transfers between devices, body(): out_weight = lax.all_gather(self_out_weight, 'seq', axis=0, tiled=True)  58 us
    all_gather x1, waiting for transfers between devices, body(): key_window = lax.all_gather(self_keys_values, 'seq', axis=0, tiled=True)  54.6 us
    all_gather x1, waiting for transfers between devices, body(): lax.all_gather(shared.astype(jnp.bfloat16), 'seq', axis=0, tiled=True)  46.6 us
    pallas_call x2, Pallas kernels, attend(): pl.pallas_call(kernel, out_shape=jax.ShapeDtypeStruct((rows, qcols), jnp....  25.6 us
    ppermute x2, waiting for transfers between devices, gather_heads(): other = lax.ppermute(x, 'heads', [(0, 1), (1, 0)])  19.8 us
    dot_general x1, matrix products, body(): jnp.dot(jnp.concatenate([normed_q, normed_kv], axis=0), cross_weight, pre...  11.2 us
    dot_general x1, matrix products, body(): jnp.dot(gather_heads(attended), out_weight, preferred_element_type=jnp.fl...  5.07 us
  transfers between devices with their start and end apart: 5, of which 5 were waited for; matrix products, arithmetic and copies ran while one was open for 1% of the time, Pallas kernels for 5%

profile of v1, /device:TPU:0, one launch (start us, length us, event | category | flops | bytes accessed | tf_op | source)
XLA Modules:
  0.0 245.2 jit_solution(14808382288571034579)
XLA Ops:
  7.2 0.0 all-gather.4.cloned.1.call-start
  7.2 0.7 all-gather.4.cloned.1.call-update
  7.9 0.0 all-gather.6.cloned.1.call-start
  7.9 0.7 all-gather.6.cloned.1.call-update
  8.6 0.0 all-gather.8.cloned.1.call-start
  8.7 54.6 %all-gather.4.cloned.1.call-done.kv_ref = bf16[2048,1024]{1,0:T(8,128)(2,1)} async-done(((bf16[128,1024]{1,0:T(8,128)(2,1)}), bf16[2048,1024]{1,0:T(8,128)(2,1)}) %all-gather.4.cloned.1.call-update) | async-done | bytes 4194320 | tf_op jit(solution)/shard_map/all_gather | solution.py:102
  63.3 11.2 %shard_map.86 = bf16[128,1536]{1,0:T(8,128)(2,1)} custom-call(s32[1]{0:T(128)} %bitcast.pos_ref, bf16[128,1536]{1,0:T(8,128)(2,1)} %q_ref.1, bf16[2048,1024]{1,0:T(8,128)(2,1)} %all-gather.4.cloned.1.call-done.kv_ref), custom_call_target="tpu_custom_call" | custom-call | tf_op jit(solution)/shard_map/pallas_call | solution.py:63
  74.5 0.0 copy-start.3
  74.5 1.5 collective-permute-start
  75.9 10.0 %collective-permute-done = bf16[128,1536]{1,0:T(8,128)(2,1)S(1)} collective-permute-done((bf16[128,1536]{1,0:T(8,128)(2,1)}, bf16[128,1536]{1,0:T(8,128)(2,1)S(1)}, u32[]{:S(2)}, u32[]{:S(2)}) %collective-permute-start) | collective-permute-done | bytes 393248 | tf_op jit(solution)/shard_map/ppermute | solution.py:81
  85.9 1.1 broadcast_select_fusion.3
  87.0 58.0 %all-gather.6.cloned.1.call-done = bf16[3072,1536]{1,0:T(8,128)(2,1)} async-done(((bf16[192,1536]{1,0:T(8,128)(2,1)}), bf16[3072,1536]{1,0:T(8,128)(2,1)}) %all-gather.6.cloned.1.call-update) | async-done | bytes 9437200 | tf_op jit(solution)/shard_map/all_gather | solution.py:105
  145.0 0.0 copy-done.3
  145.0 5.1 %fusion = bf16[128,1536]{1,0:T(8,128)(2,1)S(1)} fusion(bf16[3072,1536]{1,0:T(8,128)(2,1)} %all-gather.6.cloned.1.call-done, bf16[128,1536]{1,0:T(8,128)(2,1)S(1)} %get-tuple-element.7, bf16[128,1536]{1,0:T(8,128)(2,1)S(1)} %get-tuple-element.6, bf16[128,1536]{1,0:T(8,128)(2,1)S(1)} %copy-done.3), kind=kOutput, calls=%fused_computation.1 | convolution fusion | flops 1210122240 | bytes 11010048 | tf_op jit(solution)/shard_map/dot_general | solution.py:106
  150.1 0.0 copy-start
  150.1 0.0 copy-start.1
  150.1 0.0 copy-start.2
  150.1 1.5 collective-permute-start.1
  151.7 9.8 %collective-permute-done.1 = bf16[128,1536]{1,0:T(8,128)(2,1)S(1)} collective-permute-done((bf16[128,1536]{1,0:T(8,128)(2,1)S(1)}, bf16[128,1536]{1,0:T(8,128)(2,1)S(1)}, u32[]{:S(2)}, u32[]{:S(2)}) %collective-permute-start.1) | collective-permute-done | bytes 393248 | tf_op jit(solution)/shard_map/ppermute | solution.py:81
  161.5 0.1 broadcast_select_fusion.1
  161.5 0.2 fusion.5
  161.8 0.0 copy-done.1
  161.8 0.0 copy-done.2
  161.8 0.4 fusion.3
  162.2 0.0 copy-done
  162.2 11.2 %fusion.6 = f32[256,2560]{0,1:T(8,128)} fusion(bf16[3072,2560]{1,0:T(8,128)(2,1)} %param.13, bf16[128,3072]{1,0:T(8,128)(2,1)S(1)} %get-tuple-element.3, bf16[128,3072]{1,0:T(8,128)(2,1)S(1)} %get-tuple-element.2), kind=kOutput, calls=%fused_computation.9 | convolution fusion | flops 4029677568 | bytes 19922944 | tf_op jit(solution)/shard_map/dot_general | solution.py:115
  173.4 1.1 slice.12
  174.5 0.9 copy.13
  175.3 0.0 all-gather.8.cloned.1.call-update
  175.4 1.2 slice.9
  176.6 1.2 copy.11.q_ref
  177.7 46.6 %all-gather.8.cloned.1.call-done.kv_ref = bf16[2048,1024]{1,0:T(8,128)(2,1)} async-done(((bf16[128,1024]{1,0:T(8,128)(2,1)}), bf16[2048,1024]{1,0:T(8,128)(2,1)}) %all-gather.8.cloned.1.call-update) | async-done | bytes 4194320 | tf_op jit(solution)/shard_map/all_gather | solution.py:122
  224.3 14.4 %shard_map.87 = bf16[128,1536]{1,0:T(8,128)(2,1)} custom-call(s32[1]{0:T(128)} %bitcast.pos_ref, f32[128,1536]{1,0:T(8,128)} %copy.11.q_ref, bf16[2048,1024]{1,0:T(8,128)(2,1)} %all-gather.8.cloned.1.call-done.kv_ref), custom_call_target="tpu_custom_call" | custom-call | tf_op jit(solution)/shard_map/pallas_call | solution.py:63
  (1 shorter events, 0.0 us)
Async XLA Ops:
  7.2 56.1 %all-gather.4.cloned.1.call-start = ((), (), s32[]{:S(2)}) async-start(), calls=%async_computation | async-start | bytes 4456448 | tf_op jit(solution)/shard_map/all_gather | solution.py:102
  7.9 137.1 %all-gather.6.cloned.1.call-start = ((), (), s32[]{:S(2)}) async-start(), calls=%async_computation.1 | async-start | bytes 10027008 | tf_op jit(solution)/shard_map/all_gather | solution.py:105
  8.6 215.7 %all-gather.8.cloned.1.call-start = ((), (), s32[]{:S(2)}) async-start(), calls=%async_computation.2 | async-start | bytes 4456448 | tf_op jit(solution)/shard_map/all_gather | solution.py:122
  74.5 70.6 %copy-start.3 = (bf16[128,1536]{1,0:T(8,128)(2,1)S(1)}, bf16[128,1536]{1,0:T(8,128)(2,1)}, u32[]{:S(2)}) copy-start(bf16[128,1536]{1,0:T(8,128)(2,1)} %param.7) | copy-start | bytes 1179652
  74.5 11.5 %collective-permute-start = (bf16[128,1536]{1,0:T(8,128)(2,1)}, bf16[128,1536]{1,0:T(8,128)(2,1)S(1)}, u32[]{:S(2)}, u32[]{:S(2)}) collective-permute-start(bf16[128,1536]{1,0:T(8,128)(2,1)} %shard_map.86), channel_id=1, source_target_pairs={{0,1},{1,0},{2,3},{3,2},{4,5},{5,4},{6,7},{7,6},{8,9},{9,8},{10,11... | collective-permute-start | bytes 1179656 | tf_op jit(solution)/shard_map/ppermute | solution.py:81
  150.1 12.1 %copy-start = (bf16[128,1536]{1,0:T(8,128)(2,1)}, bf16[128,1536]{1,0:T(8,128)(2,1)S(1)}, u32[]{:S(2)}) copy-start(bf16[128,1536]{1,0:T(8,128)(2,1)S(1)} %fusion) | copy-start | bytes 1179652
  150.1 11.7 %copy-start.1 = (f32[3072]{0:T(1024)S(1)}, f32[3072]{0:T(1024)}, u32[]{:S(2)}) copy-start(f32[3072]{0:T(1024)} %param.11) | copy-start | bytes 36868
  150.1 11.7 %copy-start.2 = (f32[3072]{0:T(1024)S(1)}, f32[3072]{0:T(1024)}, u32[]{:S(2)}) copy-start(f32[3072]{0:T(1024)} %param.12) | copy-start | bytes 36868
  150.1 11.3 %collective-permute-start.1 = (bf16[128,1536]{1,0:T(8,128)(2,1)S(1)}, bf16[128,1536]{1,0:T(8,128)(2,1)S(1)}, u32[]{:S(2)}, u32[]{:S(2)}) collective-permute-start(bf16[128,1536]{1,0:T(8,128)(2,1)S(1)} %fusion), channel_id=1, source_target_pairs={{0,1},{1,0},{2,3},{3,2},{4,5},{5,4},{6,7},{7,6},{8,9},{9,8},{10,11... | collective-permute-start | bytes 1179656 | tf_op jit(solution)/shard_map/ppermute | solution.py:81
Sparse Core Ops, SparseCore 0:
  10.1 53.0 all-gather.3
  65.5 79.4 all-gather.5
  175.5 48.7 all-gather.7

commit v2 on v1

v2 whole, which is shorter than its diff:
```python
import functools
import math

import jax
import jax.numpy as jnp
from jax import lax
from jax.experimental import pallas as pl
from jax.experimental.pallas import tpu as pltpu
from jax.sharding import Mesh, PartitionSpec as P

HD = 128
QPK = 3
WINDOW = 2048


def _split(x):
    high = x.astype(jnp.bfloat16)
    low = (x - high.astype(jnp.float32)).astype(jnp.bfloat16)
    return high, low


def _attend_kernel(pos_ref, q_ref, *refs, window, exact, block_rows, cores):
    kv_refs = refs[:-1]
    o_ref = refs[-1]
    rows = q_ref.shape[0]
    first = pos_ref[0]
    masks = []
    for part, kv_ref in enumerate(kv_refs):
        keys = kv_ref.shape[0]
        query_pos = first + lax.broadcasted_iota(jnp.int32, (rows, keys), 0)
        index = lax.broadcasted_iota(jnp.int32, (rows, keys), 1)
        key_pos = ((index // block_rows) * cores + pos_ref[1 + part]) * block_rows + index % block_rows
        allowed = key_pos <= query_pos
        if window is not None:
            allowed = allowed & (key_pos > query_pos - window)
        masks.append(allowed)
    score_scale = 1.0 / math.sqrt(HD)
    contract = (((1,), (1,)), ((), ()))
    for head in range(q_ref.shape[1] // HD):
        query = q_ref[:, head * HD:(head + 1) * HD]
        if exact:
            q_hi, q_lo = _split(query.astype(jnp.float32))
        parts = []
        for kv_ref, allowed in zip(kv_refs, masks):
            key = kv_ref[:, :HD]
            if exact:
                scores = lax.dot_general(q_hi, key, contract, preferred_element_type=jnp.float32)
                scores = scores + lax.dot_general(q_lo, key, contract, preferred_element_type=jnp.float32)
            else:
                scores = lax.dot_general(query, key, contract, preferred_element_type=jnp.float32)
            parts.append(jnp.where(allowed, scores * score_scale, -jnp.inf))
        row_top = functools.reduce(
            jnp.maximum, [jnp.max(m, axis=-1, keepdims=True) for m in parts]
        )
        totals = 0.0
        acc = 0.0
        for kv_ref, allowed, masked in zip(kv_refs, masks, parts):
            value = kv_ref[:, HD:]
            weights = jnp.where(allowed, jnp.exp(masked - row_top), 0.0)
            totals = totals + jnp.sum(weights, axis=-1, keepdims=True)
            if exact:
                w_hi, w_lo = _split(weights)
                acc = acc + jnp.dot(w_hi, value, preferred_element_type=jnp.float32)
                acc = acc + jnp.dot(w_lo, value, preferred_element_type=jnp.float32)
            else:
                acc = acc + jnp.dot(weights.astype(jnp.bfloat16), value, preferred_element_type=jnp.float32)
        o_ref[:, head * HD:(head + 1) * HD] = (acc / totals).astype(o_ref.dtype)


def attend(places, queries, parts, window, exact, cores):
    rows, qcols = queries.shape
    groups = parts[0].shape[1] // (2 * HD)
    qblock = qcols // groups
    kernel = functools.partial(
        _attend_kernel, window=window, exact=exact, block_rows=rows, cores=cores
    )
    return pl.pallas_call(
        kernel,
        out_shape=jax.ShapeDtypeStruct((rows, qcols), jnp.bfloat16),
        grid_spec=pltpu.PrefetchScalarGridSpec(
            num_scalar_prefetch=1,
            grid=(groups,),
            in_specs=[pl.BlockSpec((rows, qblock), lambda g, pos: (0, g))]
            + [pl.BlockSpec((p.shape[0], 2 * HD), lambda g, pos: (0, g)) for p in parts],
            out_specs=pl.BlockSpec((rows, qblock), lambda g, pos: (0, g)),
        ),
    )(places, queries, *parts)


def make_body(heads_count):
    def gather_heads(x):
        if heads_count == 2:
            other = lax.ppermute(x, "heads", [(0, 1), (1, 0)])
            first = lax.axis_index("heads") == 0
            low = jnp.where(first, x, other)
            high = jnp.where(first, other, x)
            return jnp.concatenate([low, high], axis=1)
        return lax.all_gather(x, "heads", axis=1, tiled=True)

    def gather_seq(x):
        own = lax.all_gather(x, "chip", axis=0, tiled=True)
        other = lax.ppermute(own, "core", [(0, 1), (1, 0)])
        return own, other

    def body(
        residual_in,
        self_queries,
        self_keys_values,
        self_out_weight,
        gain_query,
        gain_keyvalue,
        cross_weight,
    ):
        tok_rows = residual_in.shape[0]
        groups = self_keys_values.shape[1] // (2 * HD)
        core = lax.axis_index("core")
        seq_place = lax.axis_index("chip") * 2 + core
        places = jnp.stack([seq_place * tok_rows, core, 1 - core]).astype(jnp.int32)

        key_parts = gather_seq(self_keys_values)
        attended = attend(places, self_queries, key_parts, WINDOW, False, 2)

        weight_own, weight_other = gather_seq(self_out_weight)
        att_full = gather_heads(attended)
        chips = weight_own.shape[0] // self_out_weight.shape[0]
        att_split = att_full.reshape(tok_rows, chips, 2, self_out_weight.shape[0])
        att_own = jnp.where(core == 0, att_split[:, :, 0], att_split[:, :, 1])
        att_other = jnp.where(core == 0, att_split[:, :, 1], att_split[:, :, 0])
        projected = jnp.dot(
            att_own.reshape(tok_rows, -1), weight_own, preferred_element_type=jnp.float32
        ) + jnp.dot(
            att_other.reshape(tok_rows, -1), weight_other, preferred_element_type=jnp.float32
        )
        hidden = (residual_in.astype(jnp.float32) + projected).astype(jnp.bfloat16)
        full_rows = gather_heads(hidden)
        widened = full_rows.astype(jnp.float32)
        inverse = lax.rsqrt(jnp.mean(widened * widened, axis=-1, keepdims=True) + 1e-06)
        normed_q = (widened * inverse * gain_query).astype(jnp.bfloat16)
        normed_kv = (widened * inverse * gain_keyvalue).astype(jnp.bfloat16)
        both = jnp.dot(
            jnp.concatenate([normed_q, normed_kv], axis=0),
            cross_weight,
            preferred_element_type=jnp.float32,
        ).reshape(2 * tok_rows, groups, QPK + 2, HD)
        cross_q = both[:tok_rows, :, :QPK].reshape(tok_rows, groups * QPK * HD)
        shared = both[tok_rows:, :, QPK:].reshape(tok_rows, groups * 2 * HD)
        shared_parts = gather_seq(shared.astype(jnp.bfloat16))
        cross_attention = attend(places, cross_q, shared_parts, None, True, 2)
        return (hidden, cross_attention)

    return body


def solution(mesh):
    seq_count = mesh.shape["seq"]
    heads_count = mesh.shape["heads"]
    split = Mesh(
        mesh.devices.reshape(seq_count // 2, 2, heads_count), ("chip", "core", "heads")
    )
    rows = P(("chip", "core"), "heads")
    return jax.shard_map(
        make_body(heads_count),
        mesh=split,
        in_specs=(rows, rows, rows, rows, P(), P(), P(None, "heads")),
        out_specs=(rows, rows),
        check_vma=False,
    )
```

time: 246 us -> 277 us (1.13)
  waiting for transfers between devices: 180 us -> 207 us
  local copies, waits for them, and re-layouts: 4.35 us -> 7.5 us
    all_gather x3, waiting for transfers between devices: 159 us -> 181 us  [gather_seq(): own = lax.all_gather(x, 'chip', axis=0, tiled=True)]
    ppermute x0 -> x3, waiting for transfers between devices: none -> 5.8 us  [gather_seq(): other = lax.ppermute(own, 'core', [(0, 1), (1, 0)])]
    unnamed x8 -> x12, local copies, waits for them, and re-layouts: 0.02 us -> 2.81 us
    dot_general x1 -> x2, matrix products: 5.07 us -> 6.38 us  [the longest x1 3.21 us: body(): jnp.dot(att_own.reshape(tok_rows, -1), weight_own, preferred_element_type...]
  transfers between devices with their start and end apart: 5 -> 8, of which waited for: 5 -> 7; matrix products, arithmetic and copies ran while one was open for 1% -> 3% of each run, Pallas kernels for 5% -> 4%
where the time goes in v2:
time: 277 us
  waiting for transfers between devices  207 us (75%)
  Pallas kernels  25.4 us (9%)
  matrix products  17.5 us (6%)
  between operations  13.9 us (5%)
  local copies, waits for them, and re-layouts  7.5 us (3%)
  starting transfers between devices  3.13 us (1%)
    all_gather x3, waiting for transfers between devices, gather_seq(): own = lax.all_gather(x, 'chip', axis=0, tiled=True)  181 us
    pallas_call x2, Pallas kernels, attend(): pl.pallas_call(kernel, out_shape=jax.ShapeDtypeStruct((rows, qcols), jnp....  25.4 us
    ppermute x2, waiting for transfers between devices, gather_heads(): other = lax.ppermute(x, 'heads', [(0, 1), (1, 0)])  18.7 us
    dot_general x1, matrix products, body(): jnp.dot(jnp.concatenate([normed_q, normed_kv], axis=0), cross_weight, pre...  11.2 us
    ppermute x3, waiting for transfers between devices, gather_seq(): other = lax.ppermute(own, 'core', [(0, 1), (1, 0)])  5.8 us
  transfers between devices with their start and end apart: 8, of which 7 were waited for; matrix products, arithmetic and copies ran while one was open for 3% of the time, Pallas kernels for 4%

profile of v2, /device:TPU:0, one launch (start us, length us, event | category | flops | bytes accessed | tf_op | source)
XLA Modules:
  0.0 276.7 jit_solution(8497955486614331363)
XLA Ops:
  7.2 0.0 all-gather.6.cloned.1.call-start
  7.2 0.7 all-gather.6.cloned.1.call-update
  7.9 0.0 all-gather.4.cloned.1.call-start
  7.9 0.7 all-gather.4.cloned.1.call-update
  8.6 0.0 all-gather.8.cloned.1.call-start
  8.7 83.5 %all-gather.6.cloned.1.call-done = bf16[1536,1536]{1,0:T(8,128)(2,1)} async-done(((bf16[192,1536]{1,0:T(8,128)(2,1)}), bf16[1536,1536]{1,0:T(8,128)(2,1)}) %all-gather.6.cloned.1.call-update) | async-done | bytes 4718608 | tf_op jit(solution)/shard_map/all_gather | solution.py:101
  92.2 0.0 collective-permute-start.2
  92.2 49.6 %all-gather.4.cloned.1.call-done.refs_0_ = bf16[1024,1024]{1,0:T(8,128)(2,1)} async-done(((bf16[128,1024]{1,0:T(8,128)(2,1)}), bf16[1024,1024]{1,0:T(8,128)(2,1)}) %all-gather.4.cloned.1.call-update) | async-done | bytes 2097168 | tf_op jit(solution)/shard_map/all_gather | solution.py:101
  141.8 0.0 collective-permute-start
  141.8 0.6 pad_add_fusion.pos_ref
  142.4 3.8 %collective-permute-done.refs_1_ = bf16[1024,1024]{1,0:T(8,128)(2,1)S(1)} collective-permute-done((bf16[1024,1024]{1,0:T(8,128)(2,1)}, bf16[1024,1024]{1,0:T(8,128)(2,1)S(1)}, u32[]{:S(2)}, u32[]{:S(2)}) %collective-permute-start) | collective-permute-done | bytes 2097184 | tf_op jit(solution)/shard_map/ppermute | solution.py:102
  146.2 0.0 copy-start
  146.2 1.5 copy-done
  147.7 10.9 %shard_map.86 = bf16[128,1536]{1,0:T(8,128)(2,1)} custom-call(s32[3]{0:T(128)} %pad_add_fusion.pos_ref, bf16[128,1536]{1,0:T(8,128)(2,1)} %q_ref.1, bf16[1024,1024]{1,0:T(8,128)(2,1)} %all-gather.4.cloned.1.call-done.refs_0_, bf16[1024,1024]{1,0:T(8,128)(2,1)} %copy-done), custom_call_target="tpu_custom_call" | custom-call | tf_op jit(solution)/shard_map/pallas_call | solution.py:77
  158.6 1.5 collective-permute-start.1
  160.1 9.9 %collective-permute-done.1 = bf16[128,1536]{1,0:T(8,128)(2,1)S(1)} collective-permute-done((bf16[128,1536]{1,0:T(8,128)(2,1)}, bf16[128,1536]{1,0:T(8,128)(2,1)S(1)}, u32[]{:S(2)}, u32[]{:S(2)}) %collective-permute-start.1) | collective-permute-done | bytes 393248 | tf_op jit(solution)/shard_map/ppermute | solution.py:93
  170.0 1.1 broadcast_select_fusion.3
  171.0 0.1 pad_maximum_fusion
  171.1 0.4 copy.9
  171.5 0.1 broadcast_select_fusion.4
  171.5 0.0 copy-start.3
  171.5 3.2 %fusion.12 = f32[128,1536]{1,0:T(8,128)S(1)} fusion(bf16[128,1536]{0,1:T(8,128)(2,1)S(1)} %bitcast.17, bf16[1536,1536]{1,0:T(8,128)(2,1)} %all-gather.6.cloned.1.call-done), kind=kOutput, calls=%fused_computation.26 | convolution fusion | flops 603979776 | bytes 5898240 | tf_op jit(solution)/shard_map/dot_general | solution.py:129
  174.8 0.0 collective-permute-done.2
  174.8 0.0 copy-done.3
  174.8 3.2 %fusion.1 = bf16[128,1536]{1,0:T(8,128)(2,1)S(1)} fusion(f32[128,1536]{1,0:T(8,128)S(1)} %fusion.12, bf16[128,1536]{0,1:T(8,128)(2,1)S(1)} %bitcast.16, bf16[1536,1536]{1,0:T(8,128)(2,1)} %collective-permute-done.2, bf16[128,1536]{1,0:T(8,128)(2,1)S(1)} %copy-done.3), kind=kOutput, calls=%fused_computation.2 | convolution fusion | flops 604766208 | bytes 6684672 | tf_op jit(solution)/shard_map/dot_general | solution.py:131
  178.0 0.0 copy-start.2
  178.0 0.0 copy-start.4
  178.0 0.0 copy-start.5
  178.0 1.5 collective-permute-start.3
  179.5 8.8 %collective-permute-done.3 = bf16[128,1536]{1,0:T(8,128)(2,1)S(1)} collective-permute-done((bf16[128,1536]{1,0:T(8,128)(2,1)S(1)}, bf16[128,1536]{1,0:T(8,128)(2,1)S(1)}, u32[]{:S(2)}, u32[]{:S(2)}) %collective-permute-start.3) | collective-permute-done | bytes 393248 | tf_op jit(solution)/shard_map/ppermute | solution.py:93
  188.3 0.1 broadcast_select_fusion.1
  188.4 0.2 fusion.6
  188.6 0.0 copy-done.4
  188.7 0.0 copy-done.5
  188.7 0.4 fusion.4
  189.1 0.0 copy-done.2
  189.1 11.2 %fusion.7 = f32[256,2560]{0,1:T(8,128)} fusion(bf16[3072,2560]{1,0:T(8,128)(2,1)} %param.13, bf16[128,3072]{1,0:T(8,128)(2,1)S(1)} %get-tuple-element.3, bf16[128,3072]{1,0:T(8,128)(2,1)S(1)} %get-tuple-element.2), kind=kOutput, calls=%fused_computation.10 | convolution fusion | flops 4029677568 | bytes 19922944 | tf_op jit(solution)/shard_map/dot_general | solution.py:140
  200.2 1.1 slice.28
  201.3 0.9 copy.14
  202.2 0.0 all-gather.8.cloned.1.call-update
  202.2 47.8 %all-gather.8.cloned.1.call-done.refs_0_ = bf16[1024,1024]{1,0:T(8,128)(2,1)} async-done(((bf16[128,1024]{1,0:T(8,128)(2,1)}), bf16[1024,1024]{1,0:T(8,128)(2,1)}) %all-gather.8.cloned.1.call-update) | async-done | bytes 2097168 | tf_op jit(solution)/shard_map/all_gather | solution.py:101
  250.0 0.0 collective-permute-start.4
  250.0 1.2 slice.21
  251.2 1.2 copy.12.q_ref
  252.4 2.0 collective-permute-done.4.refs_1_
  254.4 0.0 copy-start.1
  254.4 1.3 copy-done.1
  255.7 14.5 %shard_map.87 = bf16[128,1536]{1,0:T(8,128)(2,1)} custom-call(s32[3]{0:T(128)} %pad_add_fusion.pos_ref, f32[128,1536]{1,0:T(8,128)} %copy.12.q_ref, bf16[1024,1024]{1,0:T(8,128)(2,1)} %all-gather.8.cloned.1.call-done.refs_0_, bf16[1024,1024]{1,0:T(8,128)(2,1)} %copy-done.1), custom_call_target="tpu_custom_call" | custom-call | tf_op jit(solution)/shard_map/pallas_call | solution.py:77
  (1 shorter events, 0.0 us)
Async XLA Ops:
  7.2 85.1 %all-gather.6.cloned.1.call-start = ((), (), s32[]{:S(2)}) async-start(), calls=%async_computation.1 | async-start | bytes 5308416 | tf_op jit(solution)/shard_map/all_gather | solution.py:101
  7.9 133.9 %all-gather.4.cloned.1.call-start = ((), (), s32[]{:S(2)}) async-start(), calls=%async_computation | async-start | bytes 2359296 | tf_op jit(solution)/shard_map/all_gather | solution.py:101
  8.6 241.4 %all-gather.8.cloned.1.call-start = ((), (), s32[]{:S(2)}) async-start(), calls=%async_computation.2 | async-start | bytes 2359296 | tf_op jit(solution)/shard_map/all_gather | solution.py:101
  92.2 82.5 %collective-permute-start.2 = (bf16[1536,1536]{1,0:T(8,128)(2,1)}, bf16[1536,1536]{1,0:T(8,128)(2,1)}, u32[]{:S(2)}, u32[]{:S(2)}) collective-permute-start(bf16[1536,1536]{1,0:T(8,128)(2,1)} %all-gather.6.cloned.1.call-done), channel_id=1, source_target_pairs={{0,2},{2,0},{1,3},{3,1},{4,6},{6,4},{5,7},{7,5},{8,10},{10,8},{9,1... | collective-permute-start | bytes 14155784 | tf_op jit(solution)/shard_map/ppermute | solution.py:102
  141.8 4.4 %collective-permute-start = (bf16[1024,1024]{1,0:T(8,128)(2,1)}, bf16[1024,1024]{1,0:T(8,128)(2,1)S(1)}, u32[]{:S(2)}, u32[]{:S(2)}) collective-permute-start(bf16[1024,1024]{1,0:T(8,128)(2,1)} %all-gather.4.cloned.1.call-done.refs_0_), channel_id=1, source_target_pairs={{0,2},{2,0},{1,3},{3,1},{4,6},{6,4},{5,7},{7,5},{8,10},{10,8},{9,1... | collective-permute-start | bytes 6291464 | tf_op jit(solution)/shard_map/ppermute | solution.py:102
  146.2 1.5 copy-start
  158.6 11.4 %collective-permute-start.1 = (bf16[128,1536]{1,0:T(8,128)(2,1)}, bf16[128,1536]{1,0:T(8,128)(2,1)S(1)}, u32[]{:S(2)}, u32[]{:S(2)}) collective-permute-start(bf16[128,1536]{1,0:T(8,128)(2,1)} %shard_map.86), channel_id=1, source_target_pairs={{0,1},{1,0},{2,3},{3,2},{4,5},{5,4},{6,7},{7,6},{8,9},{9,8},{10,11... | collective-permute-start | bytes 1179656 | tf_op jit(solution)/shard_map/ppermute | solution.py:93
  171.5 3.2 %copy-start.3 = (bf16[128,1536]{1,0:T(8,128)(2,1)S(1)}, bf16[128,1536]{1,0:T(8,128)(2,1)}, u32[]{:S(2)}) copy-start(bf16[128,1536]{1,0:T(8,128)(2,1)} %param.7) | copy-start | bytes 1179652
  178.0 11.1 %copy-start.2 = (bf16[128,1536]{1,0:T(8,128)(2,1)}, bf16[128,1536]{1,0:T(8,128)(2,1)S(1)}, u32[]{:S(2)}) copy-start(bf16[128,1536]{1,0:T(8,128)(2,1)S(1)} %fusion.1) | copy-start | bytes 1179652
  178.0 10.7 %copy-start.4 = (f32[3072]{0:T(1024)S(1)}, f32[3072]{0:T(1024)}, u32[]{:S(2)}) copy-start(f32[3072]{0:T(1024)} %param.11) | copy-start | bytes 36868
  178.0 10.7 %copy-start.5 = (f32[3072]{0:T(1024)S(1)}, f32[3072]{0:T(1024)}, u32[]{:S(2)}) copy-start(f32[3072]{0:T(1024)} %param.12) | copy-start | bytes 36868
  178.0 10.3 %collective-permute-start.3 = (bf16[128,1536]{1,0:T(8,128)(2,1)S(1)}, bf16[128,1536]{1,0:T(8,128)(2,1)S(1)}, u32[]{:S(2)}, u32[]{:S(2)}) collective-permute-start(bf16[128,1536]{1,0:T(8,128)(2,1)S(1)} %fusion.1), channel_id=1, source_target_pairs={{0,1},{1,0},{2,3},{3,2},{4,5},{5,4},{6,7},{7,6},{8,9},{9,8},{10,11... | collective-permute-start | bytes 1179656 | tf_op jit(solution)/shard_map/ppermute | solution.py:93
  250.0 4.4 %collective-permute-start.4 = (bf16[1024,1024]{1,0:T(8,128)(2,1)}, bf16[1024,1024]{1,0:T(8,128)(2,1)S(1)}, u32[]{:S(2)}, u32[]{:S(2)}) collective-permute-start(bf16[1024,1024]{1,0:T(8,128)(2,1)} %all-gather.8.cloned.1.call-done.refs_0_), channel_id=1, source_target_pairs={{0,2},{2,0},{1,3},{3,1},{4,6},{6,4},{5,7},{7,5},{8,10},{10,8},{9,1... | collective-permute-start | bytes 6291464 | tf_op jit(solution)/shard_map/ppermute | solution.py:102
  254.4 1.3 copy-start.1
Sparse Core Ops, SparseCore 0:
  10.2 82.0 all-gather.5
  94.4 47.4 all-gather.3
  202.3 47.6 all-gather.7

commit v3 on v1

--- a/solution.py
+++ b/solution.py
@@ -99,10 +99,20 @@
         seq_place = lax.axis_index("seq")
         first_pos = (seq_place * tok_rows).astype(jnp.int32).reshape(1)
 
-        key_window = lax.all_gather(self_keys_values, "seq", axis=0, tiled=True)
+        kv_size = self_keys_values.size
+        packed = jnp.concatenate([self_keys_values.reshape(-1), self_out_weight.reshape(-1)])
+        gathered = lax.all_gather(packed[None], "seq", axis=0, tiled=True)
+        col_layout = cross_weight.reshape(cross_weight.shape[0], groups, QPK + 2, HD)
+        weight_kv = col_layout[:, :, QPK:].reshape(cross_weight.shape[0], groups * 2 * HD)
+        weight_q = col_layout[:, :, :QPK].reshape(cross_weight.shape[0], groups * QPK * HD)
+        gathered, weight_kv, weight_q = lax.optimization_barrier((gathered, weight_kv, weight_q))
+        seq_count = gathered.shape[0]
+        key_window = gathered[:, :kv_size].reshape(seq_count * tok_rows, -1)
+        out_weight = gathered[:, kv_size:].reshape(
+            seq_count * self_out_weight.shape[0], self_out_weight.shape[1]
+        )
         attended = attend(first_pos, self_queries, key_window, WINDOW, False)
 
-        out_weight = lax.all_gather(self_out_weight, "seq", axis=0, tiled=True)
         projected = jnp.dot(
             gather_heads(attended), out_weight, preferred_element_type=jnp.float32
         )
@@ -112,14 +122,9 @@
         inverse = lax.rsqrt(jnp.mean(widened * widened, axis=-1, keepdims=True) + 1e-06)
         normed_q = (widened * inverse * gain_query).astype(jnp.bfloat16)
         normed_kv = (widened * inverse * gain_keyvalue).astype(jnp.bfloat16)
-        both = jnp.dot(
-            jnp.concatenate([normed_q, normed_kv], axis=0),
-            cross_weight,
-            preferred_element_type=jnp.float32,
-        ).reshape(2 * tok_rows, groups, QPK + 2, HD)
-        cross_q = both[:tok_rows, :, :QPK].reshape(tok_rows, groups * QPK * HD)
-        shared = both[tok_rows:, :, QPK:].reshape(tok_rows, groups * 2 * HD)
+        shared = jnp.dot(normed_kv, weight_kv, preferred_element_type=jnp.float32)
         shared_all = lax.all_gather(shared.astype(jnp.bfloat16), "seq", axis=0, tiled=True)
+        cross_q = jnp.dot(normed_q, weight_q, preferred_element_type=jnp.float32)
         cross_attention = attend(first_pos, cross_q, shared_all, None, True)
         return (hidden, cross_attention)
 

time: 246 us -> 273 us (1.11)
  local copies, waits for them, and re-layouts: 4.35 us -> 87.7 us
  waiting for transfers between devices: 180 us -> 125 us
    all_gather x2 -> x1, waiting for transfers between devices: 113 us -> 74.8 us  [body(): gathered = lax.all_gather(packed[None], 'seq', axis=0, tiled=True)]
    slice x2 -> x4, local copies, waits for them, and re-layouts: 2.31 us -> 27.7 us  [the longest x1 9.12 us: body(): gathered[:, kv_size:]]
    unnamed x8 -> x16, local copies, waits for them, and re-layouts: 0.02 us -> 22.8 us
    reshape x1 -> x3, local copies, waits for them, and re-layouts: 1.17 us -> 20 us  [the longest x1 13.3 us: body(): gathered[:, kv_size:]]
    all_gather x0 -> x1, local copies, waits for them, and re-layouts: none -> 17.3 us  [body(): gathered = lax.all_gather(packed[None], 'seq', axis=0, tiled=True)]
    ppermute x2, waiting for transfers between devices: 19.8 us -> 10.4 us  [gather_heads(): other = lax.ppermute(x, 'heads', [(0, 1), (1, 0)])]
    all_gather x1, waiting for transfers between devices: 46.6 us -> 40 us  [body(): lax.all_gather(shared.astype(jnp.bfloat16), 'seq', axis=0, tiled=True)]
    dot_general x1 -> x2, matrix products: 11.2 us -> 10.8 us  [the longest x1 7.82 us: body(): cross_q = jnp.dot(normed_q, weight_q, preferred_element_type=jnp.float32)]
  transfers between devices with their start and end apart: 5 -> 4, of which waited for: 5 -> 3; matrix products, arithmetic and copies ran while one was open for 1% -> 24% of each run, Pallas kernels for 5% -> 0%
where the time goes in v3:
time: 273 us; the launch traced here: 272 us
  waiting for transfers between devices  125 us (46%)
  local copies, waits for them, and re-layouts  87.7 us (32%)
  Pallas kernels  25.6 us (9%)
  matrix products  16.3 us (6%)
  between operations  14.2 us (5%)
    all_gather x1, waiting for transfers between devices, body(): gathered = lax.all_gather(packed[None], 'seq', axis=0, tiled=True)  74.8 us
    all_gather x1, waiting for transfers between devices, body(): lax.all_gather(shared.astype(jnp.bfloat16), 'seq', axis=0, tiled=True)  40 us
    pallas_call x2, Pallas kernels, attend(): pl.pallas_call(kernel, out_shape=jax.ShapeDtypeStruct((rows, qcols), jnp....  25.6 us
    unnamed x16, local copies, waits for them, and re-layouts  22.8 us
    all_gather x1, local copies, waits for them, and re-layouts, body(): gathered = lax.all_gather(packed[None], 'seq', axis=0, tiled=True)  17.3 us
    reshape x1, local copies, waits for them, and re-layouts, body(): gathered[:, kv_size:]  13.3 us
    ppermute x2, waiting for transfers between devices, gather_heads(): other = lax.ppermute(x, 'heads', [(0, 1), (1, 0)])  10.4 us
    slice x1, local copies, waits for them, and re-layouts, body(): gathered[:, kv_size:]  9.12 us
  transfers between devices with their start and end apart: 4, of which 3 were waited for; matrix products, arithmetic and copies ran while one was open for 24% of the time, Pallas kernels for 0%

profile of v3, /device:TPU:0, one launch (start us, length us, event | category | flops | bytes accessed | tf_op | source)
XLA Modules:
  0.0 272.4 jit_solution(2358724766212562720)
XLA Ops:
  7.2 0.0 all-gather.6.cloned.1.call-start
  7.2 1.8 reshape.40
  9.0 1.0 copy.11
  10.0 1.0 pad_maximum_fusion
  11.0 0.0 all-gather.6.cloned.1.call-update
  11.0 0.0 all-gather.4.cloned.1.call-start
  11.1 20.8 %copy.10 = bf16[3072,2560]{0,1:T(8,128)(2,1)} copy(bf16[3072,2560]{1,0:T(8,128)(2,1)} %param.13) | data formatting | bytes 31457280 | tf_op args[6]
  31.9 8.2 %slice.17 = bf16[3072,4,3,128]{0,3,2,1:T(8,128)(2,1)} slice(bf16[3072,4,5,128]{0,3,2,1:T(8,128)(2,1)} %bitcast.9), slice={[0:3072], [0:4], [0:3], [0:128]} | slice | bytes 18874368 | tf_op jit(solution)/shard_map/slice | solution.py:107
  40.1 5.9 %slice.16 = bf16[3072,4,2,128]{0,3,2,1:T(8,128)(2,1)} slice(bf16[3072,4,5,128]{0,3,2,1:T(8,128)(2,1)} %bitcast.10), slice={[0:3072], [0:4], [3:5], [0:128]} | slice | bytes 12582912 | tf_op jit(solution)/shard_map/slice | solution.py:106
  46.0 74.8 %all-gather.6.cloned.1.call-done = bf16[6815744]{0:T(1024)(128)(2,1)} async-done(((bf16[425984]{0:T(1024)(128)(2,1)}), bf16[6815744]{0:T(1024)(128)(2,1)}) %all-gather.6.cloned.1.call-update) | async-done | bytes 13631504 | tf_op jit(solution)/shard_map/all_gather | solution.py:104
  120.8 17.3 %reshape.46 = bf16[16,425984]{1,0:T(8,128)(2,1)} reshape(bf16[6815744]{0:T(1024)(128)(2,1)} %all-gather.6.cloned.1.call-done) | data formatting | bytes 27262976 | tf_op jit(solution)/shard_map/all_gather | solution.py:104
  138.1 4.4 %slice.14 = bf16[16,131072]{1,0:T(8,128)(2,1)} slice(bf16[16,425984]{1,0:T(8,128)(2,1)} %reshape.46), slice={[0:16], [0:131072]} | slice | bytes 8388608 | tf_op jit(solution)/shard_map/slice | solution.py:110
  142.5 4.9 %reshape.44.kv_ref = bf16[2048,1024]{1,0:T(8,128)(2,1)} reshape(bf16[16,131072]{1,0:T(8,128)(2,1)} %slice.14) | data formatting | bytes 8388608 | tf_op jit(solution)/shard_map/reshape | solution.py:110
  147.3 11.2 %shard_map.86 = bf16[128,1536]{1,0:T(8,128)(2,1)} custom-call(s32[1]{0:T(128)} %bitcast.pos_ref, bf16[128,1536]{1,0:T(8,128)(2,1)} %q_ref.1, bf16[2048,1024]{1,0:T(8,128)(2,1)} %reshape.44.kv_ref), custom_call_target="tpu_custom_call" | custom-call | tf_op jit(solution)/shard_map/pallas_call | solution.py:63
  158.5 1.5 collective-permute-start
  160.0 9.1 %slice.15 = bf16[16,294912]{1,0:T(8,128)(2,1)} slice(bf16[16,425984]{1,0:T(8,128)(2,1)} %reshape.46), slice={[0:16], [131072:425984]} | slice | bytes 18874368 | tf_op jit(solution)/shard_map/slice | solution.py:111
  169.1 0.0 copy-start
  169.1 13.3 %reshape.45 = bf16[3072,1536]{1,0:T(8,128)(2,1)} reshape(bf16[16,294912]{1,0:T(8,128)(2,1)} %slice.15) | data formatting | bytes 18874368 | tf_op jit(solution)/shard_map/reshape | solution.py:111
  182.4 0.0 copy-start.3
  182.4 0.0 collective-permute-done
  182.4 0.0 copy-done
  182.4 0.1 broadcast_select_fusion.3
  182.5 0.0 slice-start
  182.5 0.9 copy-done.3
  183.4 0.0 slice-start.1
  183.4 5.5 %fusion = bf16[128,1536]{1,0:T(8,128)(2,1)S(1)} fusion(bf16[3072,1536]{1,0:T(8,128)(2,1)} %reshape.45, bf16[128,1536]{1,0:T(8,128)(2,1)S(1)} %get-tuple-element.11, bf16[128,1536]{1,0:T(8,128)(2,1)S(1)} %get-tuple-element.10, bf16[128,1536]{1,0:T(8,128)(2,1)S(1)} %copy-done.3), kind=kOutput, calls=%fused_computation.1 | convolution fusion | flops 1210122240 | bytes 11010048 | tf_op jit(solution)/shard_map/dot_general | solution.py:116
  188.9 0.0 copy-start.1
  188.9 0.0 copy-start.4
  188.9 0.6 collective-permute-start.1
  189.6 10.4 %collective-permute-done.1 = bf16[128,1536]{1,0:T(8,128)(2,1)S(1)} collective-permute-done((bf16[128,1536]{1,0:T(8,128)(2,1)S(1)}, bf16[128,1536]{1,0:T(8,128)(2,1)S(1)}, u32[]{:S(2)}, u32[]{:S(2)}) %collective-permute-start.1) | collective-permute-done | bytes 393248 | tf_op jit(solution)/shard_map/ppermute | solution.py:81
  200.0 0.1 broadcast_select_fusion.1
  200.1 0.2 fusion.5
  200.3 0.0 slice-done
  200.3 0.0 slice-done.1
  200.3 0.0 copy-done.4
  200.3 0.0 copy-start.2
  200.4 2.9 %convolution_convert_fusion = bf16[128,1024]{1,0:T(8,128)(2,1)} fusion(bf16[3072,1024]{0,1:T(8,128)(2,1)S(1)} %bitcast.14, f32[3072]{0:T(1024)S(1)} %copy-done.4, f32[128]{0:T(128)S(1)} %add_rsqrt_fusion, bf16[128,1536]{1,0:T(8,128)(2,1)S(1)} %get-tuple-element.9, bf16[128,1536]{1,0:T(8,128)(2,1)S(1)} %get-tuple-element.8), kind=kOutput, calls=%fused_computation.9 | convolution fusion | flops 808189952 | bytes 7352832 | tf_op jit(solution)/shard_map/dot_general | solution.py:125
  203.3 0.0 copy-done.1
  203.3 0.0 all-gather.4.cloned.1.call-update
  203.3 0.0 copy-done.2
  203.3 7.8 %fusion.7.q_ref = f32[128,1536]{1,0:T(8,128)} fusion(bf16[3072,1536]{0,1:T(8,128)(2,1)} %bitcast.11, f32[3072]{0:T(1024)S(1)} %copy-done.2, f32[128]{0:T(128)S(1)} %add_rsqrt_fusion, bf16[128,1536]{1,0:T(8,128)(2,1)S(1)} %get-tuple-element.9, bf16[128,1536]{1,0:T(8,128)(2,1)S(1)} %get-tuple-element.8), kind=kOutput, calls=%fused_computation.11 | convolution fusion | flops 1210712064 | bytes 11022848 | tf_op jit(solution)/shard_map/dot_general | solution.py:127
  211.2 40.0 %all-gather.4.cloned.1.call-done.kv_ref = bf16[2048,1024]{1,0:T(8,128)(2,1)} async-done(((bf16[128,1024]{1,0:T(8,128)(2,1)}), bf16[2048,1024]{1,0:T(8,128)(2,1)}) %all-gather.4.cloned.1.call-update) | async-done | bytes 4194320 | tf_op jit(solution)/shard_map/all_gather | solution.py:126
  251.1 14.4 %shard_map.87 = bf16[128,1536]{1,0:T(8,128)(2,1)} custom-call(s32[1]{0:T(128)} %bitcast.pos_ref, f32[128,1536]{1,0:T(8,128)} %fusion.7.q_ref, bf16[2048,1024]{1,0:T(8,128)(2,1)} %all-gather.4.cloned.1.call-done.kv_ref), custom_call_target="tpu_custom_call" | custom-call | tf_op jit(solution)/shard_map/pallas_call | solution.py:63
  (2 shorter events, 0.0 us)
Async XLA Ops:
  7.2 113.6 %all-gather.6.cloned.1.call-start = ((), (), s32[]{:S(2)}) async-start(), calls=%async_computation.1 | async-start | bytes 14483456 | tf_op jit(solution)/shard_map/all_gather | solution.py:104
  11.0 240.1 %all-gather.4.cloned.1.call-start = ((), (), s32[]{:S(2)}) async-start(), calls=%async_computation | async-start | bytes 4456448 | tf_op jit(solution)/shard_map/all_gather | solution.py:126
  158.5 23.9 %collective-permute-start = (bf16[128,1536]{1,0:T(8,128)(2,1)}, bf16[128,1536]{1,0:T(8,128)(2,1)S(1)}, u32[]{:S(2)}, u32[]{:S(2)}) collective-permute-start(bf16[128,1536]{1,0:T(8,128)(2,1)} %shard_map.86), channel_id=1, source_target_pairs={{0,1},{1,0},{2,3},{3,2},{4,5},{5,4},{6,7},{7,6},{8,9},{9,8},{10,11... | collective-permute-start | bytes 1179656 | tf_op jit(solution)/shard_map/ppermute | solution.py:81
  169.1 13.3 %copy-start = (bf16[128,1536]{1,0:T(8,128)(2,1)S(1)}, bf16[128,1536]{1,0:T(8,128)(2,1)}, u32[]{:S(2)}) copy-start(bf16[128,1536]{1,0:T(8,128)(2,1)} %shard_map.86) | copy-start | bytes 1179652
  182.4 1.0 copy-start.3
  182.5 17.8 %slice-start = ((s8[6291456]{0:T(1024)(128)(4,1)}), s8[4194304]{0:T(1024)(128)(4,1)S(1)}, s32[]{:S(2)}) async-start(s8[6291456]{0:T(1024)(128)(4,1)} %bitcast.12), calls=%async_computation.2 | async-start | bytes 8388608
  183.4 16.9 %slice-start.1 = ((s8[6291456]{0:T(1024)(128)(4,1)}), s8[2097152]{0:T(1024)(128)(4,1)S(1)}, s32[]{:S(2)}) async-start(s8[6291456]{0:T(1024)(128)(4,1)} %bitcast.12), calls=%async_computation.3 | async-start | bytes 4194304
  188.9 14.4 %copy-start.1 = (bf16[128,1536]{1,0:T(8,128)(2,1)}, bf16[128,1536]{1,0:T(8,128)(2,1)S(1)}, u32[]{:S(2)}) copy-start(bf16[128,1536]{1,0:T(8,128)(2,1)S(1)} %fusion) | copy-start | bytes 1179652
  188.9 11.4 %copy-start.4 = (f32[3072]{0:T(1024)S(1)}, f32[3072]{0:T(1024)}, u32[]{:S(2)}) copy-start(f32[3072]{0:T(1024)} %param.12) | copy-start | bytes 36868
  188.9 11.0 %collective-permute-start.1 = (bf16[128,1536]{1,0:T(8,128)(2,1)S(1)}, bf16[128,1536]{1,0:T(8,128)(2,1)S(1)}, u32[]{:S(2)}, u32[]{:S(2)}) collective-permute-start(bf16[128,1536]{1,0:T(8,128)(2,1)S(1)} %fusion), channel_id=1, source_target_pairs={{0,1},{1,0},{2,3},{3,2},{4,5},{5,4},{6,7},{7,6},{8,9},{9,8},{10,11... | collective-permute-start | bytes 1179656 | tf_op jit(solution)/shard_map/ppermute | solution.py:81
  200.3 3.0 %copy-start.2 = (f32[3072]{0:T(1024)S(1)}, f32[3072]{0:T(1024)}, u32[]{:S(2)}) copy-start(f32[3072]{0:T(1024)} %param.11) | copy-start | bytes 36868
Sparse Core Ops, SparseCore 0:
  11.1 109.5 all-gather.5
  203.4 47.6 all-gather.3

commit v4 on v1

--- a/solution.py
+++ b/solution.py
@@ -21,15 +21,20 @@
 
 def _attend_kernel(pos_ref, q_ref, kv_ref, o_ref, *, window, exact):
     rows = q_ref.shape[0]
-    keys = kv_ref.shape[0]
+    keys = kv_ref.shape[0] * (kv_ref.shape[1] // 2 if len(kv_ref.shape) == 3 else 1)
     first = pos_ref[0]
     query_pos = first + lax.broadcasted_iota(jnp.int32, (rows, keys), 0)
     key_pos = lax.broadcasted_iota(jnp.int32, (rows, keys), 1)
     allowed = key_pos <= query_pos
     if window is not None:
         allowed = allowed & (key_pos > query_pos - window)
-    key = kv_ref[:, :HD]
-    value = kv_ref[:, HD:]
+    if len(kv_ref.shape) == 3:
+        half = kv_ref.shape[1] // 2
+        key = kv_ref[:, :half, :].reshape(-1, HD)
+        value = kv_ref[:, half:, :].reshape(-1, HD)
+    else:
+        key = kv_ref[:, :HD]
+        value = kv_ref[:, HD:]
     score_scale = 1.0 / math.sqrt(HD)
     contract = (((1,), (1,)), ((), ()))
     for head in range(q_ref.shape[1] // HD):
@@ -54,10 +59,13 @@
         o_ref[:, head * HD:(head + 1) * HD] = (acc / totals).astype(o_ref.dtype)
 
 
-def attend(first_pos, queries, pairs, window, exact):
+def attend(first_pos, queries, pairs, window, exact, groups=None, offset=0):
     rows, qcols = queries.shape
-    keys, kvcols = pairs.shape
-    groups = kvcols // (2 * HD)
+    if groups is None:
+        groups = pairs.shape[1] // (2 * HD)
+        kv_spec = pl.BlockSpec((pairs.shape[0], 2 * HD), lambda g, pos: (0, g))
+    else:
+        kv_spec = pl.BlockSpec((pairs.shape[0], 2 * rows, HD), lambda g, pos: (0, offset + g, 0))
     qblock = qcols // groups
     kernel = functools.partial(_attend_kernel, window=window, exact=exact)
     return pl.pallas_call(
@@ -68,11 +76,37 @@
             grid=(groups,),
             in_specs=[
                 pl.BlockSpec((rows, qblock), lambda g, pos: (0, g)),
-                pl.BlockSpec((keys, 2 * HD), lambda g, pos: (0, g)),
+                kv_spec,
             ],
             out_specs=pl.BlockSpec((rows, qblock), lambda g, pos: (0, g)),
         ),
     )(first_pos, queries, pairs)
+
+
+def _project_kernel(att_ref, w_ref, res_ref, o_ref):
+    weight = w_ref[...].reshape(-1, w_ref.shape[-1])
+    acc = jnp.dot(att_ref[...], weight, preferred_element_type=jnp.float32)
+    o_ref[...] = (res_ref[...].astype(jnp.float32) + acc).astype(o_ref.dtype)
+
+
+def project(attended, slab, residual, weight_rows):
+    rows, width = residual.shape
+    return pl.pallas_call(
+        _project_kernel,
+        out_shape=jax.ShapeDtypeStruct((rows, width), jnp.bfloat16),
+        grid=(width // HD,),
+        in_specs=[
+            pl.BlockSpec(attended.shape, lambda c: (0, 0)),
+            pl.BlockSpec((slab.shape[0], weight_rows, HD), lambda c: (0, c, 0)),
+            pl.BlockSpec((rows, HD), lambda c: (0, c)),
+        ],
+        out_specs=pl.BlockSpec((rows, HD), lambda c: (0, c)),
+    )(attended, slab, residual)
+
+
+def to_slab(x):
+    rows, cols = x.shape
+    return x.reshape(rows, cols // HD, HD).transpose(1, 0, 2).reshape(-1, HD)
 
 
 def make_body(heads_count):
@@ -99,14 +133,15 @@
         seq_place = lax.axis_index("seq")
         first_pos = (seq_place * tok_rows).astype(jnp.int32).reshape(1)
 
-        key_window = lax.all_gather(self_keys_values, "seq", axis=0, tiled=True)
-        attended = attend(first_pos, self_queries, key_window, WINDOW, False)
-
-        out_weight = lax.all_gather(self_out_weight, "seq", axis=0, tiled=True)
-        projected = jnp.dot(
-            gather_heads(attended), out_weight, preferred_element_type=jnp.float32
-        )
-        hidden = (residual_in.astype(jnp.float32) + projected).astype(jnp.bfloat16)
+        weight_rows = self_out_weight.shape[0]
+        weight_part = to_slab(self_out_weight)
+        pad = (-weight_part.shape[0]) % (2 * tok_rows)
+        weight_part = jnp.pad(weight_part, ((0, pad), (0, 0)))
+        offset = weight_part.shape[0] // (2 * tok_rows)
+        packed = jnp.concatenate([weight_part, to_slab(self_keys_values)], axis=0)
+        slab = lax.all_gather(packed[None], "seq", axis=0, tiled=True)
+        attended = attend(first_pos, self_queries, slab, WINDOW, False, groups, offset)
+        hidden = project(gather_heads(attended), slab, residual_in, weight_rows)
         full_rows = gather_heads(hidden)
         widened = full_rows.astype(jnp.float32)
         inverse = lax.rsqrt(jnp.mean(widened * widened, axis=-1, keepdims=True) + 1e-06)

time: 246 us -> 252 us (1.024)
  Pallas kernels: 25.6 us -> 36.4 us
  matrix products: 16.3 us -> 11.2 us
  waiting for transfers between devices: 180 us -> 175 us
  other arithmetic: 1.73 us -> 4.68 us
  local copies, waits for them, and re-layouts: 4.35 us -> 6.92 us
    pallas_call x0 -> x1, Pallas kernels: none -> 10.8 us  [project(): pl.pallas_call(_project_kernel, out_shape=jax.ShapeDtypeStruct((rows, wid...]
    dot_general x1 -> x0, matrix products: 5.07 us -> none  [body(): jnp.dot(gather_heads(attended), out_weight, preferred_element_type=jnp.fl...]
    all_gather x2 -> x1, waiting for transfers between devices: 113 us -> 110 us  [body(): slab = lax.all_gather(packed[None], 'seq', axis=0, tiled=True)]
  transfers between devices with their start and end apart: 5 -> 4, of which waited for: 5 -> 4; matrix products, arithmetic and copies ran while one was open for 1% -> 1% of each run, Pallas kernels for 5% -> 0%
where the time goes in v4:
time: 252 us
  waiting for transfers between devices  175 us (69%)
  Pallas kernels  36.4 us (14%)
  between operations  14.1 us (6%)
  matrix products  11.2 us (4%)
  local copies, waits for them, and re-layouts  6.92 us (3%)
  other arithmetic  4.68 us (2%)
  starting transfers between devices  3.01 us (1%)
    all_gather x1, waiting for transfers between devices, body(): slab = lax.all_gather(packed[None], 'seq', axis=0, tiled=True)  110 us
    all_gather x1, waiting for transfers between devices, body(): lax.all_gather(shared.astype(jnp.bfloat16), 'seq', axis=0, tiled=True)  46.3 us
    pallas_call x2, Pallas kernels, attend(): pl.pallas_call(kernel, out_shape=jax.ShapeDtypeStruct((rows, qcols), jnp....  25.6 us
    ppermute x2, waiting for transfers between devices, gather_heads(): other = lax.ppermute(x, 'heads', [(0, 1), (1, 0)])  19.2 us
    dot_general x1, matrix products, body(): jnp.dot(jnp.concatenate([normed_q, normed_kv], axis=0), cross_weight, pre...  11.2 us
    pallas_call x1, Pallas kernels, project(): pl.pallas_call(_project_kernel, out_shape=jax.ShapeDtypeStruct((rows, wid...  10.8 us
  transfers between devices with their start and end apart: 4, of which 4 were waited for; matrix products, arithmetic and copies ran while one was open for 1% of the time, Pallas kernels for 0%

profile of v4, /device:TPU:0, one launch (start us, length us, event | category | flops | bytes accessed | tf_op | source)
XLA Modules:
  0.0 251.6 jit_solution(273118806792686248)
XLA Ops:
  7.2 0.0 copy-start
  7.2 0.0 all-gather.6.cloned.1.call-start
  7.2 0.9 copy-done
  8.2 1.5 reshape.38
  9.7 0.2 copy.15
  9.8 1.0 pad_maximum_fusion
  10.8 0.0 all-gather.6.cloned.1.call-update
  10.8 0.0 all-gather.4.cloned.1.call-start
  10.9 109.7 %all-gather.6.cloned.1.call-done = bf16[53248,128]{1,0:T(8,128)(2,1)} async-done(((bf16[3328,128]{1,0:T(8,128)(2,1)}), bf16[53248,128]{1,0:T(8,128)(2,1)}) %all-gather.6.cloned.1.call-update) | async-done | bytes 13631504 | tf_op jit(solution)/shard_map/all_gather | solution.py:142
  120.6 11.2 %shard_map.86 = bf16[128,1536]{1,0:T(8,128)(2,1)} custom-call(s32[1]{0:T(128)} %bitcast.pos_ref, bf16[128,1536]{1,0:T(8,128)(2,1)} %q_ref.1, bf16[16,3328,128]{2,1,0:T(8,128)(2,1)} %bitcast.16), custom_call_target="tpu_custom_call" | custom-call | tf_op jit(solution)/shard_map/pallas_call | solution.py:71
  131.8 1.5 collective-permute-start
  133.2 10.0 %collective-permute-done = bf16[128,1536]{1,0:T(8,128)(2,1)S(1)} collective-permute-done((bf16[128,1536]{1,0:T(8,128)(2,1)}, bf16[128,1536]{1,0:T(8,128)(2,1)S(1)}, u32[]{:S(2)}, u32[]{:S(2)}) %collective-permute-start) | collective-permute-done | bytes 393248 | tf_op jit(solution)/shard_map/ppermute | solution.py:115
  143.3 1.1 broadcast_select_fusion.3
  144.3 1.0 pad_maximum_fusion.1.att_ref
  145.3 10.8 %shard_map.87 = bf16[128,1536]{1,0:T(8,128)(2,1)} custom-call(bf16[128,3072]{1,0:T(8,128)(2,1)} %pad_maximum_fusion.1.att_ref, bf16[16,3328,128]{2,1,0:T(8,128)(2,1)} %bitcast.17, bf16[128,1536]{1,0:T(8,128)(2,1)} %res_ref.1), custom_call_target="tpu_custom_call" | custom-call | tf_op jit(solution)/shard_map/pallas_call | solution.py:94
  156.1 0.0 copy-start.1
  156.1 0.0 copy-start.2
  156.1 1.5 collective-permute-start.1
  157.6 9.2 %collective-permute-done.1 = bf16[128,1536]{1,0:T(8,128)(2,1)S(1)} collective-permute-done((bf16[128,1536]{1,0:T(8,128)(2,1)}, bf16[128,1536]{1,0:T(8,128)(2,1)S(1)}, u32[]{:S(2)}, u32[]{:S(2)}) %collective-permute-start.1) | collective-permute-done | bytes 393248 | tf_op jit(solution)/shard_map/ppermute | solution.py:115
  166.8 1.1 broadcast_select_fusion.1
  167.8 0.2 fusion.4
  168.1 0.0 copy-done.1
  168.1 0.0 copy-done.2
  168.1 0.4 fusion.2
  168.5 11.2 %fusion.5 = f32[256,2560]{0,1:T(8,128)} fusion(bf16[3072,2560]{1,0:T(8,128)(2,1)} %param.13, bf16[128,3072]{1,0:T(8,128)(2,1)S(1)} %get-tuple-element.3, bf16[128,3072]{1,0:T(8,128)(2,1)S(1)} %get-tuple-element.2), kind=kOutput, calls=%fused_computation.7 | convolution fusion | flops 4029677568 | bytes 19922944 | tf_op jit(solution)/shard_map/dot_general | solution.py:150
  179.7 1.1 slice.12
  180.8 0.9 copy.21
  181.6 0.0 all-gather.4.cloned.1.call-update
  181.7 1.2 slice.9
  182.9 1.1 copy.19.q_ref
  184.0 46.3 %all-gather.4.cloned.1.call-done.kv_ref = bf16[2048,1024]{1,0:T(8,128)(2,1)} async-done(((bf16[128,1024]{1,0:T(8,128)(2,1)}), bf16[2048,1024]{1,0:T(8,128)(2,1)}) %all-gather.4.cloned.1.call-update) | async-done | bytes 4194320 | tf_op jit(solution)/shard_map/all_gather | solution.py:157
  230.4 14.4 %shard_map.88 = bf16[128,1536]{1,0:T(8,128)(2,1)} custom-call(s32[1]{0:T(128)} %bitcast.pos_ref, f32[128,1536]{1,0:T(8,128)} %copy.19.q_ref, bf16[2048,1024]{1,0:T(8,128)(2,1)} %all-gather.4.cloned.1.call-done.kv_ref), custom_call_target="tpu_custom_call" | custom-call | tf_op jit(solution)/shard_map/pallas_call | solution.py:71
  (2 shorter events, 0.1 us)
Async XLA Ops:
  7.2 1.0 copy-start
  7.2 113.4 %all-gather.6.cloned.1.call-start = ((), (), s32[]{:S(2)}) async-start(), calls=%async_computation.1 | async-start | bytes 14483456 | tf_op jit(solution)/shard_map/all_gather | solution.py:142
  10.8 219.5 %all-gather.4.cloned.1.call-start = ((), (), s32[]{:S(2)}) async-start(), calls=%async_computation | async-start | bytes 4456448 | tf_op jit(solution)/shard_map/all_gather | solution.py:157
  131.8 11.5 %collective-permute-start = (bf16[128,1536]{1,0:T(8,128)(2,1)}, bf16[128,1536]{1,0:T(8,128)(2,1)S(1)}, u32[]{:S(2)}, u32[]{:S(2)}) collective-permute-start(bf16[128,1536]{1,0:T(8,128)(2,1)} %shard_map.86), channel_id=1, source_target_pairs={{0,1},{1,0},{2,3},{3,2},{4,5},{5,4},{6,7},{7,6},{8,9},{9,8},{10,11... | collective-permute-start | bytes 1179656 | tf_op jit(solution)/shard_map/ppermute | solution.py:115
  156.1 11.9 %copy-start.1 = (f32[3072]{0:T(1024)S(1)}, f32[3072]{0:T(1024)}, u32[]{:S(2)}) copy-start(f32[3072]{0:T(1024)} %param.11) | copy-start | bytes 36868
  156.1 11.9 %copy-start.2 = (f32[3072]{0:T(1024)S(1)}, f32[3072]{0:T(1024)}, u32[]{:S(2)}) copy-start(f32[3072]{0:T(1024)} %param.12) | copy-start | bytes 36868
  156.1 10.6 %collective-permute-start.1 = (bf16[128,1536]{1,0:T(8,128)(2,1)}, bf16[128,1536]{1,0:T(8,128)(2,1)S(1)}, u32[]{:S(2)}, u32[]{:S(2)}) collective-permute-start(bf16[128,1536]{1,0:T(8,128)(2,1)} %shard_map.87), channel_id=1, source_target_pairs={{0,1},{1,0},{2,3},{3,2},{4,5},{5,4},{6,7},{7,6},{8,9},{9,8},{10,11... | collective-permute-start | bytes 1179656 | tf_op jit(solution)/shard_map/ppermute | solution.py:115
Sparse Core Ops, SparseCore 0:
  11.0 109.5 all-gather.5
  181.8 48.5 all-gather.3

commit v5 on v4

--- a/solution.py
+++ b/solution.py
@@ -83,24 +83,28 @@
     )(first_pos, queries, pairs)
 
 
-def _project_kernel(att_ref, w_ref, res_ref, o_ref):
-    weight = w_ref[...].reshape(-1, w_ref.shape[-1])
-    acc = jnp.dot(att_ref[...], weight, preferred_element_type=jnp.float32)
-    o_ref[...] = (res_ref[...].astype(jnp.float32) + acc).astype(o_ref.dtype)
+def _project_kernel(att_ref, w_ref, res_ref, o_ref, *, weight_rows):
+    for part in range(o_ref.shape[1] // HD):
+        weight = w_ref[:, part * weight_rows:(part + 1) * weight_rows, :].reshape(-1, HD)
+        acc = jnp.dot(att_ref[...], weight, preferred_element_type=jnp.float32)
+        cols = slice(part * HD, (part + 1) * HD)
+        o_ref[:, cols] = (res_ref[:, cols].astype(jnp.float32) + acc).astype(o_ref.dtype)
 
 
 def project(attended, slab, residual, weight_rows):
     rows, width = residual.shape
+    blocks = width // HD
+    per_step = next(n for n in (4, 3, 2, 1) if blocks % n == 0)
     return pl.pallas_call(
-        _project_kernel,
+        functools.partial(_project_kernel, weight_rows=weight_rows),
         out_shape=jax.ShapeDtypeStruct((rows, width), jnp.bfloat16),
-        grid=(width // HD,),
+        grid=(blocks // per_step,),
         in_specs=[
             pl.BlockSpec(attended.shape, lambda c: (0, 0)),
-            pl.BlockSpec((slab.shape[0], weight_rows, HD), lambda c: (0, c, 0)),
-            pl.BlockSpec((rows, HD), lambda c: (0, c)),
+            pl.BlockSpec((slab.shape[0], per_step * weight_rows, HD), lambda c: (0, c, 0)),
+            pl.BlockSpec((rows, per_step * HD), lambda c: (0, c)),
         ],
-        out_specs=pl.BlockSpec((rows, HD), lambda c: (0, c)),
+        out_specs=pl.BlockSpec((rows, per_step * HD), lambda c: (0, c)),
     )(attended, slab, residual)
 
 
@@ -140,6 +144,10 @@
         offset = weight_part.shape[0] // (2 * tok_rows)
         packed = jnp.concatenate([weight_part, to_slab(self_keys_values)], axis=0)
         slab = lax.all_gather(packed[None], "seq", axis=0, tiled=True)
+        col_layout = cross_weight.reshape(cross_weight.shape[0], groups, QPK + 2, HD)
+        weight_kv = col_layout[:, :, QPK:].reshape(cross_weight.shape[0], groups * 2 * HD)
+        weight_q = col_layout[:, :, :QPK].reshape(cross_weight.shape[0], groups * QPK * HD)
+        slab, weight_kv, weight_q = lax.optimization_barrier((slab, weight_kv, weight_q))
         attended = attend(first_pos, self_queries, slab, WINDOW, False, groups, offset)
         hidden = project(gather_heads(attended), slab, residual_in, weight_rows)
         full_rows = gather_heads(hidden)
@@ -147,14 +155,9 @@
         inverse = lax.rsqrt(jnp.mean(widened * widened, axis=-1, keepdims=True) + 1e-06)
         normed_q = (widened * inverse * gain_query).astype(jnp.bfloat16)
         normed_kv = (widened * inverse * gain_keyvalue).astype(jnp.bfloat16)
-        both = jnp.dot(
-            jnp.concatenate([normed_q, normed_kv], axis=0),
-            cross_weight,
-            preferred_element_type=jnp.float32,
-        ).reshape(2 * tok_rows, groups, QPK + 2, HD)
-        cross_q = both[:tok_rows, :, :QPK].reshape(tok_rows, groups * QPK * HD)
-        shared = both[tok_rows:, :, QPK:].reshape(tok_rows, groups * 2 * HD)
+        shared = jnp.dot(normed_kv, weight_kv, preferred_element_type=jnp.float32)
         shared_all = lax.all_gather(shared.astype(jnp.bfloat16), "seq", axis=0, tiled=True)
+        cross_q = jnp.dot(normed_q, weight_q, preferred_element_type=jnp.float32)
         cross_attention = attend(first_pos, cross_q, shared_all, None, True)
         return (hidden, cross_attention)
 

time: 252 us -> 240 us (0.952)
  waiting for transfers between devices: 175 us -> 135 us
  local copies, waits for them, and re-layouts: 6.92 us -> 36.7 us
  Pallas kernels: 36.4 us -> 32.3 us
    all_gather x1, waiting for transfers between devices: 110 us -> 75 us  [body(): slab = lax.all_gather(packed[None], 'seq', axis=0, tiled=True)]
    unnamed x6 -> x9, local copies, waits for them, and re-layouts: 0.91 us -> 20.8 us
    slice x2, local copies, waits for them, and re-layouts: 2.31 us -> 14.1 us  [the longest x1 8.24 us: body(): col_layout[:, :, :QPK].reshape(cross_weight.shape[0], groups * QPK * HD)]
    all_gather x1, waiting for transfers between devices: 46.3 us -> 40.8 us  [body(): lax.all_gather(shared.astype(jnp.bfloat16), 'seq', axis=0, tiled=True)]
    pallas_call x1, Pallas kernels: 10.8 us -> 6.69 us  [project(): pl.pallas_call(functools.partial(_project_kernel, weight_rows=weight_rows...]
    dot_general x1 -> x2, matrix products: 11.2 us -> 13.6 us  [the longest x1 7.86 us: body(): cross_q = jnp.dot(normed_q, weight_q, preferred_element_type=jnp.float32)]
  transfers between devices with their start and end apart: 4 -> 4, of which waited for: 4 -> 4; matrix products, arithmetic and copies ran while one was open for 1% -> 18% of each run, Pallas kernels for 0% -> 0%
where the time goes in v5:
time: 240 us; the launch traced here: 239 us
  waiting for transfers between devices  135 us (56%)
  local copies, waits for them, and re-layouts  36.7 us (15%)
  Pallas kernels  32.3 us (13%)
  between operations  14.1 us (6%)
  matrix products  13.6 us (6%)
  other arithmetic  4.27 us (2%)
  starting transfers between devices  3.02 us (1%)
    all_gather x1, waiting for transfers between devices, body(): slab = lax.all_gather(packed[None], 'seq', axis=0, tiled=True)  75 us
    all_gather x1, waiting for transfers between devices, body(): lax.all_gather(shared.astype(jnp.bfloat16), 'seq', axis=0, tiled=True)  40.8 us
    pallas_call x2, Pallas kernels, attend(): pl.pallas_call(kernel, out_shape=jax.ShapeDtypeStruct((rows, qcols), jnp....  25.6 us
    unnamed x9, local copies, waits for them, and re-layouts  20.8 us
    ppermute x2, waiting for transfers between devices, gather_heads(): other = lax.ppermute(x, 'heads', [(0, 1), (1, 0)])  19.2 us
    slice x1, local copies, waits for them, and re-layouts, body(): col_layout[:, :, :QPK].reshape(cross_weight.shape[0], groups * QPK * HD)  8.24 us
    dot_general x1, matrix products, body(): cross_q = jnp.dot(normed_q, weight_q, preferred_element_type=jnp.float32)  7.86 us
    pallas_call x1, Pallas kernels, project(): pl.pallas_call(functools.partial(_project_kernel, weight_rows=weight_rows...  6.69 us
  transfers between devices with their start and end apart: 4, of which 4 were waited for; matrix products, arithmetic and copies ran while one was open for 18% of the time, Pallas kernels for 0%

profile of v5, /device:TPU:0, one launch (start us, length us, event | category | flops | bytes accessed | tf_op | source)
XLA Modules:
  0.0 238.9 jit_solution(8121143558831567869)
XLA Ops:
  7.2 0.0 copy-start
  7.2 0.0 all-gather.6.cloned.1.call-start
  7.2 1.5 reshape.39
  8.8 0.2 copy.13
  8.9 0.0 copy-done
  9.0 0.9 pad_maximum_fusion
  9.9 0.0 all-gather.6.cloned.1.call-update
  10.0 0.0 all-gather.4.cloned.1.call-start
  10.0 20.8 %copy.15 = bf16[3072,2560]{0,1:T(8,128)(2,1)} copy(bf16[3072,2560]{1,0:T(8,128)(2,1)} %param.13) | data formatting | bytes 31457280 | tf_op args[6]
  30.8 8.2 %slice.9 = bf16[3072,4,3,128]{0,3,2,1:T(8,128)(2,1)} slice(bf16[3072,4,5,128]{0,3,2,1:T(8,128)(2,1)} %bitcast.17), slice={[0:3072], [0:4], [0:3], [0:128]} | slice | bytes 18874368 | tf_op jit(solution)/shard_map/slice | solution.py:149
  39.1 5.9 %slice.8 = bf16[3072,4,2,128]{0,3,2,1:T(8,128)(2,1)} slice(bf16[3072,4,5,128]{0,3,2,1:T(8,128)(2,1)} %bitcast.18), slice={[0:3072], [0:4], [3:5], [0:128]} | slice | bytes 12582912 | tf_op jit(solution)/shard_map/slice | solution.py:148
  44.9 75.0 %all-gather.6.cloned.1.call-done = bf16[53248,128]{1,0:T(8,128)(2,1)} async-done(((bf16[3328,128]{1,0:T(8,128)(2,1)}), bf16[53248,128]{1,0:T(8,128)(2,1)}) %all-gather.6.cloned.1.call-update) | async-done | bytes 13631504 | tf_op jit(solution)/shard_map/all_gather | solution.py:146
  119.9 11.2 %shard_map.86 = bf16[128,1536]{1,0:T(8,128)(2,1)} custom-call(s32[1]{0:T(128)} %bitcast.pos_ref, bf16[128,1536]{1,0:T(8,128)(2,1)} %q_ref.1, bf16[16,3328,128]{2,1,0:T(8,128)(2,1)} %bitcast.19), custom_call_target="tpu_custom_call" | custom-call | tf_op jit(solution)/shard_map/pallas_call | solution.py:71
  131.1 1.5 collective-permute-start
  132.6 10.0 %collective-permute-done = bf16[128,1536]{1,0:T(8,128)(2,1)S(1)} collective-permute-done((bf16[128,1536]{1,0:T(8,128)(2,1)}, bf16[128,1536]{1,0:T(8,128)(2,1)S(1)}, u32[]{:S(2)}, u32[]{:S(2)}) %collective-permute-start) | collective-permute-done | bytes 393248 | tf_op jit(solution)/shard_map/ppermute | solution.py:119
  142.6 1.1 broadcast_select_fusion.3
  143.6 1.0 pad_maximum_fusion.1.att_ref
  144.6 6.7 %shard_map.87 = bf16[128,1536]{1,0:T(8,128)(2,1)} custom-call(bf16[128,3072]{1,0:T(8,128)(2,1)} %pad_maximum_fusion.1.att_ref, bf16[16,3328,128]{2,1,0:T(8,128)(2,1)} %bitcast.20, bf16[128,1536]{1,0:T(8,128)(2,1)} %res_ref.1), custom_call_target="tpu_custom_call" | custom-call | tf_op jit(solution)/shard_map/pallas_call | solution.py:98
  151.3 0.0 copy-start.3
  151.3 1.5 collective-permute-start.1
  152.8 9.1 %collective-permute-done.1 = bf16[128,1536]{1,0:T(8,128)(2,1)S(1)} collective-permute-done((bf16[128,1536]{1,0:T(8,128)(2,1)}, bf16[128,1536]{1,0:T(8,128)(2,1)S(1)}, u32[]{:S(2)}, u32[]{:S(2)}) %collective-permute-start.1) | collective-permute-done | bytes 393248 | tf_op jit(solution)/shard_map/ppermute | solution.py:119
  161.9 1.1 broadcast_select_fusion.1
  163.0 0.2 fusion.4
  163.2 0.0 copy-done.3
  163.2 0.0 copy-start.2
  163.2 5.7 %convolution_convert_fusion = bf16[128,1024]{1,0:T(8,128)(2,1)} fusion(bf16[3072,1024]{0,1:T(8,128)(2,1)} %bitcast.22, f32[3072]{0:T(1024)S(1)} %copy-done.3, f32[128]{0:T(128)S(1)} %add_rsqrt_fusion, bf16[128,1536]{1,0:T(8,128)(2,1)S(1)} %get-tuple-element.9, bf16[128,1536]{1,0:T(8,128)(2,1)S(1)} %get-tuple-element.8), kind=kOutput, calls=%fused_computation.7 | convolution fusion | flops 808189952 | bytes 7352832 | tf_op jit(solution)/shard_map/dot_general | solution.py:158
  169.0 0.0 all-gather.4.cloned.1.call-update
  169.0 0.0 copy-done.2
  169.0 0.0 copy-start.1
  169.0 7.9 %fusion.6.q_ref = f32[128,1536]{1,0:T(8,128)} fusion(bf16[3072,1536]{0,1:T(8,128)(2,1)} %bitcast.21, f32[3072]{0:T(1024)S(1)} %copy-done.2, f32[128]{0:T(128)S(1)} %add_rsqrt_fusion, bf16[128,1536]{1,0:T(8,128)(2,1)S(1)} %get-tuple-element.9, bf16[128,1536]{1,0:T(8,128)(2,1)S(1)} %get-tuple-element.8), kind=kOutput, calls=%fused_computation.9 | convolution fusion | flops 1210712064 | bytes 11022848 | tf_op jit(solution)/shard_map/dot_general | solution.py:160
  176.9 40.8 %all-gather.4.cloned.1.call-done.kv_ref = bf16[2048,1024]{1,0:T(8,128)(2,1)} async-done(((bf16[128,1024]{1,0:T(8,128)(2,1)}), bf16[2048,1024]{1,0:T(8,128)(2,1)}) %all-gather.4.cloned.1.call-update) | async-done | bytes 4194320 | tf_op jit(solution)/shard_map/all_gather | solution.py:159
  217.7 14.4 %shard_map.88 = bf16[128,1536]{1,0:T(8,128)(2,1)} custom-call(s32[1]{0:T(128)} %bitcast.pos_ref, f32[128,1536]{1,0:T(8,128)} %fusion.6.q_ref, bf16[2048,1024]{1,0:T(8,128)(2,1)} %all-gather.4.cloned.1.call-done.kv_ref), custom_call_target="tpu_custom_call" | custom-call | tf_op jit(solution)/shard_map/pallas_call | solution.py:71
  232.1 0.0 copy-done.1
  (2 shorter events, 0.1 us)
Async XLA Ops:
  7.2 1.8 copy-start
  7.2 112.7 %all-gather.6.cloned.1.call-start = ((), (), s32[]{:S(2)}) async-start(), calls=%async_computation.1 | async-start | bytes 14483456 | tf_op jit(solution)/shard_map/all_gather | solution.py:146
  10.0 207.7 %all-gather.4.cloned.1.call-start = ((), (), s32[]{:S(2)}) async-start(), calls=%async_computation | async-start | bytes 4456448 | tf_op jit(solution)/shard_map/all_gather | solution.py:159
  131.1 11.5 %collective-permute-start = (bf16[128,1536]{1,0:T(8,128)(2,1)}, bf16[128,1536]{1,0:T(8,128)(2,1)S(1)}, u32[]{:S(2)}, u32[]{:S(2)}) collective-permute-start(bf16[128,1536]{1,0:T(8,128)(2,1)} %shard_map.86), channel_id=1, source_target_pairs={{0,1},{1,0},{2,3},{3,2},{4,5},{5,4},{6,7},{7,6},{8,9},{9,8},{10,11... | collective-permute-start | bytes 1179656 | tf_op jit(solution)/shard_map/ppermute | solution.py:119
  151.3 11.9 %copy-start.3 = (f32[3072]{0:T(1024)S(1)}, f32[3072]{0:T(1024)}, u32[]{:S(2)}) copy-start(f32[3072]{0:T(1024)} %param.12) | copy-start | bytes 36868
  151.3 10.6 %collective-permute-start.1 = (bf16[128,1536]{1,0:T(8,128)(2,1)}, bf16[128,1536]{1,0:T(8,128)(2,1)S(1)}, u32[]{:S(2)}, u32[]{:S(2)}) collective-permute-start(bf16[128,1536]{1,0:T(8,128)(2,1)} %shard_map.87), channel_id=1, source_target_pairs={{0,1},{1,0},{2,3},{3,2},{4,5},{5,4},{6,7},{7,6},{8,9},{9,8},{10,11... | collective-permute-start | bytes 1179656 | tf_op jit(solution)/shard_map/ppermute | solution.py:119
  163.2 5.8 %copy-start.2 = (f32[3072]{0:T(1024)S(1)}, f32[3072]{0:T(1024)}, u32[]{:S(2)}) copy-start(f32[3072]{0:T(1024)} %param.11) | copy-start | bytes 36868
  169.0 63.1 %copy-start.1 = (bf16[128,1024]{1,0:T(8,128)(2,1)S(1)}, bf16[128,1024]{1,0:T(8,128)(2,1)}, u32[]{:S(2)}) copy-start(bf16[128,1024]{1,0:T(8,128)(2,1)} %param.9) | copy-start | bytes 786436
Sparse Core Ops, SparseCore 0:
  10.3 109.5 all-gather.5
  169.1 48.5 all-gather.3

commit v6 on v5

--- a/solution.py
+++ b/solution.py
@@ -108,6 +108,38 @@
     )(attended, slab, residual)
 
 
+def _half_kernel(sel_ref, att_ref, w_ref, *refs, weight_rows):
+    o_ref = refs[-1]
+    for part in range(o_ref.shape[1] // HD):
+        weight = w_ref[:, part * weight_rows:(part + 1) * weight_rows, :].reshape(-1, HD)
+        acc = jnp.dot(att_ref[...], weight, preferred_element_type=jnp.float32)
+        cols = slice(part * HD, (part + 1) * HD)
+        for base_ref in refs[:-1]:
+            acc = acc + base_ref[:, cols].astype(jnp.float32)
+        o_ref[:, cols] = acc.astype(o_ref.dtype)
+
+
+def project_half(which, attended, slab, bases, weight_rows, out_dtype, width):
+    rows = attended.shape[0]
+    blocks = width // HD
+    per_step = next(n for n in (4, 3, 2, 1) if blocks % n == 0)
+    devices = attended.shape[1] // weight_rows
+    return pl.pallas_call(
+        functools.partial(_half_kernel, weight_rows=weight_rows),
+        out_shape=jax.ShapeDtypeStruct((rows, width), out_dtype),
+        grid_spec=pltpu.PrefetchScalarGridSpec(
+            num_scalar_prefetch=1,
+            grid=(blocks // per_step,),
+            in_specs=[
+                pl.BlockSpec(attended.shape, lambda c, sel: (0, 0)),
+                pl.BlockSpec((devices, per_step * weight_rows, HD), lambda c, sel: (sel[0], c, 0)),
+            ]
+            + [pl.BlockSpec((rows, per_step * HD), lambda c, sel: (0, c)) for _ in bases],
+            out_specs=pl.BlockSpec((rows, per_step * HD), lambda c, sel: (0, c)),
+        ),
+    )(which, attended, slab, *bases)
+
+
 def to_slab(x):
     rows, cols = x.shape
     return x.reshape(rows, cols // HD, HD).transpose(1, 0, 2).reshape(-1, HD)
@@ -149,7 +181,20 @@
         weight_q = col_layout[:, :, :QPK].reshape(cross_weight.shape[0], groups * QPK * HD)
         slab, weight_kv, weight_q = lax.optimization_barrier((slab, weight_kv, weight_q))
         attended = attend(first_pos, self_queries, slab, WINDOW, False, groups, offset)
-        hidden = project(gather_heads(attended), slab, residual_in, weight_rows)
+        if heads_count == 2:
+            place = lax.axis_index("heads")
+            other = lax.ppermute(attended, "heads", [(0, 1), (1, 0)])
+            width = residual_in.shape[1]
+            own_part = project_half(
+                place.astype(jnp.int32).reshape(1), attended, slab,
+                [], weight_rows, jnp.float32, width,
+            )
+            hidden = project_half(
+                (1 - place).astype(jnp.int32).reshape(1), other, slab,
+                [own_part, residual_in], weight_rows, jnp.bfloat16, width,
+            )
+        else:
+            hidden = project(gather_heads(attended), slab, residual_in, weight_rows)
         full_rows = gather_heads(hidden)
         widened = full_rows.astype(jnp.float32)
         inverse = lax.rsqrt(jnp.mean(widened * widened, axis=-1, keepdims=True) + 1e-06)

time: 240 us -> 237 us (0.988)
  waiting for transfers between devices: 135 us -> 130 us
  Pallas kernels: 32.3 us -> 35.4 us
    ppermute x2 -> x1, waiting for transfers between devices: 19.2 us -> 9.15 us  [gather_heads(): other = lax.ppermute(x, 'heads', [(0, 1), (1, 0)])]
    ppermute x0 -> x1, waiting for transfers between devices: none -> 5.16 us  [body(): other = lax.ppermute(attended, 'heads', [(0, 1), (1, 0)])]
    pallas_call x1 -> x2, Pallas kernels: 6.69 us -> 9.8 us  [project_half(): pl.pallas_call(functools.partial(_half_kernel, weight_rows=weight_rows),...]
    unnamed x9 -> x11, local copies, waits for them, and re-layouts: 20.8 us -> 21.6 us
  transfers between devices with their start and end apart: 4 -> 4, of which waited for: 4 -> 4; matrix products, arithmetic and copies ran while one was open for 18% -> 18% of each run, Pallas kernels for 0% -> 2%
where the time goes in v6:
time: 237 us; the launch traced here: 236 us
  waiting for transfers between devices  130 us (55%)
  local copies, waits for them, and re-layouts  37.4 us (16%)
  Pallas kernels  35.4 us (15%)
  between operations  14.1 us (6%)
  matrix products  13.6 us (6%)
  starting transfers between devices  3.02 us (1%)
    all_gather x1, waiting for transfers between devices, body(): slab = lax.all_gather(packed[None], 'seq', axis=0, tiled=True)  75 us
    all_gather x1, waiting for transfers between devices, body(): lax.all_gather(shared.astype(jnp.bfloat16), 'seq', axis=0, tiled=True)  40.8 us
    pallas_call x2, Pallas kernels, attend(): pl.pallas_call(kernel, out_shape=jax.ShapeDtypeStruct((rows, qcols), jnp....  25.6 us
    unnamed x11, local copies, waits for them, and re-layouts  21.6 us
    pallas_call x2, Pallas kernels, project_half(): pl.pallas_call(functools.partial(_half_kernel, weight_rows=weight_rows),...  9.8 us
    ppermute x1, waiting for transfers between devices, gather_heads(): other = lax.ppermute(x, 'heads', [(0, 1), (1, 0)])  9.15 us
    slice x1, local copies, waits for them, and re-layouts, body(): col_layout[:, :, :QPK].reshape(cross_weight.shape[0], groups * QPK * HD)  8.24 us
    dot_general x1, matrix products, body(): cross_q = jnp.dot(normed_q, weight_q, preferred_element_type=jnp.float32)  7.86 us
  transfers between devices with their start and end apart: 4, of which 4 were waited for; matrix products, arithmetic and copies ran while one was open for 18% of the time, Pallas kernels for 2%

profile of v6, /device:TPU:0, one launch (start us, length us, event | category | flops | bytes accessed | tf_op | source)
XLA Modules:
  0.0 235.9 jit_solution(16824256076797911662)
XLA Ops:
  7.2 0.0 copy-start
  7.2 0.0 all-gather.6.cloned.1.call-start
  7.2 1.5 reshape.46
  8.8 0.2 copy.13
  8.9 0.0 copy-done
  9.0 0.9 pad_maximum_fusion
  9.9 0.0 all-gather.6.cloned.1.call-update
  10.0 0.0 all-gather.4.cloned.1.call-start
  10.0 20.8 %copy.15 = bf16[3072,2560]{0,1:T(8,128)(2,1)} copy(bf16[3072,2560]{1,0:T(8,128)(2,1)} %param.13) | data formatting | bytes 31457280 | tf_op args[6]
  30.8 8.2 %slice.9 = bf16[3072,4,3,128]{0,3,2,1:T(8,128)(2,1)} slice(bf16[3072,4,5,128]{0,3,2,1:T(8,128)(2,1)} %bitcast.22), slice={[0:3072], [0:4], [0:3], [0:128]} | slice | bytes 18874368 | tf_op jit(solution)/shard_map/slice | solution.py:181
  39.1 5.9 %slice.8 = bf16[3072,4,2,128]{0,3,2,1:T(8,128)(2,1)} slice(bf16[3072,4,5,128]{0,3,2,1:T(8,128)(2,1)} %bitcast.23), slice={[0:3072], [0:4], [3:5], [0:128]} | slice | bytes 12582912 | tf_op jit(solution)/shard_map/slice | solution.py:180
  44.9 75.0 %all-gather.6.cloned.1.call-done = bf16[53248,128]{1,0:T(8,128)(2,1)} async-done(((bf16[3328,128]{1,0:T(8,128)(2,1)}), bf16[53248,128]{1,0:T(8,128)(2,1)}) %all-gather.6.cloned.1.call-update) | async-done | bytes 13631504 | tf_op jit(solution)/shard_map/all_gather | solution.py:178
  119.9 11.2 %shard_map.86.att_ref = bf16[128,1536]{1,0:T(8,128)(2,1)} custom-call(s32[1]{0:T(128)} %bitcast.1.pos_ref, bf16[128,1536]{1,0:T(8,128)(2,1)} %q_ref.1, bf16[16,3328,128]{2,1,0:T(8,128)(2,1)} %bitcast.19), custom_call_target="tpu_custom_call" | custom-call | tf_op jit(solution)/shard_map/pallas_call | solution.py:71
  131.1 1.5 collective-permute-start
  132.6 4.9 %shard_map.87.refs_0_ = f32[128,1536]{1,0:T(8,128)} custom-call(s32[1]{0:T(128)} %bitcast.10.sel_ref, bf16[128,1536]{1,0:T(8,128)(2,1)} %shard_map.86.att_ref, bf16[16,3328,128]{2,1,0:T(8,128)(2,1)} %bitcast.20), custom_call_target="tpu_custom_call" | custom-call | tf_op jit(solution)/shard_map/pallas_call | solution.py:127
  137.4 5.2 %collective-permute-done.att_ref = bf16[128,1536]{1,0:T(8,128)(2,1)S(1)} collective-permute-done((bf16[128,1536]{1,0:T(8,128)(2,1)}, bf16[128,1536]{1,0:T(8,128)(2,1)S(1)}, u32[]{:S(2)}, u32[]{:S(2)}) %collective-permute-start) | collective-permute-done | bytes 393248 | tf_op jit(solution)/shard_map/ppermute | solution.py:186
  142.6 0.0 copy-start.2
  142.6 0.7 copy-done.2
  143.3 5.0 %shard_map.88 = bf16[128,1536]{1,0:T(8,128)(2,1)} custom-call(s32[1]{0:T(128)} %bitcast.sel_ref, bf16[128,1536]{1,0:T(8,128)(2,1)} %copy-done.2, bf16[16,3328,128]{2,1,0:T(8,128)(2,1)} %bitcast.21, f32[128,1536]{1,0:T(8,128)} %shard_map.87.refs_0_, bf16[128,1536]{1,0:T(8,128)(2,1)} %refs_1_.1), custom_call_target="tpu_custom_call" | custom-call | tf_op jit(solution)/shard_map/pallas_call | solution.py:127
  148.3 0.0 copy-start.4
  148.3 1.5 collective-permute-start.1
  149.8 9.1 %collective-permute-done.1 = bf16[128,1536]{1,0:T(8,128)(2,1)S(1)} collective-permute-done((bf16[128,1536]{1,0:T(8,128)(2,1)}, bf16[128,1536]{1,0:T(8,128)(2,1)S(1)}, u32[]{:S(2)}, u32[]{:S(2)}) %collective-permute-start.1) | collective-permute-done | bytes 393248 | tf_op jit(solution)/shard_map/ppermute | solution.py:151
  158.9 1.1 broadcast_select_fusion.1
  160.0 0.2 fusion.4
  160.2 0.0 copy-done.4
  160.2 0.0 copy-start.3
  160.2 5.7 %convolution_convert_fusion = bf16[128,1024]{1,0:T(8,128)(2,1)} fusion(bf16[3072,1024]{0,1:T(8,128)(2,1)} %bitcast.25, f32[3072]{0:T(1024)S(1)} %copy-done.4, f32[128]{0:T(128)S(1)} %add_rsqrt_fusion, bf16[128,1536]{1,0:T(8,128)(2,1)S(1)} %get-tuple-element.9, bf16[128,1536]{1,0:T(8,128)(2,1)S(1)} %get-tuple-element.8), kind=kOutput, calls=%fused_computation.7 | convolution fusion | flops 808189952 | bytes 7352832 | tf_op jit(solution)/shard_map/dot_general | solution.py:203
  165.9 0.0 all-gather.4.cloned.1.call-update
  166.0 0.0 copy-done.3
  166.0 0.0 copy-start.1
  166.0 7.9 %fusion.6.q_ref = f32[128,1536]{1,0:T(8,128)} fusion(bf16[3072,1536]{0,1:T(8,128)(2,1)} %bitcast.24, f32[3072]{0:T(1024)S(1)} %copy-done.3, f32[128]{0:T(128)S(1)} %add_rsqrt_fusion, bf16[128,1536]{1,0:T(8,128)(2,1)S(1)} %get-tuple-element.9, bf16[128,1536]{1,0:T(8,128)(2,1)S(1)} %get-tuple-element.8), kind=kOutput, calls=%fused_computation.9 | convolution fusion | flops 1210712064 | bytes 11022848 | tf_op jit(solution)/shard_map/dot_general | solution.py:205
  173.8 40.8 %all-gather.4.cloned.1.call-done.kv_ref = bf16[2048,1024]{1,0:T(8,128)(2,1)} async-done(((bf16[128,1024]{1,0:T(8,128)(2,1)}), bf16[2048,1024]{1,0:T(8,128)(2,1)}) %all-gather.4.cloned.1.call-update) | async-done | bytes 4194320 | tf_op jit(solution)/shard_map/all_gather | solution.py:204
  214.7 14.4 %shard_map.89 = bf16[128,1536]{1,0:T(8,128)(2,1)} custom-call(s32[1]{0:T(128)} %bitcast.1.pos_ref, f32[128,1536]{1,0:T(8,128)} %fusion.6.q_ref, bf16[2048,1024]{1,0:T(8,128)(2,1)} %all-gather.4.cloned.1.call-done.kv_ref), custom_call_target="tpu_custom_call" | custom-call | tf_op jit(solution)/shard_map/pallas_call | solution.py:71
  229.1 0.0 copy-done.1
  (2 shorter events, 0.1 us)
Async XLA Ops:
  7.2 1.8 copy-start
  7.2 112.7 %all-gather.6.cloned.1.call-start = ((), (), s32[]{:S(2)}) async-start(), calls=%async_computation.1 | async-start | bytes 14483456 | tf_op jit(solution)/shard_map/all_gather | solution.py:178
  10.0 204.7 %all-gather.4.cloned.1.call-start = ((), (), s32[]{:S(2)}) async-start(), calls=%async_computation | async-start | bytes 4456448 | tf_op jit(solution)/shard_map/all_gather | solution.py:204
  131.1 11.5 %collective-permute-start = (bf16[128,1536]{1,0:T(8,128)(2,1)}, bf16[128,1536]{1,0:T(8,128)(2,1)S(1)}, u32[]{:S(2)}, u32[]{:S(2)}) collective-permute-start(bf16[128,1536]{1,0:T(8,128)(2,1)} %shard_map.86.att_ref), channel_id=1, source_target_pairs={{0,1},{1,0},{2,3},{3,2},{4,5},{5,4},{6,7},{7,6},{8,9},{9,8},{10,11... | collective-permute-start | bytes 1179656 | tf_op jit(solution)/shard_map/ppermute | solution.py:186
  142.6 0.7 copy-start.2
  148.3 11.9 %copy-start.4 = (f32[3072]{0:T(1024)S(1)}, f32[3072]{0:T(1024)}, u32[]{:S(2)}) copy-start(f32[3072]{0:T(1024)} %param.12) | copy-start | bytes 36868
  148.3 10.6 %collective-permute-start.1 = (bf16[128,1536]{1,0:T(8,128)(2,1)}, bf16[128,1536]{1,0:T(8,128)(2,1)S(1)}, u32[]{:S(2)}, u32[]{:S(2)}) collective-permute-start(bf16[128,1536]{1,0:T(8,128)(2,1)} %shard_map.88), channel_id=1, source_target_pairs={{0,1},{1,0},{2,3},{3,2},{4,5},{5,4},{6,7},{7,6},{8,9},{9,8},{10,11... | collective-permute-start | bytes 1179656 | tf_op jit(solution)/shard_map/ppermute | solution.py:151
  160.2 5.8 %copy-start.3 = (f32[3072]{0:T(1024)S(1)}, f32[3072]{0:T(1024)}, u32[]{:S(2)}) copy-start(f32[3072]{0:T(1024)} %param.11) | copy-start | bytes 36868
  166.0 63.1 %copy-start.1 = (bf16[128,1024]{1,0:T(8,128)(2,1)S(1)}, bf16[128,1024]{1,0:T(8,128)(2,1)}, u32[]{:S(2)}) copy-start(bf16[128,1024]{1,0:T(8,128)(2,1)} %param.9) | copy-start | bytes 786436
Sparse Core Ops, SparseCore 0:
  10.3 109.5 all-gather.5
  166.1 48.5 all-gather.3

commit v7 on v6

--- a/solution.py
+++ b/solution.py
@@ -145,10 +145,19 @@
     return x.reshape(rows, cols // HD, HD).transpose(1, 0, 2).reshape(-1, HD)
 
 
+def swap_heads(x):
+    half = x.shape[1] // 2
+    pieces = [
+        lax.ppermute(x[:, :half], "heads", [(0, 1), (1, 0)]),
+        lax.ppermute(x[:, half:], "heads", [(0, 1), (1, 0)]),
+    ]
+    return jnp.concatenate(pieces, axis=1)
+
+
 def make_body(heads_count):
     def gather_heads(x):
         if heads_count == 2:
-            other = lax.ppermute(x, "heads", [(0, 1), (1, 0)])
+            other = swap_heads(x)
             first = lax.axis_index("heads") == 0
             low = jnp.where(first, x, other)
             high = jnp.where(first, other, x)
@@ -183,7 +192,7 @@
         attended = attend(first_pos, self_queries, slab, WINDOW, False, groups, offset)
         if heads_count == 2:
             place = lax.axis_index("heads")
-            other = lax.ppermute(attended, "heads", [(0, 1), (1, 0)])
+            other = swap_heads(attended)
             width = residual_in.shape[1]
             own_part = project_half(
                 place.astype(jnp.int32).reshape(1), attended, slab,

time: 237 us -> 238 us (level)
    ppermute x2 -> x4, waiting for transfers between devices: 14.3 us -> 12.8 us  [the longest x2 6.65 us: swap_heads(): lax.ppermute(x[:, :half], 'heads', [(0, 1), (1, 0)])]
    unnamed x11 -> x12, local copies, waits for them, and re-layouts: 21.6 us -> 20.9 us
  transfers between devices with their start and end apart: 4 -> 6, of which waited for: 4 -> 6; matrix products, arithmetic and copies ran while one was open for 18% -> 18% of each run, Pallas kernels for 2% -> 2%
where the time goes in v7:
time: 238 us; the launch traced here: 237 us
  waiting for transfers between devices  129 us (54%)
  local copies, waits for them, and re-layouts  38.9 us (16%)
  Pallas kernels  35.4 us (15%)
  between operations  14.1 us (6%)
  matrix products  13.6 us (6%)
  starting transfers between devices  4.26 us (2%)
    all_gather x1, waiting for transfers between devices, body(): slab = lax.all_gather(packed[None], 'seq', axis=0, tiled=True)  75 us
    all_gather x1, waiting for transfers between devices, body(): lax.all_gather(shared.astype(jnp.bfloat16), 'seq', axis=0, tiled=True)  40.8 us
    pallas_call x2, Pallas kernels, attend(): pl.pallas_call(kernel, out_shape=jax.ShapeDtypeStruct((rows, qcols), jnp....  25.6 us
    unnamed x12, local copies, waits for them, and re-layouts  20.9 us
    pallas_call x2, Pallas kernels, project_half(): pl.pallas_call(functools.partial(_half_kernel, weight_rows=weight_rows),...  9.79 us
    slice x1, local copies, waits for them, and re-layouts, body(): col_layout[:, :, :QPK].reshape(cross_weight.shape[0], groups * QPK * HD)  8.24 us
    dot_general x1, matrix products, body(): cross_q = jnp.dot(normed_q, weight_q, preferred_element_type=jnp.float32)  7.87 us
    ppermute x2, waiting for transfers between devices, swap_heads(): lax.ppermute(x[:, :half], 'heads', [(0, 1), (1, 0)])  6.65 us
  transfers between devices with their start and end apart: 6, of which 6 were waited for; matrix products, arithmetic and copies ran while one was open for 18% of the time, Pallas kernels for 2%

profile of v7, /device:TPU:0, one launch (start us, length us, event | category | flops | bytes accessed | tf_op | source)
XLA Modules:
  0.0 236.8 jit_solution(528381663917701043)
XLA Ops:
  7.2 0.0 copy-start
  7.2 0.0 all-gather.6.cloned.1.call-start
  7.2 1.5 reshape.46
  8.8 0.2 copy.13
  8.9 0.0 copy-done
  9.0 1.0 pad_maximum_fusion
  10.0 0.0 all-gather.6.cloned.1.call-update
  10.0 0.0 all-gather.4.cloned.1.call-start
  10.0 20.8 %copy.15 = bf16[3072,2560]{0,1:T(8,128)(2,1)} copy(bf16[3072,2560]{1,0:T(8,128)(2,1)} %param.13) | data formatting | bytes 31457280 | tf_op args[6]
  30.9 8.2 %slice.25 = bf16[3072,4,3,128]{0,3,2,1:T(8,128)(2,1)} slice(bf16[3072,4,5,128]{0,3,2,1:T(8,128)(2,1)} %bitcast.22), slice={[0:3072], [0:4], [0:3], [0:128]} | slice | bytes 18874368 | tf_op jit(solution)/shard_map/slice | solution.py:190
  39.1 5.9 %slice.24 = bf16[3072,4,2,128]{0,3,2,1:T(8,128)(2,1)} slice(bf16[3072,4,5,128]{0,3,2,1:T(8,128)(2,1)} %bitcast.23), slice={[0:3072], [0:4], [3:5], [0:128]} | slice | bytes 12582912 | tf_op jit(solution)/shard_map/slice | solution.py:189
  45.0 75.0 %all-gather.6.cloned.1.call-done = bf16[53248,128]{1,0:T(8,128)(2,1)} async-done(((bf16[3328,128]{1,0:T(8,128)(2,1)}), bf16[53248,128]{1,0:T(8,128)(2,1)}) %all-gather.6.cloned.1.call-update) | async-done | bytes 13631504 | tf_op jit(solution)/shard_map/all_gather | solution.py:187
  119.9 11.2 %shard_map.86.att_ref = bf16[128,1536]{1,0:T(8,128)(2,1)} custom-call(s32[1]{0:T(128)} %bitcast.1.pos_ref, bf16[128,1536]{1,0:T(8,128)(2,1)} %q_ref.1, bf16[16,3328,128]{2,1,0:T(8,128)(2,1)} %bitcast.19), custom_call_target="tpu_custom_call" | custom-call | tf_op jit(solution)/shard_map/pallas_call | solution.py:71
  131.1 1.0 fusion.15
  132.2 1.5 collective-permute-start
  133.7 0.6 collective-permute-start.1
  134.2 4.8 %shard_map.87.refs_0_ = f32[128,1536]{1,0:T(8,128)} custom-call(s32[1]{0:T(128)} %bitcast.10.sel_ref, bf16[128,1536]{1,0:T(8,128)(2,1)} %shard_map.86.att_ref, bf16[16,3328,128]{2,1,0:T(8,128)(2,1)} %bitcast.20), custom_call_target="tpu_custom_call" | custom-call | tf_op jit(solution)/shard_map/pallas_call | solution.py:127
  139.1 0.9 collective-permute-done
  140.0 3.5 %collective-permute-done.1 = bf16[128,768]{1,0:T(8,128)(2,1)S(1)} collective-permute-done((bf16[128,768]{1,0:T(8,128)(2,1)S(1)}, bf16[128,768]{1,0:T(8,128)(2,1)S(1)}, u32[]{:S(2)}, u32[]{:S(2)}) %collective-permute-start.1) | collective-permute-done | bytes 196640 | tf_op jit(solution)/shard_map/ppermute | solution.py:152
  143.5 0.8 pad_maximum_fusion.2.att_ref
  144.3 4.9 %shard_map.88 = bf16[128,1536]{1,0:T(8,128)(2,1)} custom-call(s32[1]{0:T(128)} %bitcast.sel_ref, bf16[128,1536]{1,0:T(8,128)(2,1)} %pad_maximum_fusion.2.att_ref, bf16[16,3328,128]{2,1,0:T(8,128)(2,1)} %bitcast.21, f32[128,1536]{1,0:T(8,128)} %shard_map.87.refs_0_, bf16[128,1536]{1,0:T(8,128)(2,1)} %refs_1_.1), custom_call_target="tpu_custom_call" | custom-call | tf_op jit(solution)/shard_map/pallas_call | solution.py:127
  149.2 0.0 copy-start.2
  149.2 1.1 fusion.14
  150.3 1.5 collective-permute-start.2
  151.9 0.6 collective-permute-start.3
  152.4 0.0 copy-start.4
  152.4 5.7 %collective-permute-done.2 = bf16[128,768]{1,0:T(8,128)(2,1)S(1)} collective-permute-done((bf16[128,768]{1,0:T(8,128)(2,1)S(1)}, bf16[128,768]{1,0:T(8,128)(2,1)S(1)}, u32[]{:S(2)}, u32[]{:S(2)}) %collective-permute-start.2) | collective-permute-done | bytes 196640 | tf_op jit(solution)/shard_map/ppermute | solution.py:151
  158.2 2.6 %collective-permute-done.3 = bf16[128,768]{1,0:T(8,128)(2,1)S(1)} collective-permute-done((bf16[128,768]{1,0:T(8,128)(2,1)S(1)}, bf16[128,768]{1,0:T(8,128)(2,1)S(1)}, u32[]{:S(2)}, u32[]{:S(2)}) %collective-permute-start.3) | collective-permute-done | bytes 196640 | tf_op jit(solution)/shard_map/ppermute | solution.py:152
  160.8 0.0 copy-done.2
  160.8 0.1 broadcast_select_fusion.1
  160.9 0.2 fusion.4
  161.1 0.0 copy-done.4
  161.1 0.0 copy-start.3
  161.2 5.7 %convolution_convert_fusion = bf16[128,1024]{1,0:T(8,128)(2,1)} fusion(bf16[3072,1024]{0,1:T(8,128)(2,1)} %bitcast.25, f32[3072]{0:T(1024)S(1)} %copy-done.4, f32[128]{0:T(128)S(1)} %add_rsqrt_fusion, bf16[128,1536]{1,0:T(8,128)(2,1)S(1)} %get-tuple-element.9, bf16[128,1536]{1,0:T(8,128)(2,1)S(1)} %get-tuple-element.8), kind=kOutput, calls=%fused_computation.7 | convolution fusion | flops 808189952 | bytes 7352832 | tf_op jit(solution)/shard_map/dot_general | solution.py:212
  166.9 0.0 all-gather.4.cloned.1.call-update
  166.9 0.0 copy-done.3
  166.9 0.0 copy-start.1
  166.9 7.9 %fusion.6.q_ref = f32[128,1536]{1,0:T(8,128)} fusion(bf16[3072,1536]{0,1:T(8,128)(2,1)} %bitcast.24, f32[3072]{0:T(1024)S(1)} %copy-done.3, f32[128]{0:T(128)S(1)} %add_rsqrt_fusion, bf16[128,1536]{1,0:T(8,128)(2,1)S(1)} %get-tuple-element.9, bf16[128,1536]{1,0:T(8,128)(2,1)S(1)} %get-tuple-element.8), kind=kOutput, calls=%fused_computation.9 | convolution fusion | flops 1210712064 | bytes 11022848 | tf_op jit(solution)/shard_map/dot_general | solution.py:214
  174.8 40.8 %all-gather.4.cloned.1.call-done.kv_ref = bf16[2048,1024]{1,0:T(8,128)(2,1)} async-done(((bf16[128,1024]{1,0:T(8,128)(2,1)}), bf16[2048,1024]{1,0:T(8,128)(2,1)}) %all-gather.4.cloned.1.call-update) | async-done | bytes 4194320 | tf_op jit(solution)/shard_map/all_gather | solution.py:213
  215.6 14.4 %shard_map.89 = bf16[128,1536]{1,0:T(8,128)(2,1)} custom-call(s32[1]{0:T(128)} %bitcast.1.pos_ref, f32[128,1536]{1,0:T(8,128)} %fusion.6.q_ref, bf16[2048,1024]{1,0:T(8,128)(2,1)} %all-gather.4.cloned.1.call-done.kv_ref), custom_call_target="tpu_custom_call" | custom-call | tf_op jit(solution)/shard_map/pallas_call | solution.py:71
  230.0 0.0 copy-done.1
  (4 shorter events, 0.1 us)
Async XLA Ops:
  7.2 1.8 copy-start
  7.2 112.7 %all-gather.6.cloned.1.call-start = ((), (), s32[]{:S(2)}) async-start(), calls=%async_computation.1 | async-start | bytes 14483456 | tf_op jit(solution)/shard_map/all_gather | solution.py:187
  10.0 205.6 %all-gather.4.cloned.1.call-start = ((), (), s32[]{:S(2)}) async-start(), calls=%async_computation | async-start | bytes 4456448 | tf_op jit(solution)/shard_map/all_gather | solution.py:213
  132.2 7.8 %collective-permute-start = (bf16[128,768]{1,0:T(8,128)(2,1)S(1)}, bf16[128,768]{1,0:T(8,128)(2,1)S(1)}, u32[]{:S(2)}, u32[]{:S(2)}) collective-permute-start(bf16[128,768]{1,0:T(8,128)(2,1)S(1)} %get-tuple-element.12), channel_id=1, source_target_pairs={{0,1},{1,0},{2,3},{3,2},{4,5},{5,4},{6,7},{7,6},{8,9},{9,8},{10,11... | collective-permute-start | bytes 589832 | tf_op jit(solution)/shard_map/ppermute | solution.py:151
  133.7 9.8 %collective-permute-start.1 = (bf16[128,768]{1,0:T(8,128)(2,1)S(1)}, bf16[128,768]{1,0:T(8,128)(2,1)S(1)}, u32[]{:S(2)}, u32[]{:S(2)}) collective-permute-start(bf16[128,768]{1,0:T(8,128)(2,1)S(1)} %get-tuple-element.13), channel_id=1, source_target_pairs={{0,1},{1,0},{2,3},{3,2},{4,5},{5,4},{6,7},{7,6},{8,9},{9,8},{10,11... | collective-permute-start | bytes 589832 | tf_op jit(solution)/shard_map/ppermute | solution.py:152
  149.2 11.6 %copy-start.2 = (bf16[128,1536]{1,0:T(8,128)(2,1)S(1)}, bf16[128,1536]{1,0:T(8,128)(2,1)}, u32[]{:S(2)}) copy-start(bf16[128,1536]{1,0:T(8,128)(2,1)} %shard_map.88) | copy-start | bytes 1179652
  150.3 7.8 %collective-permute-start.2 = (bf16[128,768]{1,0:T(8,128)(2,1)S(1)}, bf16[128,768]{1,0:T(8,128)(2,1)S(1)}, u32[]{:S(2)}, u32[]{:S(2)}) collective-permute-start(bf16[128,768]{1,0:T(8,128)(2,1)S(1)} %get-tuple-element.11), channel_id=1, source_target_pairs={{0,1},{1,0},{2,3},{3,2},{4,5},{5,4},{6,7},{7,6},{8,9},{9,8},{10,11... | collective-permute-start | bytes 589832 | tf_op jit(solution)/shard_map/ppermute | solution.py:151
  151.9 8.9 %collective-permute-start.3 = (bf16[128,768]{1,0:T(8,128)(2,1)S(1)}, bf16[128,768]{1,0:T(8,128)(2,1)S(1)}, u32[]{:S(2)}, u32[]{:S(2)}) collective-permute-start(bf16[128,768]{1,0:T(8,128)(2,1)S(1)} %get-tuple-element.10), channel_id=1, source_target_pairs={{0,1},{1,0},{2,3},{3,2},{4,5},{5,4},{6,7},{7,6},{8,9},{9,8},{10,11... | collective-permute-start | bytes 589832 | tf_op jit(solution)/shard_map/ppermute | solution.py:152
  152.4 8.7 %copy-start.4 = (f32[3072]{0:T(1024)S(1)}, f32[3072]{0:T(1024)}, u32[]{:S(2)}) copy-start(f32[3072]{0:T(1024)} %param.12) | copy-start | bytes 36868
  161.1 5.8 %copy-start.3 = (f32[3072]{0:T(1024)S(1)}, f32[3072]{0:T(1024)}, u32[]{:S(2)}) copy-start(f32[3072]{0:T(1024)} %param.11) | copy-start | bytes 36868
  166.9 63.1 %copy-start.1 = (bf16[128,1024]{1,0:T(8,128)(2,1)S(1)}, bf16[128,1024]{1,0:T(8,128)(2,1)}, u32[]{:S(2)}) copy-start(bf16[128,1024]{1,0:T(8,128)(2,1)} %param.9) | copy-start | bytes 786436
Sparse Core Ops, SparseCore 0:
  10.3 109.5 all-gather.5
  167.0 48.5 all-gather.3

commit v8 on v6

--- a/solution.py
+++ b/solution.py
@@ -19,15 +19,18 @@
     return high, low
 
 
-def _attend_kernel(pos_ref, q_ref, kv_ref, o_ref, *, window, exact):
-    rows = q_ref.shape[0]
-    keys = kv_ref.shape[0] * (kv_ref.shape[1] // 2 if len(kv_ref.shape) == 3 else 1)
-    first = pos_ref[0]
-    query_pos = first + lax.broadcasted_iota(jnp.int32, (rows, keys), 0)
-    key_pos = lax.broadcasted_iota(jnp.int32, (rows, keys), 1)
-    allowed = key_pos <= query_pos
-    if window is not None:
-        allowed = allowed & (key_pos > query_pos - window)
+def _attend_kernel(pos_ref, q_ref, kv_ref, o_ref, bias_ref, *, window, exact):
+    rows, keys = bias_ref.shape
+
+    @pl.when(pl.program_id(0) == 0)
+    def _():
+        query_pos = pos_ref[0] + lax.broadcasted_iota(jnp.int32, (rows, keys), 0)
+        key_pos = lax.broadcasted_iota(jnp.int32, (rows, keys), 1)
+        allowed = key_pos <= query_pos
+        if window is not None:
+            allowed = allowed & (key_pos > query_pos - window)
+        bias_ref[...] = jnp.where(allowed, 0.0, -jnp.inf)
+
     if len(kv_ref.shape) == 3:
         half = kv_ref.shape[1] // 2
         key = kv_ref[:, :half, :].reshape(-1, HD)
@@ -45,10 +48,9 @@
             scores = scores + lax.dot_general(q_lo, key, contract, preferred_element_type=jnp.float32)
         else:
             scores = lax.dot_general(query, key, contract, preferred_element_type=jnp.float32)
-        scores = scores * score_scale
-        masked = jnp.where(allowed, scores, -jnp.inf)
+        masked = scores * score_scale + bias_ref[...]
         row_top = jnp.max(masked, axis=-1, keepdims=True)
-        weights = jnp.where(allowed, jnp.exp(masked - row_top), 0.0)
+        weights = jnp.exp(masked - row_top)
         totals = jnp.sum(weights, axis=-1, keepdims=True)
         if exact:
             w_hi, w_lo = _split(weights)
@@ -67,6 +69,7 @@
     else:
         kv_spec = pl.BlockSpec((pairs.shape[0], 2 * rows, HD), lambda g, pos: (0, offset + g, 0))
     qblock = qcols // groups
+    keys = pairs.shape[0] * (rows if pairs.ndim == 3 else 1)
     kernel = functools.partial(_attend_kernel, window=window, exact=exact)
     return pl.pallas_call(
         kernel,
@@ -79,6 +82,7 @@
                 kv_spec,
             ],
             out_specs=pl.BlockSpec((rows, qblock), lambda g, pos: (0, g)),
+            scratch_shapes=[pltpu.VMEM((rows, keys), jnp.float32)],
         ),
     )(first_pos, queries, pairs)
 

time: 237 us -> 233 us (0.983)
  Pallas kernels: 35.4 us -> 32 us
    pallas_call x2, Pallas kernels: 25.6 us -> 22.2 us  [attend(): pl.pallas_call(kernel, out_shape=jax.ShapeDtypeStruct((rows, qcols), jnp....]
where the time goes in v8:
time: 233 us
  waiting for transfers between devices  130 us (56%)
  local copies, waits for them, and re-layouts  37.4 us (16%)
  Pallas kernels  32 us (14%)
  between operations  14.1 us (6%)
  matrix products  13.6 us (6%)
  starting transfers between devices  3.02 us (1%)
    all_gather x1, waiting for transfers between devices, body(): slab = lax.all_gather(packed[None], 'seq', axis=0, tiled=True)  75 us
    all_gather x1, waiting for transfers between devices, body(): lax.all_gather(shared.astype(jnp.bfloat16), 'seq', axis=0, tiled=True)  40.8 us
    pallas_call x2, Pallas kernels, attend(): pl.pallas_call(kernel, out_shape=jax.ShapeDtypeStruct((rows, qcols), jnp....  22.2 us
    unnamed x11, local copies, waits for them, and re-layouts  21.6 us
    pallas_call x2, Pallas kernels, project_half(): pl.pallas_call(functools.partial(_half_kernel, weight_rows=weight_rows),...  9.8 us
    ppermute x1, waiting for transfers between devices, gather_heads(): other = lax.ppermute(x, 'heads', [(0, 1), (1, 0)])  9.15 us
    slice x1, local copies, waits for them, and re-layouts, body(): col_layout[:, :, :QPK].reshape(cross_weight.shape[0], groups * QPK * HD)  8.24 us
    dot_general x1, matrix products, body(): cross_q = jnp.dot(normed_q, weight_q, preferred_element_type=jnp.float32)  7.86 us
  transfers between devices with their start and end apart: 4, of which 4 were waited for; matrix products, arithmetic and copies ran while one was open for 18% of the time, Pallas kernels for 2%

profile of v8, /device:TPU:0, one launch (start us, length us, event | category | flops | bytes accessed | tf_op | source)
XLA Modules:
  0.0 232.6 jit_solution(8641890595814134975)
XLA Ops:
  7.2 0.0 copy-start
  7.2 0.0 all-gather.6.cloned.1.call-start
  7.2 1.5 reshape.46
  8.8 0.2 copy.13
  8.9 0.0 copy-done
  9.0 0.9 pad_maximum_fusion
  9.9 0.0 all-gather.6.cloned.1.call-update
  10.0 0.0 all-gather.4.cloned.1.call-start
  10.0 20.8 %copy.15 = bf16[3072,2560]{0,1:T(8,128)(2,1)} copy(bf16[3072,2560]{1,0:T(8,128)(2,1)} %param.13) | data formatting | bytes 31457280 | tf_op args[6]
  30.8 8.2 %slice.9 = bf16[3072,4,3,128]{0,3,2,1:T(8,128)(2,1)} slice(bf16[3072,4,5,128]{0,3,2,1:T(8,128)(2,1)} %bitcast.22), slice={[0:3072], [0:4], [0:3], [0:128]} | slice | bytes 18874368 | tf_op jit(solution)/shard_map/slice | solution.py:185
  39.1 5.9 %slice.8 = bf16[3072,4,2,128]{0,3,2,1:T(8,128)(2,1)} slice(bf16[3072,4,5,128]{0,3,2,1:T(8,128)(2,1)} %bitcast.23), slice={[0:3072], [0:4], [3:5], [0:128]} | slice | bytes 12582912 | tf_op jit(solution)/shard_map/slice | solution.py:184
  44.9 75.0 %all-gather.6.cloned.1.call-done = bf16[53248,128]{1,0:T(8,128)(2,1)} async-done(((bf16[3328,128]{1,0:T(8,128)(2,1)}), bf16[53248,128]{1,0:T(8,128)(2,1)}) %all-gather.6.cloned.1.call-update) | async-done | bytes 13631504 | tf_op jit(solution)/shard_map/all_gather | solution.py:182
  119.9 9.2 %shard_map.86.att_ref = bf16[128,1536]{1,0:T(8,128)(2,1)} custom-call(s32[1]{0:T(128)} %bitcast.1.pos_ref, bf16[128,1536]{1,0:T(8,128)(2,1)} %q_ref.1, bf16[16,3328,128]{2,1,0:T(8,128)(2,1)} %bitcast.19), custom_call_target="tpu_custom_call" | custom-call | tf_op jit(solution)/shard_map/pallas_call | solution.py:74
  129.1 1.5 collective-permute-start
  130.6 4.8 %shard_map.87.refs_0_ = f32[128,1536]{1,0:T(8,128)} custom-call(s32[1]{0:T(128)} %bitcast.10.sel_ref, bf16[128,1536]{1,0:T(8,128)(2,1)} %shard_map.86.att_ref, bf16[16,3328,128]{2,1,0:T(8,128)(2,1)} %bitcast.20), custom_call_target="tpu_custom_call" | custom-call | tf_op jit(solution)/shard_map/pallas_call | solution.py:131
  135.4 5.2 %collective-permute-done.att_ref = bf16[128,1536]{1,0:T(8,128)(2,1)S(1)} collective-permute-done((bf16[128,1536]{1,0:T(8,128)(2,1)}, bf16[128,1536]{1,0:T(8,128)(2,1)S(1)}, u32[]{:S(2)}, u32[]{:S(2)}) %collective-permute-start) | collective-permute-done | bytes 393248 | tf_op jit(solution)/shard_map/ppermute | solution.py:190
  140.6 0.0 copy-start.2
  140.6 0.7 copy-done.2
  141.3 4.9 %shard_map.88 = bf16[128,1536]{1,0:T(8,128)(2,1)} custom-call(s32[1]{0:T(128)} %bitcast.sel_ref, bf16[128,1536]{1,0:T(8,128)(2,1)} %copy-done.2, bf16[16,3328,128]{2,1,0:T(8,128)(2,1)} %bitcast.21, f32[128,1536]{1,0:T(8,128)} %shard_map.87.refs_0_, bf16[128,1536]{1,0:T(8,128)(2,1)} %refs_1_.1), custom_call_target="tpu_custom_call" | custom-call | tf_op jit(solution)/shard_map/pallas_call | solution.py:131
  146.3 0.0 copy-start.4
  146.3 1.5 collective-permute-start.1
  147.7 9.1 %collective-permute-done.1 = bf16[128,1536]{1,0:T(8,128)(2,1)S(1)} collective-permute-done((bf16[128,1536]{1,0:T(8,128)(2,1)}, bf16[128,1536]{1,0:T(8,128)(2,1)S(1)}, u32[]{:S(2)}, u32[]{:S(2)}) %collective-permute-start.1) | collective-permute-done | bytes 393248 | tf_op jit(solution)/shard_map/ppermute | solution.py:155
  156.9 1.1 broadcast_select_fusion.1
  157.9 0.2 fusion.4
  158.2 0.0 copy-done.4
  158.2 0.0 copy-start.3
  158.2 5.7 %convolution_convert_fusion = bf16[128,1024]{1,0:T(8,128)(2,1)} fusion(bf16[3072,1024]{0,1:T(8,128)(2,1)} %bitcast.25, f32[3072]{0:T(1024)S(1)} %copy-done.4, f32[128]{0:T(128)S(1)} %add_rsqrt_fusion, bf16[128,1536]{1,0:T(8,128)(2,1)S(1)} %get-tuple-element.9, bf16[128,1536]{1,0:T(8,128)(2,1)S(1)} %get-tuple-element.8), kind=kOutput, calls=%fused_computation.7 | convolution fusion | flops 808189952 | bytes 7352832 | tf_op jit(solution)/shard_map/dot_general | solution.py:207
  163.9 0.0 all-gather.4.cloned.1.call-update
  164.0 0.0 copy-done.3
  164.0 0.0 copy-start.1
  164.0 7.9 %fusion.6.q_ref = f32[128,1536]{1,0:T(8,128)} fusion(bf16[3072,1536]{0,1:T(8,128)(2,1)} %bitcast.24, f32[3072]{0:T(1024)S(1)} %copy-done.3, f32[128]{0:T(128)S(1)} %add_rsqrt_fusion, bf16[128,1536]{1,0:T(8,128)(2,1)S(1)} %get-tuple-element.9, bf16[128,1536]{1,0:T(8,128)(2,1)S(1)} %get-tuple-element.8), kind=kOutput, calls=%fused_computation.9 | convolution fusion | flops 1210712064 | bytes 11022848 | tf_op jit(solution)/shard_map/dot_general | solution.py:209
  171.8 40.8 %all-gather.4.cloned.1.call-done.kv_ref = bf16[2048,1024]{1,0:T(8,128)(2,1)} async-done(((bf16[128,1024]{1,0:T(8,128)(2,1)}), bf16[2048,1024]{1,0:T(8,128)(2,1)}) %all-gather.4.cloned.1.call-update) | async-done | bytes 4194320 | tf_op jit(solution)/shard_map/all_gather | solution.py:208
  212.7 13.0 %shard_map.89 = bf16[128,1536]{1,0:T(8,128)(2,1)} custom-call(s32[1]{0:T(128)} %bitcast.1.pos_ref, f32[128,1536]{1,0:T(8,128)} %fusion.6.q_ref, bf16[2048,1024]{1,0:T(8,128)(2,1)} %all-gather.4.cloned.1.call-done.kv_ref), custom_call_target="tpu_custom_call" | custom-call | tf_op jit(solution)/shard_map/pallas_call | solution.py:74
  225.7 0.0 copy-done.1
  (2 shorter events, 0.1 us)
Async XLA Ops:
  7.2 1.8 copy-start
  7.2 112.7 %all-gather.6.cloned.1.call-start = ((), (), s32[]{:S(2)}) async-start(), calls=%async_computation.1 | async-start | bytes 14483456 | tf_op jit(solution)/shard_map/all_gather | solution.py:182
  10.0 202.7 %all-gather.4.cloned.1.call-start = ((), (), s32[]{:S(2)}) async-start(), calls=%async_computation | async-start | bytes 4456448 | tf_op jit(solution)/shard_map/all_gather | solution.py:208
  129.1 11.5 %collective-permute-start = (bf16[128,1536]{1,0:T(8,128)(2,1)}, bf16[128,1536]{1,0:T(8,128)(2,1)S(1)}, u32[]{:S(2)}, u32[]{:S(2)}) collective-permute-start(bf16[128,1536]{1,0:T(8,128)(2,1)} %shard_map.86.att_ref), channel_id=1, source_target_pairs={{0,1},{1,0},{2,3},{3,2},{4,5},{5,4},{6,7},{7,6},{8,9},{9,8},{10,11... | collective-permute-start | bytes 1179656 | tf_op jit(solution)/shard_map/ppermute | solution.py:190
  140.6 0.7 copy-start.2
  146.3 11.9 %copy-start.4 = (f32[3072]{0:T(1024)S(1)}, f32[3072]{0:T(1024)}, u32[]{:S(2)}) copy-start(f32[3072]{0:T(1024)} %param.12) | copy-start | bytes 36868
  146.3 10.6 %collective-permute-start.1 = (bf16[128,1536]{1,0:T(8,128)(2,1)}, bf16[128,1536]{1,0:T(8,128)(2,1)S(1)}, u32[]{:S(2)}, u32[]{:S(2)}) collective-permute-start(bf16[128,1536]{1,0:T(8,128)(2,1)} %shard_map.88), channel_id=1, source_target_pairs={{0,1},{1,0},{2,3},{3,2},{4,5},{5,4},{6,7},{7,6},{8,9},{9,8},{10,11... | collective-permute-start | bytes 1179656 | tf_op jit(solution)/shard_map/ppermute | solution.py:155
  158.2 5.8 %copy-start.3 = (f32[3072]{0:T(1024)S(1)}, f32[3072]{0:T(1024)}, u32[]{:S(2)}) copy-start(f32[3072]{0:T(1024)} %param.11) | copy-start | bytes 36868
  164.0 61.7 %copy-start.1 = (bf16[128,1024]{1,0:T(8,128)(2,1)S(1)}, bf16[128,1024]{1,0:T(8,128)(2,1)}, u32[]{:S(2)}) copy-start(bf16[128,1024]{1,0:T(8,128)(2,1)} %param.9) | copy-start | bytes 786436
Sparse Core Ops, SparseCore 0:
  10.3 109.5 all-gather.5
  164.1 48.5 all-gather.3

commit v9 on v8

--- a/solution.py
+++ b/solution.py
@@ -52,12 +52,7 @@
         row_top = jnp.max(masked, axis=-1, keepdims=True)
         weights = jnp.exp(masked - row_top)
         totals = jnp.sum(weights, axis=-1, keepdims=True)
-        if exact:
-            w_hi, w_lo = _split(weights)
-            acc = jnp.dot(w_hi, value, preferred_element_type=jnp.float32)
-            acc = acc + jnp.dot(w_lo, value, preferred_element_type=jnp.float32)
-        else:
-            acc = jnp.dot(weights.astype(jnp.bfloat16), value, preferred_element_type=jnp.float32)
+        acc = jnp.dot(weights.astype(jnp.bfloat16), value, preferred_element_type=jnp.float32)
         o_ref[:, head * HD:(head + 1) * HD] = (acc / totals).astype(o_ref.dtype)
 
 

time: 233 us -> 231 us (level)
  transfers between devices with their start and end apart: 4 -> 4, of which waited for: 4 -> 4; matrix products, arithmetic and copies ran while one was open for 18% -> 19% of each run, Pallas kernels for 2% -> 2%
where the time goes in v9:
time: 231 us; the launch traced here: 230 us
  waiting for transfers between devices  130 us (56%)
  local copies, waits for them, and re-layouts  37.4 us (16%)
  Pallas kernels  29.7 us (13%)
  between operations  14.1 us (6%)
  matrix products  13.6 us (6%)
  starting transfers between devices  3.02 us (1%)
    all_gather x1, waiting for transfers between devices, body(): slab = lax.all_gather(packed[None], 'seq', axis=0, tiled=True)  75 us
    all_gather x1, waiting for transfers between devices, body(): lax.all_gather(shared.astype(jnp.bfloat16), 'seq', axis=0, tiled=True)  40.8 us
    unnamed x11, local copies, waits for them, and re-layouts  21.6 us
    pallas_call x2, Pallas kernels, attend(): pl.pallas_call(kernel, out_shape=jax.ShapeDtypeStruct((rows, qcols), jnp....  19.9 us
    pallas_call x2, Pallas kernels, project_half(): pl.pallas_call(functools.partial(_half_kernel, weight_rows=weight_rows),...  9.8 us
    ppermute x1, waiting for transfers between devices, gather_heads(): other = lax.ppermute(x, 'heads', [(0, 1), (1, 0)])  9.15 us
    slice x1, local copies, waits for them, and re-layouts, body(): col_layout[:, :, :QPK].reshape(cross_weight.shape[0], groups * QPK * HD)  8.24 us
    dot_general x1, matrix products, body(): cross_q = jnp.dot(normed_q, weight_q, preferred_element_type=jnp.float32)  7.86 us
  transfers between devices with their start and end apart: 4, of which 4 were waited for; matrix products, arithmetic and copies ran while one was open for 19% of the time, Pallas kernels for 2%

profile of v9, /device:TPU:0, one launch (start us, length us, event | category | flops | bytes accessed | tf_op | source)
XLA Modules:
  0.0 230.3 jit_solution(18413564055033393332)
XLA Ops:
  7.2 0.0 copy-start
  7.2 0.0 all-gather.6.cloned.1.call-start
  7.2 1.5 reshape.46
  8.8 0.2 copy.13
  8.9 0.0 copy-done
  9.0 0.9 pad_maximum_fusion
  9.9 0.0 all-gather.6.cloned.1.call-update
  10.0 0.0 all-gather.4.cloned.1.call-start
  10.0 20.8 %copy.15 = bf16[3072,2560]{0,1:T(8,128)(2,1)} copy(bf16[3072,2560]{1,0:T(8,128)(2,1)} %param.13) | data formatting | bytes 31457280 | tf_op args[6]
  30.8 8.2 %slice.9 = bf16[3072,4,3,128]{0,3,2,1:T(8,128)(2,1)} slice(bf16[3072,4,5,128]{0,3,2,1:T(8,128)(2,1)} %bitcast.22), slice={[0:3072], [0:4], [0:3], [0:128]} | slice | bytes 18874368 | tf_op jit(solution)/shard_map/slice | solution.py:180
  39.1 5.9 %slice.8 = bf16[3072,4,2,128]{0,3,2,1:T(8,128)(2,1)} slice(bf16[3072,4,5,128]{0,3,2,1:T(8,128)(2,1)} %bitcast.23), slice={[0:3072], [0:4], [3:5], [0:128]} | slice | bytes 12582912 | tf_op jit(solution)/shard_map/slice | solution.py:179
  44.9 75.0 %all-gather.6.cloned.1.call-done = bf16[53248,128]{1,0:T(8,128)(2,1)} async-done(((bf16[3328,128]{1,0:T(8,128)(2,1)}), bf16[53248,128]{1,0:T(8,128)(2,1)}) %all-gather.6.cloned.1.call-update) | async-done | bytes 13631504 | tf_op jit(solution)/shard_map/all_gather | solution.py:177
  119.9 9.2 %shard_map.86.att_ref = bf16[128,1536]{1,0:T(8,128)(2,1)} custom-call(s32[1]{0:T(128)} %bitcast.1.pos_ref, bf16[128,1536]{1,0:T(8,128)(2,1)} %q_ref.1, bf16[16,3328,128]{2,1,0:T(8,128)(2,1)} %bitcast.19), custom_call_target="tpu_custom_call" | custom-call | tf_op jit(solution)/shard_map/pallas_call | solution.py:69
  129.1 1.5 collective-permute-start
  130.6 4.8 %shard_map.87.refs_0_ = f32[128,1536]{1,0:T(8,128)} custom-call(s32[1]{0:T(128)} %bitcast.10.sel_ref, bf16[128,1536]{1,0:T(8,128)(2,1)} %shard_map.86.att_ref, bf16[16,3328,128]{2,1,0:T(8,128)(2,1)} %bitcast.20), custom_call_target="tpu_custom_call" | custom-call | tf_op jit(solution)/shard_map/pallas_call | solution.py:126
  135.4 5.2 %collective-permute-done.att_ref = bf16[128,1536]{1,0:T(8,128)(2,1)S(1)} collective-permute-done((bf16[128,1536]{1,0:T(8,128)(2,1)}, bf16[128,1536]{1,0:T(8,128)(2,1)S(1)}, u32[]{:S(2)}, u32[]{:S(2)}) %collective-permute-start) | collective-permute-done | bytes 393248 | tf_op jit(solution)/shard_map/ppermute | solution.py:185
  140.6 0.0 copy-start.2
  140.6 0.7 copy-done.2
  141.3 4.9 %shard_map.88 = bf16[128,1536]{1,0:T(8,128)(2,1)} custom-call(s32[1]{0:T(128)} %bitcast.sel_ref, bf16[128,1536]{1,0:T(8,128)(2,1)} %copy-done.2, bf16[16,3328,128]{2,1,0:T(8,128)(2,1)} %bitcast.21, f32[128,1536]{1,0:T(8,128)} %shard_map.87.refs_0_, bf16[128,1536]{1,0:T(8,128)(2,1)} %refs_1_.1), custom_call_target="tpu_custom_call" | custom-call | tf_op jit(solution)/shard_map/pallas_call | solution.py:126
  146.3 0.0 copy-start.4
  146.3 1.5 collective-permute-start.1
  147.7 9.1 %collective-permute-done.1 = bf16[128,1536]{1,0:T(8,128)(2,1)S(1)} collective-permute-done((bf16[128,1536]{1,0:T(8,128)(2,1)}, bf16[128,1536]{1,0:T(8,128)(2,1)S(1)}, u32[]{:S(2)}, u32[]{:S(2)}) %collective-permute-start.1) | collective-permute-done | bytes 393248 | tf_op jit(solution)/shard_map/ppermute | solution.py:150
  156.9 1.1 broadcast_select_fusion.1
  157.9 0.2 fusion.4
  158.2 0.0 copy-done.4
  158.2 0.0 copy-start.3
  158.2 5.7 %convolution_convert_fusion = bf16[128,1024]{1,0:T(8,128)(2,1)} fusion(bf16[3072,1024]{0,1:T(8,128)(2,1)} %bitcast.25, f32[3072]{0:T(1024)S(1)} %copy-done.4, f32[128]{0:T(128)S(1)} %add_rsqrt_fusion, bf16[128,1536]{1,0:T(8,128)(2,1)S(1)} %get-tuple-element.9, bf16[128,1536]{1,0:T(8,128)(2,1)S(1)} %get-tuple-element.8), kind=kOutput, calls=%fused_computation.7 | convolution fusion | flops 808189952 | bytes 7352832 | tf_op jit(solution)/shard_map/dot_general | solution.py:202
  163.9 0.0 all-gather.4.cloned.1.call-update
  164.0 0.0 copy-done.3
  164.0 0.0 copy-start.1
  164.0 7.9 %fusion.6.q_ref = f32[128,1536]{1,0:T(8,128)} fusion(bf16[3072,1536]{0,1:T(8,128)(2,1)} %bitcast.24, f32[3072]{0:T(1024)S(1)} %copy-done.3, f32[128]{0:T(128)S(1)} %add_rsqrt_fusion, bf16[128,1536]{1,0:T(8,128)(2,1)S(1)} %get-tuple-element.9, bf16[128,1536]{1,0:T(8,128)(2,1)S(1)} %get-tuple-element.8), kind=kOutput, calls=%fused_computation.9 | convolution fusion | flops 1210712064 | bytes 11022848 | tf_op jit(solution)/shard_map/dot_general | solution.py:204
  171.8 40.8 %all-gather.4.cloned.1.call-done.kv_ref = bf16[2048,1024]{1,0:T(8,128)(2,1)} async-done(((bf16[128,1024]{1,0:T(8,128)(2,1)}), bf16[2048,1024]{1,0:T(8,128)(2,1)}) %all-gather.4.cloned.1.call-update) | async-done | bytes 4194320 | tf_op jit(solution)/shard_map/all_gather | solution.py:203
  212.7 10.8 %shard_map.89 = bf16[128,1536]{1,0:T(8,128)(2,1)} custom-call(s32[1]{0:T(128)} %bitcast.1.pos_ref, f32[128,1536]{1,0:T(8,128)} %fusion.6.q_ref, bf16[2048,1024]{1,0:T(8,128)(2,1)} %all-gather.4.cloned.1.call-done.kv_ref), custom_call_target="tpu_custom_call" | custom-call | tf_op jit(solution)/shard_map/pallas_call | solution.py:69
  223.4 0.0 copy-done.1
  (2 shorter events, 0.1 us)
Async XLA Ops:
  7.2 1.8 copy-start
  7.2 112.7 %all-gather.6.cloned.1.call-start = ((), (), s32[]{:S(2)}) async-start(), calls=%async_computation.1 | async-start | bytes 14483456 | tf_op jit(solution)/shard_map/all_gather | solution.py:177
  10.0 202.7 %all-gather.4.cloned.1.call-start = ((), (), s32[]{:S(2)}) async-start(), calls=%async_computation | async-start | bytes 4456448 | tf_op jit(solution)/shard_map/all_gather | solution.py:203
  129.1 11.5 %collective-permute-start = (bf16[128,1536]{1,0:T(8,128)(2,1)}, bf16[128,1536]{1,0:T(8,128)(2,1)S(1)}, u32[]{:S(2)}, u32[]{:S(2)}) collective-permute-start(bf16[128,1536]{1,0:T(8,128)(2,1)} %shard_map.86.att_ref), channel_id=1, source_target_pairs={{0,1},{1,0},{2,3},{3,2},{4,5},{5,4},{6,7},{7,6},{8,9},{9,8},{10,11... | collective-permute-start | bytes 1179656 | tf_op jit(solution)/shard_map/ppermute | solution.py:185
  140.6 0.7 copy-start.2
  146.3 11.9 %copy-start.4 = (f32[3072]{0:T(1024)S(1)}, f32[3072]{0:T(1024)}, u32[]{:S(2)}) copy-start(f32[3072]{0:T(1024)} %param.12) | copy-start | bytes 36868
  146.3 10.6 %collective-permute-start.1 = (bf16[128,1536]{1,0:T(8,128)(2,1)}, bf16[128,1536]{1,0:T(8,128)(2,1)S(1)}, u32[]{:S(2)}, u32[]{:S(2)}) collective-permute-start(bf16[128,1536]{1,0:T(8,128)(2,1)} %shard_map.88), channel_id=1, source_target_pairs={{0,1},{1,0},{2,3},{3,2},{4,5},{5,4},{6,7},{7,6},{8,9},{9,8},{10,11... | collective-permute-start | bytes 1179656 | tf_op jit(solution)/shard_map/ppermute | solution.py:150
  158.2 5.8 %copy-start.3 = (f32[3072]{0:T(1024)S(1)}, f32[3072]{0:T(1024)}, u32[]{:S(2)}) copy-start(f32[3072]{0:T(1024)} %param.11) | copy-start | bytes 36868
  164.0 59.5 %copy-start.1 = (bf16[128,1024]{1,0:T(8,128)(2,1)S(1)}, bf16[128,1024]{1,0:T(8,128)(2,1)}, u32[]{:S(2)}) copy-start(bf16[128,1024]{1,0:T(8,128)(2,1)} %param.9) | copy-start | bytes 786436
Sparse Core Ops, SparseCore 0:
  10.3 109.5 all-gather.5
  164.1 48.5 all-gather.3

commit v10 on v9

--- a/solution.py
+++ b/solution.py
@@ -178,6 +178,14 @@
         col_layout = cross_weight.reshape(cross_weight.shape[0], groups, QPK + 2, HD)
         weight_kv = col_layout[:, :, QPK:].reshape(cross_weight.shape[0], groups * 2 * HD)
         weight_q = col_layout[:, :, :QPK].reshape(cross_weight.shape[0], groups * QPK * HD)
+        if heads_count == 2:
+            place = lax.axis_index("heads")
+            feats = residual_in.shape[1]
+            halves = [place * feats, (1 - place) * feats]
+            weight_kv = [lax.dynamic_slice_in_dim(weight_kv, at, feats, 0) for at in halves]
+            weight_q = [lax.dynamic_slice_in_dim(weight_q, at, feats, 0) for at in halves]
+            gains_kv = [lax.dynamic_slice_in_dim(gain_keyvalue, at, feats, 0) for at in halves]
+            gains_q = [lax.dynamic_slice_in_dim(gain_query, at, feats, 0) for at in halves]
         slab, weight_kv, weight_q = lax.optimization_barrier((slab, weight_kv, weight_q))
         attended = attend(first_pos, self_queries, slab, WINDOW, False, groups, offset)
         if heads_count == 2:
@@ -194,14 +202,37 @@
             )
         else:
             hidden = project(gather_heads(attended), slab, residual_in, weight_rows)
-        full_rows = gather_heads(hidden)
-        widened = full_rows.astype(jnp.float32)
-        inverse = lax.rsqrt(jnp.mean(widened * widened, axis=-1, keepdims=True) + 1e-06)
-        normed_q = (widened * inverse * gain_query).astype(jnp.bfloat16)
-        normed_kv = (widened * inverse * gain_keyvalue).astype(jnp.bfloat16)
-        shared = jnp.dot(normed_kv, weight_kv, preferred_element_type=jnp.float32)
-        shared_all = lax.all_gather(shared.astype(jnp.bfloat16), "seq", axis=0, tiled=True)
-        cross_q = jnp.dot(normed_q, weight_q, preferred_element_type=jnp.float32)
+        if heads_count == 2:
+            own = hidden.astype(jnp.float32)
+            own_squares = jnp.sum(own * own, axis=-1, keepdims=True)
+            other_squares = lax.ppermute(own_squares, "heads", [(0, 1), (1, 0)])
+            other = lax.ppermute(hidden, "heads", [(0, 1), (1, 0)]).astype(jnp.float32)
+            mean = (own_squares + other_squares) / (2 * own.shape[1])
+            inverse = lax.rsqrt(mean + 1e-06)
+            shared = jnp.dot(
+                (own * inverse * gains_kv[0]).astype(jnp.bfloat16), weight_kv[0],
+                preferred_element_type=jnp.float32,
+            ) + jnp.dot(
+                (other * inverse * gains_kv[1]).astype(jnp.bfloat16), weight_kv[1],
+                preferred_element_type=jnp.float32,
+            )
+            shared_all = lax.all_gather(shared.astype(jnp.bfloat16), "seq", axis=0, tiled=True)
+            cross_q = jnp.dot(
+                (own * inverse * gains_q[0]).astype(jnp.bfloat16), weight_q[0],
+                preferred_element_type=jnp.float32,
+            ) + jnp.dot(
+                (other * inverse * gains_q[1]).astype(jnp.bfloat16), weight_q[1],
+                preferred_element_type=jnp.float32,
+            )
+        else:
+            full_rows = gather_heads(hidden)
+            widened = full_rows.astype(jnp.float32)
+            inverse = lax.rsqrt(jnp.mean(widened * widened, axis=-1, keepdims=True) + 1e-06)
+            normed_q = (widened * inverse * gain_query).astype(jnp.bfloat16)
+            normed_kv = (widened * inverse * gain_keyvalue).astype(jnp.bfloat16)
+            shared = jnp.dot(normed_kv, weight_kv, preferred_element_type=jnp.float32)
+            shared_all = lax.all_gather(shared.astype(jnp.bfloat16), "seq", axis=0, tiled=True)
+            cross_q = jnp.dot(normed_q, weight_q, preferred_element_type=jnp.float32)
         cross_attention = attend(first_pos, cross_q, shared_all, None, True)
         return (hidden, cross_attention)
 

time: 231 us -> 229 us (level)
  waiting for transfers between devices: 130 us -> 114 us
  local copies, waits for them, and re-layouts: 37.4 us -> 50.8 us
    all_gather x1, waiting for transfers between devices: 75 us -> 62.4 us  [body(): slab = lax.all_gather(packed[None], 'seq', axis=0, tiled=True)]
    dynamic_slice x0 -> x3, local copies, waits for them, and re-layouts: none -> 11.4 us  [the longest x1 6.61 us: body(): lax.dynamic_slice_in_dim(weight_kv, at, feats, 0)]
    unnamed x11 -> x23, local copies, waits for them, and re-layouts: 21.6 us -> 23.5 us
    ppermute x1 -> x2, waiting for transfers between devices: 9.15 us -> 7.62 us  [the longest x1 6.18 us: body(): other = lax.ppermute(hidden, 'heads', [(0, 1), (1, 0)]).astype(jnp.float32)]
    dot_general x2 -> x4, matrix products: 13.6 us -> 13.2 us  [the longest x1 5.12 us: body(): jnp.dot((other * inverse * gains_q[1]).astype(jnp.bfloat16), weight_q[1],...]
  transfers between devices with their start and end apart: 4 -> 5, of which waited for: 4 -> 5; matrix products, arithmetic and copies ran while one was open for 19% -> 25% of each run, Pallas kernels for 2% -> 2%
where the time goes in v10:
time: 229 us; the launch traced here: 228 us
  waiting for transfers between devices  114 us (50%)
  local copies, waits for them, and re-layouts  50.8 us (22%)
  Pallas kernels  29.9 us (13%)
  between operations  14.2 us (6%)
  matrix products  13.2 us (6%)
  starting transfers between devices  3.64 us (2%)
    all_gather x1, waiting for transfers between devices, body(): slab = lax.all_gather(packed[None], 'seq', axis=0, tiled=True)  62.4 us
    all_gather x1, waiting for transfers between devices, body(): lax.all_gather(shared.astype(jnp.bfloat16), 'seq', axis=0, tiled=True)  38.6 us
    unnamed x23, local copies, waits for them, and re-layouts  23.5 us
    pallas_call x2, Pallas kernels, attend(): pl.pallas_call(kernel, out_shape=jax.ShapeDtypeStruct((rows, qcols), jnp....  19.9 us
    pallas_call x2, Pallas kernels, project_half(): pl.pallas_call(functools.partial(_half_kernel, weight_rows=weight_rows),...  9.98 us
    slice x1, local copies, waits for them, and re-layouts, body(): col_layout[:, :, :QPK].reshape(cross_weight.shape[0], groups * QPK * HD)  8.24 us
    dynamic_slice x1, local copies, waits for them, and re-layouts, body(): lax.dynamic_slice_in_dim(weight_kv, at, feats, 0)  6.61 us
    ppermute x1, waiting for transfers between devices, body(): other = lax.ppermute(hidden, 'heads', [(0, 1), (1, 0)]).astype(jnp.float32)  6.18 us
  transfers between devices with their start and end apart: 5, of which 5 were waited for; matrix products, arithmetic and copies ran while one was open for 25% of the time, Pallas kernels for 2%

profile of v10, /device:TPU:0, one launch (start us, length us, event | category | flops | bytes accessed | tf_op | source)
XLA Modules:
  0.0 227.8 jit_solution(2255408577886055669)
XLA Ops:
  7.2 0.0 copy-start
  7.2 0.0 all-gather.6.cloned.1.call-start
  7.2 1.5 reshape.40
  8.8 0.2 copy.13
  8.9 0.0 copy-done
  9.0 1.0 pad_maximum_fusion
  9.9 0.0 all-gather.6.cloned.1.call-update
  10.0 0.0 all-gather.4.cloned.1.call-start
  10.0 20.8 %copy.15 = bf16[3072,2560]{0,1:T(8,128)(2,1)} copy(bf16[3072,2560]{1,0:T(8,128)(2,1)} %param.13) | data formatting | bytes 31457280 | tf_op args[6]
  30.8 8.2 %slice.9 = bf16[3072,4,3,128]{0,3,2,1:T(8,128)(2,1)} slice(bf16[3072,4,5,128]{0,3,2,1:T(8,128)(2,1)} %bitcast.28), slice={[0:3072], [0:4], [0:3], [0:128]} | slice | bytes 18874368 | tf_op jit(solution)/shard_map/slice | solution.py:180
  39.1 5.9 %slice.8 = bf16[3072,4,2,128]{0,3,2,1:T(8,128)(2,1)} slice(bf16[3072,4,5,128]{0,3,2,1:T(8,128)(2,1)} %bitcast.29), slice={[0:3072], [0:4], [3:5], [0:128]} | slice | bytes 12582912 | tf_op jit(solution)/shard_map/slice | solution.py:179
  44.9 0.0 copy-start.2
  44.9 6.6 %constant_dynamic-slice_fusion.2 = (bf16[1536,1024]{0,1:T(8,128)(2,1)}, bf16[1536,1024]{0,1:T(8,128)(2,1)}) fusion(bf16[3072,1024]{0,1:T(8,128)(2,1)} %bitcast.31, s32[]{:T(128)S(6)} %select_n.5, s32[]{:T(128)S(6)} %select_n.4), kind=kLoop, calls=%fused_computation.27 | loop fusion | bytes 12582920 | tf_op jit(solution)/shard_map/dynamic_slice | solution.py:185
  51.5 1.2 copy-done.2
  52.8 4.7 %constant_dynamic-slice_fusion = (bf16[1536,1536]{0,1:T(8,128)(2,1)}, bf16[1536,1536]{0,1:T(8,128)(2,1)}) fusion(bf16[3072,1536]{0,1:T(8,128)(2,1)S(1)} %bitcast.30, s32[]{:T(128)S(6)} %select_n.5, s32[]{:T(128)S(6)} %select_n.4), kind=kLoop, calls=%fused_computation.25 | loop fusion | bytes 18874376 | tf_op jit(solution)/shard_map/dynamic_slice | solution.py:186
  57.5 62.4 %all-gather.6.cloned.1.call-done = bf16[53248,128]{1,0:T(8,128)(2,1)} async-done(((bf16[3328,128]{1,0:T(8,128)(2,1)}), bf16[53248,128]{1,0:T(8,128)(2,1)}) %all-gather.6.cloned.1.call-update) | async-done | bytes 13631504 | tf_op jit(solution)/shard_map/all_gather | solution.py:177
  119.9 9.2 %shard_map.86.att_ref = bf16[128,1536]{1,0:T(8,128)(2,1)} custom-call(s32[1]{0:T(128)} %bitcast.1.pos_ref, bf16[128,1536]{1,0:T(8,128)(2,1)} %q_ref.1, bf16[16,3328,128]{2,1,0:T(8,128)(2,1)} %bitcast.25), custom_call_target="tpu_custom_call" | custom-call | tf_op jit(solution)/shard_map/pallas_call | solution.py:69
  129.1 1.5 collective-permute-start
  130.6 4.9 %shard_map.87.refs_0_ = f32[128,1536]{1,0:T(8,128)} custom-call(s32[1]{0:T(128)} %bitcast.10.sel_ref, bf16[128,1536]{1,0:T(8,128)(2,1)} %shard_map.86.att_ref, bf16[16,3328,128]{2,1,0:T(8,128)(2,1)} %bitcast.26), custom_call_target="tpu_custom_call" | custom-call | tf_op jit(solution)/shard_map/pallas_call | solution.py:126
  135.4 5.2 %collective-permute-done.att_ref = bf16[128,1536]{1,0:T(8,128)(2,1)S(1)} collective-permute-done((bf16[128,1536]{1,0:T(8,128)(2,1)}, bf16[128,1536]{1,0:T(8,128)(2,1)S(1)}, u32[]{:S(2)}, u32[]{:S(2)}) %collective-permute-start) | collective-permute-done | bytes 393248 | tf_op jit(solution)/shard_map/ppermute | solution.py:193
  140.6 0.0 copy-start.8
  140.6 0.7 copy-done.8
  141.3 0.0 copy-start.9
  141.3 0.0 copy-start.10
  141.3 0.0 copy-start.4
  141.3 5.1 %shard_map.88 = bf16[128,1536]{1,0:T(8,128)(2,1)} custom-call(s32[1]{0:T(128)} %bitcast.sel_ref, bf16[128,1536]{1,0:T(8,128)(2,1)} %copy-done.8, bf16[16,3328,128]{2,1,0:T(8,128)(2,1)} %bitcast.27, f32[128,1536]{1,0:T(8,128)} %shard_map.87.refs_0_, bf16[128,1536]{1,0:T(8,128)(2,1)} %refs_1_.1), custom_call_target="tpu_custom_call" | custom-call | tf_op jit(solution)/shard_map/pallas_call | solution.py:126
  146.4 0.0 copy-start.3
  146.5 1.3 fusion.5
  147.8 1.5 collective-permute-start.1
  149.3 0.0 copy-done.9
  149.3 0.0 copy-done.10
  149.3 0.1 fusion.18
  149.4 0.6 collective-permute-start.2
  149.9 1.4 collective-permute-done.1
  151.4 0.0 copy-done.4
  151.4 2.1 fusion.6
  153.6 0.0 copy-start.5
  153.6 6.2 %collective-permute-done.2 = bf16[128,1536]{1,0:T(8,128)(2,1)S(1)} collective-permute-done((bf16[128,1536]{1,0:T(8,128)(2,1)}, bf16[128,1536]{1,0:T(8,128)(2,1)S(1)}, u32[]{:S(2)}, u32[]{:S(2)}) %collective-permute-start.2) | collective-permute-done | bytes 393248 | tf_op jit(solution)/shard_map/ppermute | solution.py:209
  159.7 0.0 copy-start.6
  159.7 0.7 copy-done.6
  160.5 0.0 copy-done.3
  160.5 1.9 fusion
  162.3 0.0 copy-start.7
  162.3 0.0 all-gather.4.cloned.1.call-update
  162.4 0.0 copy-done.5
  162.4 4.0 %fusion.8 = f32[128,1536]{1,0:T(8,128)S(1)} fusion(bf16[1536,1536]{0,1:T(8,128)(2,1)} %get-tuple-element.8, bf16[128,1536]{1,0:T(8,128)(2,1)S(1)} %copy-done.5, f32[1536]{0:T(1024)S(1)} %get-tuple-element.20, f32[128]{0:T(128)S(1)} %rsqrt_bitcast_fusion), kind=kOutput, calls=%fused_computation.15 | convolution fusion | flops 604766208 | bytes 5904896 | tf_op jit(solution)/shard_map/dot_general | solution.py:220
  166.4 0.0 copy-start.1
  166.4 0.0 copy-done.7
  166.4 5.1 %convolution_add_fusion.q_ref = f32[128,1536]{1,0:T(8,128)} fusion(f32[128,1536]{1,0:T(8,128)S(1)} %fusion.8, bf16[1536,1536]{0,1:T(8,128)(2,1)} %get-tuple-element.9, bf16[128,1536]{1,0:T(8,128)(2,1)S(1)} %copy-done.7, f32[1536]{0:T(1024)S(1)} %get-tuple-element.21, f32[128]{0:T(128)S(1)} %rsqrt_bitcast_fusion), kind=kOutput, calls=%fused_computation | convolution fusion | flops 604962816 | bytes 6691328 | tf_op jit(solution)/shard_map/dot_general | solution.py:223
  171.6 38.6 %all-gather.4.cloned.1.call-done.kv_ref = bf16[2048,1024]{1,0:T(8,128)(2,1)} async-done(((bf16[128,1024]{1,0:T(8,128)(2,1)}), bf16[2048,1024]{1,0:T(8,128)(2,1)}) %all-gather.4.cloned.1.call-update) | async-done | bytes 4194320 | tf_op jit(solution)/shard_map/all_gather | solution.py:219
  210.2 10.8 %shard_map.89 = bf16[128,1536]{1,0:T(8,128)(2,1)} custom-call(s32[1]{0:T(128)} %bitcast.1.pos_ref, f32[128,1536]{1,0:T(8,128)} %convolution_add_fusion.q_ref, bf16[2048,1024]{1,0:T(8,128)(2,1)} %all-gather.4.cloned.1.call-done.kv_ref), custom_call_target="tpu_custom_call" | custom-call | tf_op jit(solution)/shard_map/pallas_call | solution.py:69
  220.9 0.0 copy-done.1
  (2 shorter events, 0.1 us)
Async XLA Ops:
  7.2 1.8 copy-start
  7.2 112.7 %all-gather.6.cloned.1.call-start = ((), (), s32[]{:S(2)}) async-start(), calls=%async_computation.1 | async-start | bytes 14483456 | tf_op jit(solution)/shard_map/all_gather | solution.py:177
  10.0 200.2 %all-gather.4.cloned.1.call-start = ((), (), s32[]{:S(2)}) async-start(), calls=%async_computation | async-start | bytes 4456448 | tf_op jit(solution)/shard_map/all_gather | solution.py:219
  44.9 7.8 %copy-start.2 = (bf16[3072,4,3,128]{0,3,2,1:T(8,128)(2,1)S(1)}, bf16[3072,4,3,128]{0,3,2,1:T(8,128)(2,1)}, u32[]{:S(2)}) copy-start(bf16[3072,4,3,128]{0,3,2,1:T(8,128)(2,1)} %slice.9) | copy-start | bytes 28311556
  129.1 11.5 %collective-permute-start = (bf16[128,1536]{1,0:T(8,128)(2,1)}, bf16[128,1536]{1,0:T(8,128)(2,1)S(1)}, u32[]{:S(2)}, u32[]{:S(2)}) collective-permute-start(bf16[128,1536]{1,0:T(8,128)(2,1)} %shard_map.86.att_ref), channel_id=1, source_target_pairs={{0,1},{1,0},{2,3},{3,2},{4,5},{5,4},{6,7},{7,6},{8,9},{9,8},{10,11... | collective-permute-start | bytes 1179656 | tf_op jit(solution)/shard_map/ppermute | solution.py:193
  140.6 0.7 copy-start.8
  141.3 8.0 %copy-start.9 = (f32[3072]{0:T(1024)S(1)}, f32[3072]{0:T(1024)}, u32[]{:S(2)}) copy-start(f32[3072]{0:T(1024)} %param.12) | copy-start | bytes 36868
  141.3 8.0 %copy-start.10 = (f32[3072]{0:T(1024)S(1)}, f32[3072]{0:T(1024)}, u32[]{:S(2)}) copy-start(f32[3072]{0:T(1024)} %param.11) | copy-start | bytes 36868
  141.3 10.1 %copy-start.4 = (bf16[1536,1024]{0,1:T(8,128)(2,1)S(1)}, bf16[1536,1024]{0,1:T(8,128)(2,1)}, u32[]{:S(2)}) copy-start(bf16[1536,1024]{0,1:T(8,128)(2,1)} %get-tuple-element.10) | copy-start | bytes 9437188
  146.4 14.0 %copy-start.3 = (bf16[1536,1024]{0,1:T(8,128)(2,1)S(1)}, bf16[1536,1024]{0,1:T(8,128)(2,1)}, u32[]{:S(2)}) copy-start(bf16[1536,1024]{0,1:T(8,128)(2,1)} %get-tuple-element.11) | copy-start | bytes 9437188
  147.8 3.6 %collective-permute-start.1 = (f32[128,1]{0,1:T(1,128)S(1)}, f32[128,1]{0,1:T(1,128)S(1)}, u32[]{:S(2)}, u32[]{:S(2)}) collective-permute-start(f32[128,1]{0,1:T(1,128)S(1)} %bitcast.35), channel_id=1, source_target_pairs={{0,1},{1,0},{2,3},{3,2},{4,5},{5,4},{6,7},{7,6},{8,9},{9,8},{10,11... | collective-permute-start | bytes 1544 | tf_op jit(solution)/shard_map/ppermute | solution.py:208
  149.4 10.4 %collective-permute-start.2 = (bf16[128,1536]{1,0:T(8,128)(2,1)}, bf16[128,1536]{1,0:T(8,128)(2,1)S(1)}, u32[]{:S(2)}, u32[]{:S(2)}) collective-permute-start(bf16[128,1536]{1,0:T(8,128)(2,1)} %shard_map.88), channel_id=1, source_target_pairs={{0,1},{1,0},{2,3},{3,2},{4,5},{5,4},{6,7},{7,6},{8,9},{9,8},{10,11... | collective-permute-start | bytes 1179656 | tf_op jit(solution)/shard_map/ppermute | solution.py:209
  153.6 8.8 %copy-start.5 = (bf16[128,1536]{1,0:T(8,128)(2,1)S(1)}, bf16[128,1536]{1,0:T(8,128)(2,1)}, u32[]{:S(2)}) copy-start(bf16[128,1536]{1,0:T(8,128)(2,1)} %shard_map.88) | copy-start | bytes 1179652
  159.7 0.7 copy-start.6
  162.3 4.1 %copy-start.7 = (bf16[128,1536]{1,0:T(8,128)(2,1)S(1)}, bf16[128,1536]{1,0:T(8,128)(2,1)}, u32[]{:S(2)}) copy-start(bf16[128,1536]{1,0:T(8,128)(2,1)} %copy-done.6) | copy-start | bytes 1179652
  166.4 54.5 %copy-start.1 = (bf16[128,1024]{1,0:T(8,128)(2,1)S(1)}, bf16[128,1024]{1,0:T(8,128)(2,1)}, u32[]{:S(2)}) copy-start(bf16[128,1024]{1,0:T(8,128)(2,1)} %param.9) | copy-start | bytes 786436
Sparse Core Ops, SparseCore 0:
  10.3 109.5 all-gather.5
  162.5 47.6 all-gather.3

commit v11 on v10

--- a/solution.py
+++ b/solution.py
@@ -56,24 +56,27 @@
         o_ref[:, head * HD:(head + 1) * HD] = (acc / totals).astype(o_ref.dtype)
 
 
-def attend(first_pos, queries, pairs, window, exact, groups=None, offset=0):
+def attend(first_pos, queries, pairs, window, exact, groups=None, offset=0, first=0, count=None):
     rows, qcols = queries.shape
     if groups is None:
         groups = pairs.shape[1] // (2 * HD)
-        kv_spec = pl.BlockSpec((pairs.shape[0], 2 * HD), lambda g, pos: (0, g))
+        kv_spec = pl.BlockSpec((pairs.shape[0], 2 * HD), lambda g, pos: (0, first + g))
     else:
-        kv_spec = pl.BlockSpec((pairs.shape[0], 2 * rows, HD), lambda g, pos: (0, offset + g, 0))
+        kv_spec = pl.BlockSpec(
+            (pairs.shape[0], 2 * rows, HD), lambda g, pos: (0, offset + first + g, 0)
+        )
     qblock = qcols // groups
+    count = groups - first if count is None else count
     keys = pairs.shape[0] * (rows if pairs.ndim == 3 else 1)
     kernel = functools.partial(_attend_kernel, window=window, exact=exact)
     return pl.pallas_call(
         kernel,
-        out_shape=jax.ShapeDtypeStruct((rows, qcols), jnp.bfloat16),
+        out_shape=jax.ShapeDtypeStruct((rows, count * qblock), jnp.bfloat16),
         grid_spec=pltpu.PrefetchScalarGridSpec(
             num_scalar_prefetch=1,
-            grid=(groups,),
+            grid=(count,),
             in_specs=[
-                pl.BlockSpec((rows, qblock), lambda g, pos: (0, g)),
+                pl.BlockSpec((rows, qblock), lambda g, pos: (0, first + g)),
                 kv_spec,
             ],
             out_specs=pl.BlockSpec((rows, qblock), lambda g, pos: (0, g)),
@@ -187,10 +190,23 @@
             gains_kv = [lax.dynamic_slice_in_dim(gain_keyvalue, at, feats, 0) for at in halves]
             gains_q = [lax.dynamic_slice_in_dim(gain_query, at, feats, 0) for at in halves]
         slab, weight_kv, weight_q = lax.optimization_barrier((slab, weight_kv, weight_q))
-        attended = attend(first_pos, self_queries, slab, WINDOW, False, groups, offset)
+        if heads_count == 2 and groups % 2 == 0:
+            pieces = [
+                attend(first_pos, self_queries, slab, WINDOW, False, groups, offset, at, groups // 2)
+                for at in (0, groups // 2)
+            ]
+            first_other = lax.ppermute(pieces[0], "heads", [(0, 1), (1, 0)])
+            second, first_other = lax.optimization_barrier((pieces[1], first_other))
+            others = [first_other, lax.ppermute(second, "heads", [(0, 1), (1, 0)])]
+            attended = jnp.concatenate(pieces, axis=1)
+        else:
+            attended = attend(first_pos, self_queries, slab, WINDOW, False, groups, offset)
         if heads_count == 2:
             place = lax.axis_index("heads")
-            other = lax.ppermute(attended, "heads", [(0, 1), (1, 0)])
+            if groups % 2 == 0:
+                other = jnp.concatenate(others, axis=1)
+            else:
+                other = lax.ppermute(attended, "heads", [(0, 1), (1, 0)])
             width = residual_in.shape[1]
             own_part = project_half(
                 place.astype(jnp.int32).reshape(1), attended, slab,

time: 229 us -> 229 us (level)
  waiting for transfers between devices: 114 us -> 109 us
  other arithmetic: 2.27 us -> 4.78 us
    ppermute x1 -> x2, waiting for transfers between devices: 5.16 us -> 0.21 us  [the longest x1 0.2 us: body(): first_other = lax.ppermute(pieces[0], 'heads', [(0, 1), (1, 0)])]
    concatenate x0 -> x2, other arithmetic: none -> 2.5 us  [the longest x1 1.73 us: body(): attended = jnp.concatenate(pieces, axis=1)]
    pallas_call x2 -> x3, Pallas kernels: 19.9 us -> 21.9 us  [attend(): pl.pallas_call(kernel, out_shape=jax.ShapeDtypeStruct((rows, count * qblo...]
  transfers between devices with their start and end apart: 5 -> 6, of which waited for: 5 -> 5; matrix products, arithmetic and copies ran while one was open for 25% -> 26% of each run, Pallas kernels for 2% -> 5%
where the time goes in v11:
time: 229 us; the launch traced here: 228 us
  waiting for transfers between devices  109 us (48%)
  local copies, waits for them, and re-layouts  50.1 us (22%)
  Pallas kernels  31.9 us (14%)
  between operations  14.2 us (6%)
  matrix products  13.1 us (6%)
  starting transfers between devices  5.11 us (2%)
  other arithmetic  4.78 us (2%)
    all_gather x1, waiting for transfers between devices, body(): slab = lax.all_gather(packed[None], 'seq', axis=0, tiled=True)  62.4 us
    all_gather x1, waiting for transfers between devices, body(): lax.all_gather(shared.astype(jnp.bfloat16), 'seq', axis=0, tiled=True)  39.2 us
    unnamed x23, local copies, waits for them, and re-layouts  22.8 us
    pallas_call x3, Pallas kernels, attend(): pl.pallas_call(kernel, out_shape=jax.ShapeDtypeStruct((rows, count * qblo...  21.9 us
    pallas_call x2, Pallas kernels, project_half(): pl.pallas_call(functools.partial(_half_kernel, weight_rows=weight_rows),...  9.98 us
    slice x1, local copies, waits for them, and re-layouts, body(): col_layout[:, :, :QPK].reshape(cross_weight.shape[0], groups * QPK * HD)  8.23 us
    dynamic_slice x1, local copies, waits for them, and re-layouts, body(): lax.dynamic_slice_in_dim(weight_kv, at, feats, 0)  6.61 us
    slice x1, local copies, waits for them, and re-layouts, body(): col_layout[:, :, QPK:].reshape(cross_weight.shape[0], groups * 2 * HD)  5.85 us
  transfers between devices with their start and end apart: 6, of which 5 were waited for; matrix products, arithmetic and copies ran while one was open for 26% of the time, Pallas kernels for 5%

profile of v11, /device:TPU:0, one launch (start us, length us, event | category | flops | bytes accessed | tf_op | source)
XLA Modules:
  0.0 227.8 jit_solution(14882377841942237257)
XLA Ops:
  7.2 0.0 copy-start
  7.2 0.0 all-gather.6.cloned.1.call-start
  7.2 1.5 reshape.40
  8.8 0.2 copy.13
  8.9 0.0 copy-done
  9.0 1.0 pad_maximum_fusion
  10.0 0.0 all-gather.6.cloned.1.call-update
  10.0 0.0 all-gather.4.cloned.1.call-start
  10.0 20.8 %copy.15 = bf16[3072,2560]{0,1:T(8,128)(2,1)} copy(bf16[3072,2560]{1,0:T(8,128)(2,1)} %param.13) | data formatting | bytes 31457280 | tf_op args[6]
  30.8 8.2 %slice.9 = bf16[3072,4,3,128]{0,3,2,1:T(8,128)(2,1)} slice(bf16[3072,4,5,128]{0,3,2,1:T(8,128)(2,1)} %bitcast.29), slice={[0:3072], [0:4], [0:3], [0:128]} | slice | bytes 18874368 | tf_op jit(solution)/shard_map/slice | solution.py:183
  39.1 5.9 %slice.8 = bf16[3072,4,2,128]{0,3,2,1:T(8,128)(2,1)} slice(bf16[3072,4,5,128]{0,3,2,1:T(8,128)(2,1)} %bitcast.30), slice={[0:3072], [0:4], [3:5], [0:128]} | slice | bytes 12582912 | tf_op jit(solution)/shard_map/slice | solution.py:182
  44.9 0.0 copy-start.2
  44.9 6.6 %constant_dynamic-slice_fusion.2 = (bf16[1536,1024]{0,1:T(8,128)(2,1)}, bf16[1536,1024]{0,1:T(8,128)(2,1)}) fusion(bf16[3072,1024]{0,1:T(8,128)(2,1)} %bitcast.32, s32[]{:T(128)S(6)} %select_n.5, s32[]{:T(128)S(6)} %select_n.4), kind=kLoop, calls=%fused_computation.29 | loop fusion | bytes 12582920 | tf_op jit(solution)/shard_map/dynamic_slice | solution.py:188
  51.5 1.2 copy-done.2
  52.7 4.8 %constant_dynamic-slice_fusion = (bf16[1536,1536]{0,1:T(8,128)(2,1)}, bf16[1536,1536]{0,1:T(8,128)(2,1)}) fusion(bf16[3072,1536]{0,1:T(8,128)(2,1)S(1)} %bitcast.31, s32[]{:T(128)S(6)} %select_n.5, s32[]{:T(128)S(6)} %select_n.4), kind=kLoop, calls=%fused_computation.27 | loop fusion | bytes 18874376 | tf_op jit(solution)/shard_map/dynamic_slice | solution.py:189
  57.5 62.4 %all-gather.6.cloned.1.call-done = bf16[53248,128]{1,0:T(8,128)(2,1)} async-done(((bf16[3328,128]{1,0:T(8,128)(2,1)}), bf16[53248,128]{1,0:T(8,128)(2,1)}) %all-gather.6.cloned.1.call-update) | async-done | bytes 13631504 | tf_op jit(solution)/shard_map/all_gather | solution.py:180
  119.9 5.6 %shard_map.87 = bf16[128,768]{1,0:T(8,128)(2,1)} custom-call(s32[1]{0:T(128)} %bitcast.1.pos_ref, bf16[128,1536]{1,0:T(8,128)(2,1)} %q_ref.3, bf16[16,3328,128]{2,1,0:T(8,128)(2,1)} %bitcast.25), custom_call_target="tpu_custom_call" | custom-call | tf_op jit(solution)/shard_map/pallas_call | solution.py:72
  125.5 0.0 copy-start.8
  125.5 1.5 collective-permute-start
  127.0 5.6 %shard_map.86 = bf16[128,768]{1,0:T(8,128)(2,1)} custom-call(s32[1]{0:T(128)} %bitcast.1.pos_ref, bf16[128,1536]{1,0:T(8,128)(2,1)} %q_ref.3, bf16[16,3328,128]{2,1,0:T(8,128)(2,1)} %bitcast.26), custom_call_target="tpu_custom_call" | custom-call | tf_op jit(solution)/shard_map/pallas_call | solution.py:72
  132.6 0.2 collective-permute-done
  132.8 1.5 collective-permute-start.1
  134.3 0.0 copy-done.8
  134.3 1.7 pad_maximum_fusion.2.att_ref
  136.0 4.9 %shard_map.88.refs_0_ = f32[128,1536]{1,0:T(8,128)} custom-call(s32[1]{0:T(128)} %bitcast.10.sel_ref, bf16[128,1536]{1,0:T(8,128)(2,1)} %pad_maximum_fusion.2.att_ref, bf16[16,3328,128]{2,1,0:T(8,128)(2,1)} %bitcast.27), custom_call_target="tpu_custom_call" | custom-call | tf_op jit(solution)/shard_map/pallas_call | solution.py:129
  140.8 0.0 collective-permute-done.1
  140.9 0.8 pad_maximum_fusion.1.att_ref
  141.6 0.0 copy-start.9
  141.6 0.0 copy-start.10
  141.6 0.0 copy-start.4
  141.6 5.1 %shard_map.89 = bf16[128,1536]{1,0:T(8,128)(2,1)} custom-call(s32[1]{0:T(128)} %bitcast.sel_ref, bf16[128,1536]{1,0:T(8,128)(2,1)} %pad_maximum_fusion.1.att_ref, bf16[16,3328,128]{2,1,0:T(8,128)(2,1)} %bitcast.28, f32[128,1536]{1,0:T(8,128)} %shard_map.88.refs_0_, bf16[128,1536]{1,0:T(8,128)(2,1)} %refs_1_.1), custom_call_target="tpu_custom_call" | custom-call | tf_op jit(solution)/shard_map/pallas_call | solution.py:129
  146.8 0.0 copy-start.3
  146.8 1.3 fusion.5
  148.1 0.6 collective-permute-start.2
  148.7 0.0 copy-done.9
  148.7 0.0 copy-done.10
  148.7 0.1 fusion.18
  148.8 1.5 collective-permute-start.3
  150.2 1.4 collective-permute-done.2
  151.7 0.0 copy-done.4
  151.7 2.1 fusion.6
  153.9 0.0 copy-start.5
  153.9 5.4 %collective-permute-done.3 = bf16[128,1536]{1,0:T(8,128)(2,1)S(1)} collective-permute-done((bf16[128,1536]{1,0:T(8,128)(2,1)}, bf16[128,1536]{1,0:T(8,128)(2,1)S(1)}, u32[]{:S(2)}, u32[]{:S(2)}) %collective-permute-start.3) | collective-permute-done | bytes 393248 | tf_op jit(solution)/shard_map/ppermute | solution.py:225
  159.2 0.0 copy-start.6
  159.2 0.7 copy-done.6
  160.0 0.0 copy-done.3
  160.0 1.9 fusion
  161.8 0.0 copy-start.7
  161.8 0.0 all-gather.4.cloned.1.call-update
  161.9 0.0 copy-done.5
  161.9 4.0 %fusion.8 = f32[128,1536]{1,0:T(8,128)S(1)} fusion(bf16[1536,1536]{0,1:T(8,128)(2,1)} %get-tuple-element.12, bf16[128,1536]{1,0:T(8,128)(2,1)S(1)} %copy-done.5, f32[1536]{0:T(1024)S(1)} %get-tuple-element.24, f32[128]{0:T(128)S(1)} %rsqrt_bitcast_fusion), kind=kOutput, calls=%fused_computation.15 | convolution fusion | flops 604766208 | bytes 5904896 | tf_op jit(solution)/shard_map/dot_general | solution.py:236
  165.9 0.0 copy-start.1
  165.9 0.0 copy-done.7
  165.9 5.1 %convolution_add_fusion.q_ref = f32[128,1536]{1,0:T(8,128)} fusion(f32[128,1536]{1,0:T(8,128)S(1)} %fusion.8, bf16[1536,1536]{0,1:T(8,128)(2,1)} %get-tuple-element.13, bf16[128,1536]{1,0:T(8,128)(2,1)S(1)} %copy-done.7, f32[1536]{0:T(1024)S(1)} %get-tuple-element.25, f32[128]{0:T(128)S(1)} %rsqrt_bitcast_fusion), kind=kOutput, calls=%fused_computation | convolution fusion | flops 604962816 | bytes 6691328 | tf_op jit(solution)/shard_map/dot_general | solution.py:239
  171.0 39.2 %all-gather.4.cloned.1.call-done.kv_ref = bf16[2048,1024]{1,0:T(8,128)(2,1)} async-done(((bf16[128,1024]{1,0:T(8,128)(2,1)}), bf16[2048,1024]{1,0:T(8,128)(2,1)}) %all-gather.4.cloned.1.call-update) | async-done | bytes 4194320 | tf_op jit(solution)/shard_map/all_gather | solution.py:235
  210.2 10.8 %shard_map.90 = bf16[128,1536]{1,0:T(8,128)(2,1)} custom-call(s32[1]{0:T(128)} %bitcast.1.pos_ref, f32[128,1536]{1,0:T(8,128)} %convolution_add_fusion.q_ref, bf16[2048,1024]{1,0:T(8,128)(2,1)} %all-gather.4.cloned.1.call-done.kv_ref), custom_call_target="tpu_custom_call" | custom-call | tf_op jit(solution)/shard_map/pallas_call | solution.py:72
  220.9 0.0 copy-done.1
  (2 shorter events, 0.1 us)
Async XLA Ops:
  7.2 1.8 copy-start
  7.2 112.7 %all-gather.6.cloned.1.call-start = ((), (), s32[]{:S(2)}) async-start(), calls=%async_computation.1 | async-start | bytes 14483456 | tf_op jit(solution)/shard_map/all_gather | solution.py:180
  10.0 200.2 %all-gather.4.cloned.1.call-start = ((), (), s32[]{:S(2)}) async-start(), calls=%async_computation | async-start | bytes 4456448 | tf_op jit(solution)/shard_map/all_gather | solution.py:235
  44.9 7.8 %copy-start.2 = (bf16[3072,4,3,128]{0,3,2,1:T(8,128)(2,1)S(1)}, bf16[3072,4,3,128]{0,3,2,1:T(8,128)(2,1)}, u32[]{:S(2)}) copy-start(bf16[3072,4,3,128]{0,3,2,1:T(8,128)(2,1)} %slice.9) | copy-start | bytes 28311556
  125.5 8.7 %copy-start.8 = (bf16[128,768]{1,0:T(8,128)(2,1)S(1)}, bf16[128,768]{1,0:T(8,128)(2,1)}, u32[]{:S(2)}) copy-start(bf16[128,768]{1,0:T(8,128)(2,1)} %shard_map.87) | copy-start | bytes 589828
  125.5 7.3 %collective-permute-start = (bf16[128,768]{1,0:T(8,128)(2,1)}, bf16[128,768]{1,0:T(8,128)(2,1)S(1)}, u32[]{:S(2)}, u32[]{:S(2)}) collective-permute-start(bf16[128,768]{1,0:T(8,128)(2,1)} %shard_map.87), channel_id=1, source_target_pairs={{0,1},{1,0},{2,3},{3,2},{4,5},{5,4},{6,7},{7,6},{8,9},{9,8},{10,11... | collective-permute-start | bytes 589832 | tf_op jit(solution)/shard_map/ppermute | solution.py:198
  132.8 8.1 %collective-permute-start.1 = (bf16[128,768]{1,0:T(8,128)(2,1)}, bf16[128,768]{1,0:T(8,128)(2,1)S(1)}, u32[]{:S(2)}, u32[]{:S(2)}) collective-permute-start(bf16[128,768]{1,0:T(8,128)(2,1)} %shard_map.86), channel_id=1, source_target_pairs={{0,1},{1,0},{2,3},{3,2},{4,5},{5,4},{6,7},{7,6},{8,9},{9,8},{10,11... | collective-permute-start | bytes 589832 | tf_op jit(solution)/shard_map/ppermute | solution.py:200
  141.6 7.0 %copy-start.9 = (f32[3072]{0:T(1024)S(1)}, f32[3072]{0:T(1024)}, u32[]{:S(2)}) copy-start(f32[3072]{0:T(1024)} %param.12) | copy-start | bytes 36868
  141.6 7.0 %copy-start.10 = (f32[3072]{0:T(1024)S(1)}, f32[3072]{0:T(1024)}, u32[]{:S(2)}) copy-start(f32[3072]{0:T(1024)} %param.11) | copy-start | bytes 36868
  141.6 10.1 %copy-start.4 = (bf16[1536,1024]{0,1:T(8,128)(2,1)S(1)}, bf16[1536,1024]{0,1:T(8,128)(2,1)}, u32[]{:S(2)}) copy-start(bf16[1536,1024]{0,1:T(8,128)(2,1)} %get-tuple-element.14) | copy-start | bytes 9437188
  146.8 13.2 %copy-start.3 = (bf16[1536,1024]{0,1:T(8,128)(2,1)S(1)}, bf16[1536,1024]{0,1:T(8,128)(2,1)}, u32[]{:S(2)}) copy-start(bf16[1536,1024]{0,1:T(8,128)(2,1)} %get-tuple-element.15) | copy-start | bytes 9437188
  148.1 3.6 %collective-permute-start.2 = (f32[128,1]{0,1:T(1,128)S(1)}, f32[128,1]{0,1:T(1,128)S(1)}, u32[]{:S(2)}, u32[]{:S(2)}) collective-permute-start(f32[128,1]{0,1:T(1,128)S(1)} %bitcast.36), channel_id=1, source_target_pairs={{0,1},{1,0},{2,3},{3,2},{4,5},{5,4},{6,7},{7,6},{8,9},{9,8},{10,11... | collective-permute-start | bytes 1544 | tf_op jit(solution)/shard_map/ppermute | solution.py:224
  148.8 10.5 %collective-permute-start.3 = (bf16[128,1536]{1,0:T(8,128)(2,1)}, bf16[128,1536]{1,0:T(8,128)(2,1)S(1)}, u32[]{:S(2)}, u32[]{:S(2)}) collective-permute-start(bf16[128,1536]{1,0:T(8,128)(2,1)} %shard_map.89), channel_id=1, source_target_pairs={{0,1},{1,0},{2,3},{3,2},{4,5},{5,4},{6,7},{7,6},{8,9},{9,8},{10,11... | collective-permute-start | bytes 1179656 | tf_op jit(solution)/shard_map/ppermute | solution.py:225
  153.9 8.0 %copy-start.5 = (bf16[128,1536]{1,0:T(8,128)(2,1)S(1)}, bf16[128,1536]{1,0:T(8,128)(2,1)}, u32[]{:S(2)}) copy-start(bf16[128,1536]{1,0:T(8,128)(2,1)} %shard_map.89) | copy-start | bytes 1179652
  159.2 0.7 copy-start.6
  161.8 4.1 %copy-start.7 = (bf16[128,1536]{1,0:T(8,128)(2,1)S(1)}, bf16[128,1536]{1,0:T(8,128)(2,1)}, u32[]{:S(2)}) copy-start(bf16[128,1536]{1,0:T(8,128)(2,1)} %copy-done.6) | copy-start | bytes 1179652
  165.9 55.0 %copy-start.1 = (bf16[128,1024]{1,0:T(8,128)(2,1)S(1)}, bf16[128,1024]{1,0:T(8,128)(2,1)}, u32[]{:S(2)}) copy-start(bf16[128,1024]{1,0:T(8,128)(2,1)} %param.9) | copy-start | bytes 786436
Sparse Core Ops, SparseCore 0:
  10.3 109.5 all-gather.5
  162.0 48.1 all-gather.3

commit v12 on v11

--- a/solution.py
+++ b/solution.py
@@ -110,36 +110,48 @@
     )(attended, slab, residual)
 
 
-def _half_kernel(sel_ref, att_ref, w_ref, *refs, weight_rows):
+def _half_kernel(sel_ref, *refs, weight_rows, pieces):
+    att_refs = refs[:pieces]
+    w_refs = refs[pieces:2 * pieces]
+    base_refs = refs[2 * pieces:-1]
     o_ref = refs[-1]
     for part in range(o_ref.shape[1] // HD):
-        weight = w_ref[:, part * weight_rows:(part + 1) * weight_rows, :].reshape(-1, HD)
-        acc = jnp.dot(att_ref[...], weight, preferred_element_type=jnp.float32)
+        span = slice(part * weight_rows, (part + 1) * weight_rows)
+        acc = 0.0
+        for att_ref, w_ref in zip(att_refs, w_refs):
+            weight = w_ref[:, span, :].reshape(-1, HD)
+            acc = acc + jnp.dot(att_ref[...], weight, preferred_element_type=jnp.float32)
         cols = slice(part * HD, (part + 1) * HD)
-        for base_ref in refs[:-1]:
+        for base_ref in base_refs:
             acc = acc + base_ref[:, cols].astype(jnp.float32)
         o_ref[:, cols] = acc.astype(o_ref.dtype)
 
 
 def project_half(which, attended, slab, bases, weight_rows, out_dtype, width):
-    rows = attended.shape[0]
+    rows = attended[0].shape[0]
     blocks = width // HD
     per_step = next(n for n in (4, 3, 2, 1) if blocks % n == 0)
-    devices = attended.shape[1] // weight_rows
+    devices = attended[0].shape[1] // weight_rows
+    count = len(attended)
+
+    def weight_map(i):
+        return lambda c, sel: (sel[0] * count + i, c, 0)
+
     return pl.pallas_call(
-        functools.partial(_half_kernel, weight_rows=weight_rows),
+        functools.partial(_half_kernel, weight_rows=weight_rows, pieces=count),
         out_shape=jax.ShapeDtypeStruct((rows, width), out_dtype),
         grid_spec=pltpu.PrefetchScalarGridSpec(
             num_scalar_prefetch=1,
             grid=(blocks // per_step,),
-            in_specs=[
-                pl.BlockSpec(attended.shape, lambda c, sel: (0, 0)),
-                pl.BlockSpec((devices, per_step * weight_rows, HD), lambda c, sel: (sel[0], c, 0)),
+            in_specs=[pl.BlockSpec(p.shape, lambda c, sel: (0, 0)) for p in attended]
+            + [
+                pl.BlockSpec((devices, per_step * weight_rows, HD), weight_map(i))
+                for i in range(count)
             ]
             + [pl.BlockSpec((rows, per_step * HD), lambda c, sel: (0, c)) for _ in bases],
             out_specs=pl.BlockSpec((rows, per_step * HD), lambda c, sel: (0, c)),
         ),
-    )(which, attended, slab, *bases)
+    )(which, *attended, *([slab] * count), *bases)
 
 
 def to_slab(x):
@@ -198,22 +210,20 @@
             first_other = lax.ppermute(pieces[0], "heads", [(0, 1), (1, 0)])
             second, first_other = lax.optimization_barrier((pieces[1], first_other))
             others = [first_other, lax.ppermute(second, "heads", [(0, 1), (1, 0)])]
-            attended = jnp.concatenate(pieces, axis=1)
         else:
             attended = attend(first_pos, self_queries, slab, WINDOW, False, groups, offset)
+            pieces = [attended]
         if heads_count == 2:
             place = lax.axis_index("heads")
-            if groups % 2 == 0:
-                other = jnp.concatenate(others, axis=1)
-            else:
-                other = lax.ppermute(attended, "heads", [(0, 1), (1, 0)])
+            if groups % 2 != 0:
+                others = [lax.ppermute(attended, "heads", [(0, 1), (1, 0)])]
             width = residual_in.shape[1]
             own_part = project_half(
-                place.astype(jnp.int32).reshape(1), attended, slab,
+                place.astype(jnp.int32).reshape(1), pieces, slab,
                 [], weight_rows, jnp.float32, width,
             )
             hidden = project_half(
-                (1 - place).astype(jnp.int32).reshape(1), other, slab,
+                (1 - place).astype(jnp.int32).reshape(1), others, slab,
                 [own_part, residual_in], weight_rows, jnp.bfloat16, width,
             )
         else:

time: 229 us -> 227 us (level)
  other arithmetic: 4.78 us -> 2.28 us
    concatenate x2 -> x0, other arithmetic: 2.5 us -> none  [the longest x1 1.73 us: body(): attended = jnp.concatenate(pieces, axis=1)]
    unnamed x23 -> x25, local copies, waits for them, and re-layouts: 22.8 us -> 23.5 us
  transfers between devices with their start and end apart: 6 -> 6, of which waited for: 5 -> 6; matrix products, arithmetic and copies ran while one was open for 26% -> 25% of each run, Pallas kernels for 5% -> 5%
where the time goes in v12:
time: 227 us; the launch traced here: 226 us
  waiting for transfers between devices  109 us (48%)
  local copies, waits for them, and re-layouts  50.8 us (22%)
  Pallas kernels  31.8 us (14%)
  between operations  14.1 us (6%)
  matrix products  13.2 us (6%)
  starting transfers between devices  5.11 us (2%)
  other arithmetic  2.28 us (1%)
    all_gather x1, waiting for transfers between devices, body(): slab = lax.all_gather(packed[None], 'seq', axis=0, tiled=True)  62.4 us
    all_gather x1, waiting for transfers between devices, body(): lax.all_gather(shared.astype(jnp.bfloat16), 'seq', axis=0, tiled=True)  39.5 us
    unnamed x25, local copies, waits for them, and re-layouts  23.5 us
    pallas_call x3, Pallas kernels, attend(): pl.pallas_call(kernel, out_shape=jax.ShapeDtypeStruct((rows, count * qblo...  22 us
    pallas_call x2, Pallas kernels, project_half(): pl.pallas_call(functools.partial(_half_kernel, weight_rows=weight_rows, p...  9.89 us
    slice x1, local copies, waits for them, and re-layouts, body(): col_layout[:, :, :QPK].reshape(cross_weight.shape[0], groups * QPK * HD)  8.23 us
    dynamic_slice x1, local copies, waits for them, and re-layouts, body(): lax.dynamic_slice_in_dim(weight_kv, at, feats, 0)  6.6 us
    slice x1, local copies, waits for them, and re-layouts, body(): col_layout[:, :, QPK:].reshape(cross_weight.shape[0], groups * 2 * HD)  5.87 us
  transfers between devices with their start and end apart: 6, of which 6 were waited for; matrix products, arithmetic and copies ran while one was open for 25% of the time, Pallas kernels for 5%

profile of v12, /device:TPU:0, one launch (start us, length us, event | category | flops | bytes accessed | tf_op | source)
XLA Modules:
  0.0 226.3 jit_solution(5376870881184258206)
XLA Ops:
  7.2 0.0 copy-start
  7.2 0.0 all-gather.6.cloned.1.call-start
  7.2 1.5 reshape.40
  8.8 0.2 copy.13
  8.9 0.0 copy-done
  9.0 1.0 pad_maximum_fusion
  10.0 0.0 all-gather.6.cloned.1.call-update
  10.0 0.0 all-gather.4.cloned.1.call-start
  10.0 20.8 %copy.15 = bf16[3072,2560]{0,1:T(8,128)(2,1)} copy(bf16[3072,2560]{1,0:T(8,128)(2,1)} %param.13) | data formatting | bytes 31457280 | tf_op args[6]
  30.9 8.2 %slice.9 = bf16[3072,4,3,128]{0,3,2,1:T(8,128)(2,1)} slice(bf16[3072,4,5,128]{0,3,2,1:T(8,128)(2,1)} %bitcast.31), slice={[0:3072], [0:4], [0:3], [0:128]} | slice | bytes 18874368 | tf_op jit(solution)/shard_map/slice | solution.py:195
  39.1 5.9 %slice.8 = bf16[3072,4,2,128]{0,3,2,1:T(8,128)(2,1)} slice(bf16[3072,4,5,128]{0,3,2,1:T(8,128)(2,1)} %bitcast.32), slice={[0:3072], [0:4], [3:5], [0:128]} | slice | bytes 12582912 | tf_op jit(solution)/shard_map/slice | solution.py:194
  44.9 0.0 copy-start.2
  45.0 6.6 %constant_dynamic-slice_fusion.2 = (bf16[1536,1024]{0,1:T(8,128)(2,1)}, bf16[1536,1024]{0,1:T(8,128)(2,1)}) fusion(bf16[3072,1024]{0,1:T(8,128)(2,1)} %bitcast.34, s32[]{:T(128)S(6)} %select_n.5, s32[]{:T(128)S(6)} %select_n.4), kind=kLoop, calls=%fused_computation.27 | loop fusion | bytes 12582920 | tf_op jit(solution)/shard_map/dynamic_slice | solution.py:200
  51.6 1.2 copy-done.2
  52.8 4.8 %constant_dynamic-slice_fusion = (bf16[1536,1536]{0,1:T(8,128)(2,1)}, bf16[1536,1536]{0,1:T(8,128)(2,1)}) fusion(bf16[3072,1536]{0,1:T(8,128)(2,1)S(1)} %bitcast.33, s32[]{:T(128)S(6)} %select_n.5, s32[]{:T(128)S(6)} %select_n.4), kind=kLoop, calls=%fused_computation.25 | loop fusion | bytes 18874376 | tf_op jit(solution)/shard_map/dynamic_slice | solution.py:201
  57.5 62.4 %all-gather.6.cloned.1.call-done = bf16[53248,128]{1,0:T(8,128)(2,1)} async-done(((bf16[3328,128]{1,0:T(8,128)(2,1)}), bf16[53248,128]{1,0:T(8,128)(2,1)}) %all-gather.6.cloned.1.call-update) | async-done | bytes 13631504 | tf_op jit(solution)/shard_map/all_gather | solution.py:192
  119.9 5.6 %shard_map.87.refs_0_ = bf16[128,768]{1,0:T(8,128)(2,1)} custom-call(s32[1]{0:T(128)} %bitcast.1.pos_ref, bf16[128,1536]{1,0:T(8,128)(2,1)} %q_ref.3, bf16[16,3328,128]{2,1,0:T(8,128)(2,1)} %bitcast.25), custom_call_target="tpu_custom_call" | custom-call | tf_op jit(solution)/shard_map/pallas_call | solution.py:72
  125.5 1.5 collective-permute-start
  127.0 5.6 %shard_map.86.refs_1_ = bf16[128,768]{1,0:T(8,128)(2,1)} custom-call(s32[1]{0:T(128)} %bitcast.1.pos_ref, bf16[128,1536]{1,0:T(8,128)(2,1)} %q_ref.3, bf16[16,3328,128]{2,1,0:T(8,128)(2,1)} %bitcast.26), custom_call_target="tpu_custom_call" | custom-call | tf_op jit(solution)/shard_map/pallas_call | solution.py:72
  132.6 0.2 collective-permute-done.refs_0_
  132.8 0.0 copy-start.8
  132.8 1.5 collective-permute-start.1
  134.3 4.8 %shard_map.88.refs_4_ = f32[128,1536]{1,0:T(8,128)} custom-call(s32[1]{0:T(128)} %bitcast.10.sel_ref, bf16[128,768]{1,0:T(8,128)(2,1)} %shard_map.87.refs_0_, bf16[128,768]{1,0:T(8,128)(2,1)} %shard_map.86.refs_1_, bf16[16,3328,128]{2,1,0:T(8,128)(2,1)} %bitcast.27, bf16[16,3328,128]{2,1,0:T(8,128)(2,1)} %bitcast.28), custom_call_target="tpu_custom_call" | custom-call | tf_op jit(solution)/shard_map/pallas_call | solution.py:140
  139.1 0.0 copy-done.8
  139.1 0.6 collective-permute-done.1.refs_1_
  139.6 0.0 copy-start.9
  139.7 0.7 copy-done.9
  140.3 0.0 copy-start.10
  140.3 0.0 copy-start.11
  140.3 0.0 copy-start.4
  140.3 5.1 %shard_map.89 = bf16[128,1536]{1,0:T(8,128)(2,1)} custom-call(s32[1]{0:T(128)} %bitcast.sel_ref, bf16[128,768]{1,0:T(8,128)(2,1)} %copy-done.8, bf16[128,768]{1,0:T(8,128)(2,1)} %copy-done.9, bf16[16,3328,128]{2,1,0:T(8,128)(2,1)} %bitcast.29, bf16[16,3328,128]{2,1,0:T(8,128)(2,1)} %bitcast.30, f32[128,1536]{1,0:T(8,128)} %shard_map.88.refs_4_, ...), custom_call_target="tpu_custom_call" | custom-call | tf_op jit(solution)/shard_map/pallas_call | solution.py:140
  145.4 0.0 copy-start.3
  145.4 1.3 fusion.5
  146.7 1.1 collective-permute-start.2
  147.8 0.0 copy-done.10
  147.8 0.0 copy-done.11
  147.8 0.1 fusion.18
  147.9 1.0 collective-permute-start.3
  148.9 1.4 collective-permute-done.2
  150.4 0.0 copy-done.4
  150.4 2.1 fusion.6
  152.5 0.0 copy-start.5
  152.5 4.9 %collective-permute-done.3 = bf16[128,1536]{1,0:T(8,128)(2,1)S(1)} collective-permute-done((bf16[128,1536]{1,0:T(8,128)(2,1)}, bf16[128,1536]{1,0:T(8,128)(2,1)S(1)}, u32[]{:S(2)}, u32[]{:S(2)}) %collective-permute-start.3) | collective-permute-done | bytes 393248 | tf_op jit(solution)/shard_map/ppermute | solution.py:235
  157.4 0.0 copy-start.6
  157.4 0.7 copy-done.6
  158.2 0.0 copy-done.3
  158.2 1.9 fusion
  160.0 0.0 copy-start.7
  160.0 0.0 all-gather.4.cloned.1.call-update
  160.1 0.0 copy-done.5
  160.1 4.0 %fusion.8 = f32[128,1536]{1,0:T(8,128)S(1)} fusion(bf16[1536,1536]{0,1:T(8,128)(2,1)} %get-tuple-element.12, bf16[128,1536]{1,0:T(8,128)(2,1)S(1)} %copy-done.5, f32[1536]{0:T(1024)S(1)} %get-tuple-element.24, f32[128]{0:T(128)S(1)} %rsqrt_bitcast_fusion), kind=kOutput, calls=%fused_computation.15 | convolution fusion | flops 604766208 | bytes 5904896 | tf_op jit(solution)/shard_map/dot_general | solution.py:246
  164.1 0.0 copy-start.1
  164.1 0.0 copy-done.7
  164.1 5.1 %convolution_add_fusion.q_ref = f32[128,1536]{1,0:T(8,128)} fusion(f32[128,1536]{1,0:T(8,128)S(1)} %fusion.8, bf16[1536,1536]{0,1:T(8,128)(2,1)} %get-tuple-element.13, bf16[128,1536]{1,0:T(8,128)(2,1)S(1)} %copy-done.7, f32[1536]{0:T(1024)S(1)} %get-tuple-element.25, f32[128]{0:T(128)S(1)} %rsqrt_bitcast_fusion), kind=kOutput, calls=%fused_computation | convolution fusion | flops 604962816 | bytes 6691328 | tf_op jit(solution)/shard_map/dot_general | solution.py:249
  169.2 39.5 %all-gather.4.cloned.1.call-done.kv_ref = bf16[2048,1024]{1,0:T(8,128)(2,1)} async-done(((bf16[128,1024]{1,0:T(8,128)(2,1)}), bf16[2048,1024]{1,0:T(8,128)(2,1)}) %all-gather.4.cloned.1.call-update) | async-done | bytes 4194320 | tf_op jit(solution)/shard_map/all_gather | solution.py:245
  208.7 10.8 %shard_map.90 = bf16[128,1536]{1,0:T(8,128)(2,1)} custom-call(s32[1]{0:T(128)} %bitcast.1.pos_ref, f32[128,1536]{1,0:T(8,128)} %convolution_add_fusion.q_ref, bf16[2048,1024]{1,0:T(8,128)(2,1)} %all-gather.4.cloned.1.call-done.kv_ref), custom_call_target="tpu_custom_call" | custom-call | tf_op jit(solution)/shard_map/pallas_call | solution.py:72
  219.5 0.0 copy-done.1
  (2 shorter events, 0.1 us)
Async XLA Ops:
  7.2 1.8 copy-start
  7.2 112.7 %all-gather.6.cloned.1.call-start = ((), (), s32[]{:S(2)}) async-start(), calls=%async_computation.1 | async-start | bytes 14483456 | tf_op jit(solution)/shard_map/all_gather | solution.py:192
  10.0 198.7 %all-gather.4.cloned.1.call-start = ((), (), s32[]{:S(2)}) async-start(), calls=%async_computation | async-start | bytes 4456448 | tf_op jit(solution)/shard_map/all_gather | solution.py:245
  44.9 7.8 %copy-start.2 = (bf16[3072,4,3,128]{0,3,2,1:T(8,128)(2,1)S(1)}, bf16[3072,4,3,128]{0,3,2,1:T(8,128)(2,1)}, u32[]{:S(2)}) copy-start(bf16[3072,4,3,128]{0,3,2,1:T(8,128)(2,1)} %slice.9) | copy-start | bytes 28311556
  125.5 7.3 %collective-permute-start = (bf16[128,768]{1,0:T(8,128)(2,1)}, bf16[128,768]{1,0:T(8,128)(2,1)S(1)}, u32[]{:S(2)}, u32[]{:S(2)}) collective-permute-start(bf16[128,768]{1,0:T(8,128)(2,1)} %shard_map.87.refs_0_), channel_id=1, source_target_pairs={{0,1},{1,0},{2,3},{3,2},{4,5},{5,4},{6,7},{7,6},{8,9},{9,8},{10,11... | collective-permute-start | bytes 589832 | tf_op jit(solution)/shard_map/ppermute | solution.py:210
  132.8 6.3 %copy-start.8 = (bf16[128,768]{1,0:T(8,128)(2,1)}, bf16[128,768]{1,0:T(8,128)(2,1)S(1)}, u32[]{:S(2)}) copy-start(bf16[128,768]{1,0:T(8,128)(2,1)S(1)} %collective-permute-done.refs_0_) | copy-start | bytes 589828
  132.8 6.9 %collective-permute-start.1 = (bf16[128,768]{1,0:T(8,128)(2,1)}, bf16[128,768]{1,0:T(8,128)(2,1)S(1)}, u32[]{:S(2)}, u32[]{:S(2)}) collective-permute-start(bf16[128,768]{1,0:T(8,128)(2,1)} %shard_map.86.refs_1_), channel_id=1, source_target_pairs={{0,1},{1,0},{2,3},{3,2},{4,5},{5,4},{6,7},{7,6},{8,9},{9,8},{10,11... | collective-permute-start | bytes 589832 | tf_op jit(solution)/shard_map/ppermute | solution.py:212
  139.6 0.7 copy-start.9
  140.3 7.5 %copy-start.10 = (f32[3072]{0:T(1024)S(1)}, f32[3072]{0:T(1024)}, u32[]{:S(2)}) copy-start(f32[3072]{0:T(1024)} %param.12) | copy-start | bytes 36868
  140.3 7.5 %copy-start.11 = (f32[3072]{0:T(1024)S(1)}, f32[3072]{0:T(1024)}, u32[]{:S(2)}) copy-start(f32[3072]{0:T(1024)} %param.11) | copy-start | bytes 36868
  140.3 10.0 %copy-start.4 = (bf16[1536,1024]{0,1:T(8,128)(2,1)S(1)}, bf16[1536,1024]{0,1:T(8,128)(2,1)}, u32[]{:S(2)}) copy-start(bf16[1536,1024]{0,1:T(8,128)(2,1)} %get-tuple-element.14) | copy-start | bytes 9437188
  145.4 12.7 %copy-start.3 = (bf16[1536,1024]{0,1:T(8,128)(2,1)S(1)}, bf16[1536,1024]{0,1:T(8,128)(2,1)}, u32[]{:S(2)}) copy-start(bf16[1536,1024]{0,1:T(8,128)(2,1)} %get-tuple-element.15) | copy-start | bytes 9437188
  146.7 3.6 %collective-permute-start.2 = (f32[128,1]{0,1:T(1,128)S(1)}, f32[128,1]{0,1:T(1,128)S(1)}, u32[]{:S(2)}, u32[]{:S(2)}) collective-permute-start(f32[128,1]{0,1:T(1,128)S(1)} %bitcast.38), channel_id=1, source_target_pairs={{0,1},{1,0},{2,3},{3,2},{4,5},{5,4},{6,7},{7,6},{8,9},{9,8},{10,11... | collective-permute-start | bytes 1544 | tf_op jit(solution)/shard_map/ppermute | solution.py:234
  147.9 9.5 %collective-permute-start.3 = (bf16[128,1536]{1,0:T(8,128)(2,1)}, bf16[128,1536]{1,0:T(8,128)(2,1)S(1)}, u32[]{:S(2)}, u32[]{:S(2)}) collective-permute-start(bf16[128,1536]{1,0:T(8,128)(2,1)} %shard_map.89), channel_id=1, source_target_pairs={{0,1},{1,0},{2,3},{3,2},{4,5},{5,4},{6,7},{7,6},{8,9},{9,8},{10,11... | collective-permute-start | bytes 1179656 | tf_op jit(solution)/shard_map/ppermute | solution.py:235
  152.5 7.5 %copy-start.5 = (bf16[128,1536]{1,0:T(8,128)(2,1)S(1)}, bf16[128,1536]{1,0:T(8,128)(2,1)}, u32[]{:S(2)}) copy-start(bf16[128,1536]{1,0:T(8,128)(2,1)} %shard_map.89) | copy-start | bytes 1179652
  157.4 0.7 copy-start.6
  160.0 4.1 %copy-start.7 = (bf16[128,1536]{1,0:T(8,128)(2,1)S(1)}, bf16[128,1536]{1,0:T(8,128)(2,1)}, u32[]{:S(2)}) copy-start(bf16[128,1536]{1,0:T(8,128)(2,1)} %copy-done.6) | copy-start | bytes 1179652
  164.1 55.4 %copy-start.1 = (bf16[128,1024]{1,0:T(8,128)(2,1)S(1)}, bf16[128,1024]{1,0:T(8,128)(2,1)}, u32[]{:S(2)}) copy-start(bf16[128,1024]{1,0:T(8,128)(2,1)} %param.9) | copy-start | bytes 786436
Sparse Core Ops, SparseCore 0:
  10.3 109.5 all-gather.5
  160.2 48.4 all-gather.3

commit v13 on v12

--- a/solution.py
+++ b/solution.py
@@ -19,18 +19,16 @@
     return high, low
 
 
-def _attend_kernel(pos_ref, q_ref, kv_ref, o_ref, bias_ref, *, window, exact):
-    rows, keys = bias_ref.shape
-
-    @pl.when(pl.program_id(0) == 0)
-    def _():
-        query_pos = pos_ref[0] + lax.broadcasted_iota(jnp.int32, (rows, keys), 0)
-        key_pos = lax.broadcasted_iota(jnp.int32, (rows, keys), 1)
-        allowed = key_pos <= query_pos
-        if window is not None:
-            allowed = allowed & (key_pos > query_pos - window)
-        bias_ref[...] = jnp.where(allowed, 0.0, -jnp.inf)
-
+def mask_bias(first_pos, rows, keys, window):
+    query_pos = first_pos[0] + lax.broadcasted_iota(jnp.int32, (rows, keys), 0)
+    key_pos = lax.broadcasted_iota(jnp.int32, (rows, keys), 1)
+    allowed = key_pos <= query_pos
+    if window is not None:
+        allowed = allowed & (key_pos > query_pos - window)
+    return jnp.where(allowed, 0.0, -jnp.inf).astype(jnp.float32)
+
+
+def _attend_kernel(pos_ref, q_ref, kv_ref, bias_ref, o_ref, *, window, exact):
     if len(kv_ref.shape) == 3:
         half = kv_ref.shape[1] // 2
         key = kv_ref[:, :half, :].reshape(-1, HD)
@@ -56,7 +54,8 @@
         o_ref[:, head * HD:(head + 1) * HD] = (acc / totals).astype(o_ref.dtype)
 
 
-def attend(first_pos, queries, pairs, window, exact, groups=None, offset=0, first=0, count=None):
+def attend(first_pos, queries, pairs, bias, exact, groups=None, offset=0, first=0, count=None):
+    window = None
     rows, qcols = queries.shape
     if groups is None:
         groups = pairs.shape[1] // (2 * HD)
@@ -78,11 +77,11 @@
             in_specs=[
                 pl.BlockSpec((rows, qblock), lambda g, pos: (0, first + g)),
                 kv_spec,
+                pl.BlockSpec((rows, keys), lambda g, pos: (0, 0)),
             ],
             out_specs=pl.BlockSpec((rows, qblock), lambda g, pos: (0, g)),
-            scratch_shapes=[pltpu.VMEM((rows, keys), jnp.float32)],
         ),
-    )(first_pos, queries, pairs)
+    )(first_pos, queries, pairs, bias)
 
 
 def _project_kernel(att_ref, w_ref, res_ref, o_ref, *, weight_rows):
@@ -190,6 +189,9 @@
         offset = weight_part.shape[0] // (2 * tok_rows)
         packed = jnp.concatenate([weight_part, to_slab(self_keys_values)], axis=0)
         slab = lax.all_gather(packed[None], "seq", axis=0, tiled=True)
+        keys = slab.shape[0] * tok_rows
+        self_bias = mask_bias(first_pos, tok_rows, keys, WINDOW)
+        cross_bias = mask_bias(first_pos, tok_rows, keys, None)
         col_layout = cross_weight.reshape(cross_weight.shape[0], groups, QPK + 2, HD)
         weight_kv = col_layout[:, :, QPK:].reshape(cross_weight.shape[0], groups * 2 * HD)
         weight_q = col_layout[:, :, :QPK].reshape(cross_weight.shape[0], groups * QPK * HD)
@@ -201,17 +203,19 @@
             weight_q = [lax.dynamic_slice_in_dim(weight_q, at, feats, 0) for at in halves]
             gains_kv = [lax.dynamic_slice_in_dim(gain_keyvalue, at, feats, 0) for at in halves]
             gains_q = [lax.dynamic_slice_in_dim(gain_query, at, feats, 0) for at in halves]
-        slab, weight_kv, weight_q = lax.optimization_barrier((slab, weight_kv, weight_q))
+        slab, weight_kv, weight_q, self_bias, cross_bias = lax.optimization_barrier(
+            (slab, weight_kv, weight_q, self_bias, cross_bias)
+        )
         if heads_count == 2 and groups % 2 == 0:
             pieces = [
-                attend(first_pos, self_queries, slab, WINDOW, False, groups, offset, at, groups // 2)
+                attend(first_pos, self_queries, slab, self_bias, False, groups, offset, at, groups // 2)
                 for at in (0, groups // 2)
             ]
             first_other = lax.ppermute(pieces[0], "heads", [(0, 1), (1, 0)])
             second, first_other = lax.optimization_barrier((pieces[1], first_other))
             others = [first_other, lax.ppermute(second, "heads", [(0, 1), (1, 0)])]
         else:
-            attended = attend(first_pos, self_queries, slab, WINDOW, False, groups, offset)
+            attended = attend(first_pos, self_queries, slab, self_bias, False, groups, offset)
             pieces = [attended]
         if heads_count == 2:
             place = lax.axis_index("heads")
@@ -259,7 +263,7 @@
             shared = jnp.dot(normed_kv, weight_kv, preferred_element_type=jnp.float32)
             shared_all = lax.all_gather(shared.astype(jnp.bfloat16), "seq", axis=0, tiled=True)
             cross_q = jnp.dot(normed_q, weight_q, preferred_element_type=jnp.float32)
-        cross_attention = attend(first_pos, cross_q, shared_all, None, True)
+        cross_attention = attend(first_pos, cross_q, shared_all, cross_bias, True)
         return (hidden, cross_attention)
 
     return body

time: 227 us -> 228 us (level)
  transfers between devices with their start and end apart: 6 -> 6, of which waited for: 6 -> 5; matrix products, arithmetic and copies ran while one was open for 25% -> 26% of each run, Pallas kernels for 5% -> 5%
where the time goes in v13:
time: 228 us; the launch traced here: 227 us
  waiting for transfers between devices  109 us (48%)
  local copies, waits for them, and re-layouts  49.5 us (22%)
  Pallas kernels  32.4 us (14%)
  between operations  14.2 us (6%)
  matrix products  13.1 us (6%)
  starting transfers between devices  5.12 us (2%)
  other arithmetic  4.01 us (2%)
    all_gather x1, waiting for transfers between devices, body(): slab = lax.all_gather(packed[None], 'seq', axis=0, tiled=True)  61.9 us
    all_gather x1, waiting for transfers between devices, body(): lax.all_gather(shared.astype(jnp.bfloat16), 'seq', axis=0, tiled=True)  39.6 us
    pallas_call x3, Pallas kernels, attend(): pl.pallas_call(kernel, out_shape=jax.ShapeDtypeStruct((rows, count * qblo...  22.5 us
    unnamed x25, local copies, waits for them, and re-layouts  22.3 us
    pallas_call x2, Pallas kernels, project_half(): pl.pallas_call(functools.partial(_half_kernel, weight_rows=weight_rows, p...  9.89 us
    slice x1, local copies, waits for them, and re-layouts, body(): col_layout[:, :, :QPK].reshape(cross_weight.shape[0], groups * QPK * HD)  8.22 us
    dynamic_slice x1, local copies, waits for them, and re-layouts, body(): lax.dynamic_slice_in_dim(weight_kv, at, feats, 0)  6.61 us
    slice x1, local copies, waits for them, and re-layouts, body(): col_layout[:, :, QPK:].reshape(cross_weight.shape[0], groups * 2 * HD)  5.86 us
  transfers between devices with their start and end apart: 6, of which 5 were waited for; matrix products, arithmetic and copies ran while one was open for 26% of the time, Pallas kernels for 5%

profile of v13, /device:TPU:0, one launch (start us, length us, event | category | flops | bytes accessed | tf_op | source)
XLA Modules:
  0.0 227.0 jit_solution(11795788300537691249)
XLA Ops:
  7.2 0.0 copy-start
  7.2 0.0 all-gather.6.cloned.1.call-start
  7.2 1.5 reshape.40
  8.8 0.2 copy.13
  8.9 0.0 copy-done
  9.0 1.0 pad_maximum_fusion
  9.9 0.0 all-gather.6.cloned.1.call-update
  10.0 0.0 all-gather.4.cloned.1.call-start
  10.0 20.8 %copy.15 = bf16[3072,2560]{0,1:T(8,128)(2,1)} copy(bf16[3072,2560]{1,0:T(8,128)(2,1)} %param.13) | data formatting | bytes 31457280 | tf_op args[6]
  30.8 8.2 %slice.9 = bf16[3072,4,3,128]{0,3,2,1:T(8,128)(2,1)} slice(bf16[3072,4,5,128]{0,3,2,1:T(8,128)(2,1)} %bitcast.31), slice={[0:3072], [0:4], [0:3], [0:128]} | slice | bytes 18874368 | tf_op jit(solution)/shard_map/slice | solution.py:197
  39.0 5.9 %slice.8 = bf16[3072,4,2,128]{0,3,2,1:T(8,128)(2,1)} slice(bf16[3072,4,5,128]{0,3,2,1:T(8,128)(2,1)} %bitcast.32), slice={[0:3072], [0:4], [3:5], [0:128]} | slice | bytes 12582912 | tf_op jit(solution)/shard_map/slice | solution.py:196
  44.9 0.0 copy-start.2
  44.9 6.6 %constant_dynamic-slice_fusion.2 = (bf16[1536,1024]{0,1:T(8,128)(2,1)}, bf16[1536,1024]{0,1:T(8,128)(2,1)}) fusion(bf16[3072,1024]{0,1:T(8,128)(2,1)} %bitcast.34, s32[]{:T(128)S(6)} %select_n.20, s32[]{:T(128)S(6)} %select_n.19), kind=kLoop, calls=%fused_computation.32 | loop fusion | bytes 12582920 | tf_op jit(solution)/shard_map/dynamic_slice | solution.py:202
  51.5 1.7 fusion.1
  53.3 0.0 copy-done.2
  53.3 4.8 %constant_dynamic-slice_fusion = (bf16[1536,1536]{0,1:T(8,128)(2,1)}, bf16[1536,1536]{0,1:T(8,128)(2,1)}) fusion(bf16[3072,1536]{0,1:T(8,128)(2,1)S(1)} %bitcast.33, s32[]{:T(128)S(6)} %select_n.20, s32[]{:T(128)S(6)} %select_n.19), kind=kLoop, calls=%fused_computation.30 | loop fusion | bytes 18874376 | tf_op jit(solution)/shard_map/dynamic_slice | solution.py:203
  58.0 61.9 %all-gather.6.cloned.1.call-done = bf16[53248,128]{1,0:T(8,128)(2,1)} async-done(((bf16[3328,128]{1,0:T(8,128)(2,1)}), bf16[53248,128]{1,0:T(8,128)(2,1)}) %all-gather.6.cloned.1.call-update) | async-done | bytes 13631504 | tf_op jit(solution)/shard_map/all_gather | solution.py:191
  119.9 5.8 %shard_map.87.refs_0_ = bf16[128,768]{1,0:T(8,128)(2,1)} custom-call(s32[1]{0:T(128)} %bitcast.1.pos_ref, bf16[128,1536]{1,0:T(8,128)(2,1)} %q_ref.3, bf16[16,3328,128]{2,1,0:T(8,128)(2,1)} %bitcast.25, f32[128,2048]{1,0:T(8,128)} %get-tuple-element.12.bias_ref), custom_call_target="tpu_custom_call" | custom-call | tf_op jit(solution)/shard_map/pallas_call | solution.py:71
  125.7 1.5 collective-permute-start
  127.2 5.8 %shard_map.86.refs_1_ = bf16[128,768]{1,0:T(8,128)(2,1)} custom-call(s32[1]{0:T(128)} %bitcast.1.pos_ref, bf16[128,1536]{1,0:T(8,128)(2,1)} %q_ref.3, bf16[16,3328,128]{2,1,0:T(8,128)(2,1)} %bitcast.26, f32[128,2048]{1,0:T(8,128)} %get-tuple-element.12.bias_ref), custom_call_target="tpu_custom_call" | custom-call | tf_op jit(solution)/shard_map/pallas_call | solution.py:71
  132.9 0.0 collective-permute-done.refs_0_
  133.0 0.0 copy-start.8
  133.0 1.5 collective-permute-start.1
  134.4 4.8 %shard_map.88.refs_4_ = f32[128,1536]{1,0:T(8,128)} custom-call(s32[1]{0:T(128)} %bitcast.10.sel_ref, bf16[128,768]{1,0:T(8,128)(2,1)} %shard_map.87.refs_0_, bf16[128,768]{1,0:T(8,128)(2,1)} %shard_map.86.refs_1_, bf16[16,3328,128]{2,1,0:T(8,128)(2,1)} %bitcast.27, bf16[16,3328,128]{2,1,0:T(8,128)(2,1)} %bitcast.28), custom_call_target="tpu_custom_call" | custom-call | tf_op jit(solution)/shard_map/pallas_call | solution.py:139
  139.2 0.0 copy-done.8
  139.2 0.8 collective-permute-done.1.refs_1_
  140.0 0.0 copy-start.9
  140.0 0.7 copy-done.9
  140.7 0.0 copy-start.10
  140.7 0.0 copy-start.11
  140.7 0.0 copy-start.4
  140.7 5.1 %shard_map.89 = bf16[128,1536]{1,0:T(8,128)(2,1)} custom-call(s32[1]{0:T(128)} %bitcast.sel_ref, bf16[128,768]{1,0:T(8,128)(2,1)} %copy-done.8, bf16[128,768]{1,0:T(8,128)(2,1)} %copy-done.9, bf16[16,3328,128]{2,1,0:T(8,128)(2,1)} %bitcast.29, bf16[16,3328,128]{2,1,0:T(8,128)(2,1)} %bitcast.30, f32[128,1536]{1,0:T(8,128)} %shard_map.88.refs_4_, ...), custom_call_target="tpu_custom_call" | custom-call | tf_op jit(solution)/shard_map/pallas_call | solution.py:139
  145.8 0.0 copy-start.3
  145.8 1.3 fusion.8
  147.1 0.9 collective-permute-start.2
  148.0 0.0 copy-done.10
  148.0 0.0 copy-done.11
  148.0 0.1 fusion.21
  148.1 1.2 collective-permute-start.3
  149.3 1.4 collective-permute-done.2
  150.7 0.0 copy-done.4
  150.7 2.1 fusion.9
  152.9 0.0 copy-start.5
  152.9 4.9 %collective-permute-done.3 = bf16[128,1536]{1,0:T(8,128)(2,1)S(1)} collective-permute-done((bf16[128,1536]{1,0:T(8,128)(2,1)}, bf16[128,1536]{1,0:T(8,128)(2,1)S(1)}, u32[]{:S(2)}, u32[]{:S(2)}) %collective-permute-start.3) | collective-permute-done | bytes 393248 | tf_op jit(solution)/shard_map/ppermute | solution.py:239
  157.7 0.0 copy-start.6
  157.7 0.7 copy-done.6
  158.5 0.0 copy-done.3
  158.5 1.9 fusion
  160.4 0.0 copy-start.7
  160.4 0.0 all-gather.4.cloned.1.call-update
  160.4 0.0 copy-done.5
  160.4 4.0 %fusion.11 = f32[128,1536]{1,0:T(8,128)S(1)} fusion(bf16[1536,1536]{0,1:T(8,128)(2,1)} %get-tuple-element.15, bf16[128,1536]{1,0:T(8,128)(2,1)S(1)} %copy-done.5, f32[1536]{0:T(1024)S(1)} %get-tuple-element.32, f32[128]{0:T(128)S(1)} %rsqrt_bitcast_fusion), kind=kOutput, calls=%fused_computation.20 | convolution fusion | flops 604766208 | bytes 5904896 | tf_op jit(solution)/shard_map/dot_general | solution.py:250
  164.4 0.0 copy-done.7
  164.4 0.0 copy-start.1
  164.5 5.1 %convolution_add_fusion.q_ref = f32[128,1536]{1,0:T(8,128)} fusion(f32[128,1536]{1,0:T(8,128)S(1)} %fusion.11, bf16[1536,1536]{0,1:T(8,128)(2,1)} %get-tuple-element.16, bf16[128,1536]{1,0:T(8,128)(2,1)S(1)} %copy-done.7, f32[1536]{0:T(1024)S(1)} %get-tuple-element.33, f32[128]{0:T(128)S(1)} %rsqrt_bitcast_fusion), kind=kOutput, calls=%fused_computation | convolution fusion | flops 604962816 | bytes 6691328 | tf_op jit(solution)/shard_map/dot_general | solution.py:253
  169.6 39.6 %all-gather.4.cloned.1.call-done.kv_ref = bf16[2048,1024]{1,0:T(8,128)(2,1)} async-done(((bf16[128,1024]{1,0:T(8,128)(2,1)}), bf16[2048,1024]{1,0:T(8,128)(2,1)}) %all-gather.4.cloned.1.call-update) | async-done | bytes 4194320 | tf_op jit(solution)/shard_map/all_gather | solution.py:249
  209.2 11.0 %shard_map.90 = bf16[128,1536]{1,0:T(8,128)(2,1)} custom-call(s32[1]{0:T(128)} %bitcast.1.pos_ref, f32[128,1536]{1,0:T(8,128)} %convolution_add_fusion.q_ref, bf16[2048,1024]{1,0:T(8,128)(2,1)} %all-gather.4.cloned.1.call-done.kv_ref, f32[128,2048]{1,0:T(8,128)} %get-tuple-element.19.bias_ref), custom_call_target="tpu_custom_call" | custom-call | tf_op jit(solution)/shard_map/pallas_call | solution.py:71
  220.2 0.0 copy-done.1
  (3 shorter events, 0.1 us)
Async XLA Ops:
  7.2 1.8 copy-start
  7.2 112.7 %all-gather.6.cloned.1.call-start = ((), (), s32[]{:S(2)}) async-start(), calls=%async_computation.1 | async-start | bytes 14483456 | tf_op jit(solution)/shard_map/all_gather | solution.py:191
  10.0 199.2 %all-gather.4.cloned.1.call-start = ((), (), s32[]{:S(2)}) async-start(), calls=%async_computation | async-start | bytes 4456448 | tf_op jit(solution)/shard_map/all_gather | solution.py:249
  44.9 8.4 %copy-start.2 = (bf16[3072,4,3,128]{0,3,2,1:T(8,128)(2,1)S(1)}, bf16[3072,4,3,128]{0,3,2,1:T(8,128)(2,1)}, u32[]{:S(2)}) copy-start(bf16[3072,4,3,128]{0,3,2,1:T(8,128)(2,1)} %slice.9) | copy-start | bytes 28311556
  125.7 7.3 %collective-permute-start = (bf16[128,768]{1,0:T(8,128)(2,1)}, bf16[128,768]{1,0:T(8,128)(2,1)S(1)}, u32[]{:S(2)}, u32[]{:S(2)}) collective-permute-start(bf16[128,768]{1,0:T(8,128)(2,1)} %shard_map.87.refs_0_), channel_id=1, source_target_pairs={{0,1},{1,0},{2,3},{3,2},{4,5},{5,4},{6,7},{7,6},{8,9},{9,8},{10,11... | collective-permute-start | bytes 589832 | tf_op jit(solution)/shard_map/ppermute | solution.py:214
  133.0 6.3 %copy-start.8 = (bf16[128,768]{1,0:T(8,128)(2,1)}, bf16[128,768]{1,0:T(8,128)(2,1)S(1)}, u32[]{:S(2)}) copy-start(bf16[128,768]{1,0:T(8,128)(2,1)S(1)} %collective-permute-done.refs_0_) | copy-start | bytes 589828
  133.0 7.0 %collective-permute-start.1 = (bf16[128,768]{1,0:T(8,128)(2,1)}, bf16[128,768]{1,0:T(8,128)(2,1)S(1)}, u32[]{:S(2)}, u32[]{:S(2)}) collective-permute-start(bf16[128,768]{1,0:T(8,128)(2,1)} %shard_map.86.refs_1_), channel_id=1, source_target_pairs={{0,1},{1,0},{2,3},{3,2},{4,5},{5,4},{6,7},{7,6},{8,9},{9,8},{10,11... | collective-permute-start | bytes 589832 | tf_op jit(solution)/shard_map/ppermute | solution.py:216
  140.0 0.7 copy-start.9
  140.7 7.3 %copy-start.10 = (f32[3072]{0:T(1024)S(1)}, f32[3072]{0:T(1024)}, u32[]{:S(2)}) copy-start(f32[3072]{0:T(1024)} %param.12) | copy-start | bytes 36868
  140.7 7.3 %copy-start.11 = (f32[3072]{0:T(1024)S(1)}, f32[3072]{0:T(1024)}, u32[]{:S(2)}) copy-start(f32[3072]{0:T(1024)} %param.11) | copy-start | bytes 36868
  140.7 10.0 %copy-start.4 = (bf16[1536,1024]{0,1:T(8,128)(2,1)S(1)}, bf16[1536,1024]{0,1:T(8,128)(2,1)}, u32[]{:S(2)}) copy-start(bf16[1536,1024]{0,1:T(8,128)(2,1)} %get-tuple-element.17) | copy-start | bytes 9437188
  145.8 12.7 %copy-start.3 = (bf16[1536,1024]{0,1:T(8,128)(2,1)S(1)}, bf16[1536,1024]{0,1:T(8,128)(2,1)}, u32[]{:S(2)}) copy-start(bf16[1536,1024]{0,1:T(8,128)(2,1)} %get-tuple-element.18) | copy-start | bytes 9437188
  147.1 3.6 %collective-permute-start.2 = (f32[128,1]{0,1:T(1,128)S(1)}, f32[128,1]{0,1:T(1,128)S(1)}, u32[]{:S(2)}, u32[]{:S(2)}) collective-permute-start(f32[128,1]{0,1:T(1,128)S(1)} %bitcast.38), channel_id=1, source_target_pairs={{0,1},{1,0},{2,3},{3,2},{4,5},{5,4},{6,7},{7,6},{8,9},{9,8},{10,11... | collective-permute-start | bytes 1544 | tf_op jit(solution)/shard_map/ppermute | solution.py:238
  148.1 9.7 %collective-permute-start.3 = (bf16[128,1536]{1,0:T(8,128)(2,1)}, bf16[128,1536]{1,0:T(8,128)(2,1)S(1)}, u32[]{:S(2)}, u32[]{:S(2)}) collective-permute-start(bf16[128,1536]{1,0:T(8,128)(2,1)} %shard_map.89), channel_id=1, source_target_pairs={{0,1},{1,0},{2,3},{3,2},{4,5},{5,4},{6,7},{7,6},{8,9},{9,8},{10,11... | collective-permute-start | bytes 1179656 | tf_op jit(solution)/shard_map/ppermute | solution.py:239
  152.9 7.5 %copy-start.5 = (bf16[128,1536]{1,0:T(8,128)(2,1)S(1)}, bf16[128,1536]{1,0:T(8,128)(2,1)}, u32[]{:S(2)}) copy-start(bf16[128,1536]{1,0:T(8,128)(2,1)} %shard_map.89) | copy-start | bytes 1179652
  157.7 0.7 copy-start.6
  160.4 4.1 %copy-start.7 = (bf16[128,1536]{1,0:T(8,128)(2,1)S(1)}, bf16[128,1536]{1,0:T(8,128)(2,1)}, u32[]{:S(2)}) copy-start(bf16[128,1536]{1,0:T(8,128)(2,1)} %copy-done.6) | copy-start | bytes 1179652
  164.4 55.8 %copy-start.1 = (bf16[128,1024]{1,0:T(8,128)(2,1)S(1)}, bf16[128,1024]{1,0:T(8,128)(2,1)}, u32[]{:S(2)}) copy-start(bf16[128,1024]{1,0:T(8,128)(2,1)} %param.9) | copy-start | bytes 786436
Sparse Core Ops, SparseCore 0:
  10.3 109.5 all-gather.5
  160.5 48.6 all-gather.3

commit v14 on v12

--- a/solution.py
+++ b/solution.py
@@ -40,20 +40,23 @@
         value = kv_ref[:, HD:]
     score_scale = 1.0 / math.sqrt(HD)
     contract = (((1,), (1,)), ((), ()))
-    for head in range(q_ref.shape[1] // HD):
-        query = q_ref[:, head * HD:(head + 1) * HD]
-        if exact:
-            q_hi, q_lo = _split(query.astype(jnp.float32))
-            scores = lax.dot_general(q_hi, key, contract, preferred_element_type=jnp.float32)
-            scores = scores + lax.dot_general(q_lo, key, contract, preferred_element_type=jnp.float32)
-        else:
-            scores = lax.dot_general(query, key, contract, preferred_element_type=jnp.float32)
-        masked = scores * score_scale + bias_ref[...]
-        row_top = jnp.max(masked, axis=-1, keepdims=True)
-        weights = jnp.exp(masked - row_top)
-        totals = jnp.sum(weights, axis=-1, keepdims=True)
-        acc = jnp.dot(weights.astype(jnp.bfloat16), value, preferred_element_type=jnp.float32)
-        o_ref[:, head * HD:(head + 1) * HD] = (acc / totals).astype(o_ref.dtype)
+    heads = q_ref.shape[1] // HD
+    query = jnp.concatenate([q_ref[:, h * HD:(h + 1) * HD] for h in range(heads)], axis=0)
+    if exact:
+        q_hi, q_lo = _split(query.astype(jnp.float32))
+        scores = lax.dot_general(q_hi, key, contract, preferred_element_type=jnp.float32)
+        scores = scores + lax.dot_general(q_lo, key, contract, preferred_element_type=jnp.float32)
+    else:
+        scores = lax.dot_general(query, key, contract, preferred_element_type=jnp.float32)
+    masked = (scores * score_scale).reshape(heads, rows, keys) + bias_ref[...][None]
+    masked = masked.reshape(heads * rows, keys)
+    row_top = jnp.max(masked, axis=-1, keepdims=True)
+    weights = jnp.exp(masked - row_top)
+    totals = jnp.sum(weights, axis=-1, keepdims=True)
+    acc = jnp.dot(weights.astype(jnp.bfloat16), value, preferred_element_type=jnp.float32)
+    result = acc / totals
+    for head in range(heads):
+        o_ref[:, head * HD:(head + 1) * HD] = result[head * rows:(head + 1) * rows].astype(o_ref.dtype)
 
 
 def attend(first_pos, queries, pairs, window, exact, groups=None, offset=0, first=0, count=None):

time: 227 us -> 232 us (1.022)
  Pallas kernels: 31.8 us -> 36.6 us
    pallas_call x3, Pallas kernels: 22 us -> 26.7 us  [attend(): pl.pallas_call(kernel, out_shape=jax.ShapeDtypeStruct((rows, count * qblo...]
  transfers between devices with their start and end apart: 6 -> 6, of which waited for: 6 -> 5; matrix products, arithmetic and copies ran while one was open for 25% -> 25% of each run, Pallas kernels for 5% -> 5%
where the time goes in v14:
time: 232 us; the launch traced here: 231 us
  waiting for transfers between devices  110 us (47%)
  local copies, waits for them, and re-layouts  50.8 us (22%)
  Pallas kernels  36.6 us (16%)
  between operations  14.2 us (6%)
  matrix products  13.2 us (6%)
  starting transfers between devices  4.26 us (2%)
    all_gather x1, waiting for transfers between devices, body(): slab = lax.all_gather(packed[None], 'seq', axis=0, tiled=True)  62.4 us
    all_gather x1, waiting for transfers between devices, body(): lax.all_gather(shared.astype(jnp.bfloat16), 'seq', axis=0, tiled=True)  39.5 us
    pallas_call x3, Pallas kernels, attend(): pl.pallas_call(kernel, out_shape=jax.ShapeDtypeStruct((rows, count * qblo...  26.7 us
    unnamed x25, local copies, waits for them, and re-layouts  23.5 us
    pallas_call x2, Pallas kernels, project_half(): pl.pallas_call(functools.partial(_half_kernel, weight_rows=weight_rows, p...  9.88 us
    slice x1, local copies, waits for them, and re-layouts, body(): col_layout[:, :, :QPK].reshape(cross_weight.shape[0], groups * QPK * HD)  8.23 us
    dynamic_slice x1, local copies, waits for them, and re-layouts, body(): lax.dynamic_slice_in_dim(weight_kv, at, feats, 0)  6.6 us
    slice x1, local copies, waits for them, and re-layouts, body(): col_layout[:, :, QPK:].reshape(cross_weight.shape[0], groups * 2 * HD)  5.87 us
  transfers between devices with their start and end apart: 6, of which 5 were waited for; matrix products, arithmetic and copies ran while one was open for 25% of the time, Pallas kernels for 5%

profile of v14, /device:TPU:0, one launch (start us, length us, event | category | flops | bytes accessed | tf_op | source)
XLA Modules:
  0.0 231.2 jit_solution(12084686778825973628)
XLA Ops:
  7.2 0.0 copy-start
  7.2 0.0 all-gather.6.cloned.1.call-start
  7.2 1.5 reshape.40
  8.8 0.2 copy.13
  8.9 0.0 copy-done
  9.0 1.0 pad_maximum_fusion
  10.0 0.0 all-gather.6.cloned.1.call-update
  10.0 0.0 all-gather.4.cloned.1.call-start
  10.0 20.8 %copy.15 = bf16[3072,2560]{0,1:T(8,128)(2,1)} copy(bf16[3072,2560]{1,0:T(8,128)(2,1)} %param.13) | data formatting | bytes 31457280 | tf_op args[6]
  30.9 8.2 %slice.9 = bf16[3072,4,3,128]{0,3,2,1:T(8,128)(2,1)} slice(bf16[3072,4,5,128]{0,3,2,1:T(8,128)(2,1)} %bitcast.31), slice={[0:3072], [0:4], [0:3], [0:128]} | slice | bytes 18874368 | tf_op jit(solution)/shard_map/slice | solution.py:198
  39.1 5.9 %slice.8 = bf16[3072,4,2,128]{0,3,2,1:T(8,128)(2,1)} slice(bf16[3072,4,5,128]{0,3,2,1:T(8,128)(2,1)} %bitcast.32), slice={[0:3072], [0:4], [3:5], [0:128]} | slice | bytes 12582912 | tf_op jit(solution)/shard_map/slice | solution.py:197
  44.9 0.0 copy-start.2
  45.0 6.6 %constant_dynamic-slice_fusion.2 = (bf16[1536,1024]{0,1:T(8,128)(2,1)}, bf16[1536,1024]{0,1:T(8,128)(2,1)}) fusion(bf16[3072,1024]{0,1:T(8,128)(2,1)} %bitcast.34, s32[]{:T(128)S(6)} %select_n.5, s32[]{:T(128)S(6)} %select_n.4), kind=kLoop, calls=%fused_computation.27 | loop fusion | bytes 12582920 | tf_op jit(solution)/shard_map/dynamic_slice | solution.py:203
  51.6 1.2 copy-done.2
  52.8 4.8 %constant_dynamic-slice_fusion = (bf16[1536,1536]{0,1:T(8,128)(2,1)}, bf16[1536,1536]{0,1:T(8,128)(2,1)}) fusion(bf16[3072,1536]{0,1:T(8,128)(2,1)S(1)} %bitcast.33, s32[]{:T(128)S(6)} %select_n.5, s32[]{:T(128)S(6)} %select_n.4), kind=kLoop, calls=%fused_computation.25 | loop fusion | bytes 18874376 | tf_op jit(solution)/shard_map/dynamic_slice | solution.py:204
  57.5 62.4 %all-gather.6.cloned.1.call-done = bf16[53248,128]{1,0:T(8,128)(2,1)} async-done(((bf16[3328,128]{1,0:T(8,128)(2,1)}), bf16[53248,128]{1,0:T(8,128)(2,1)}) %all-gather.6.cloned.1.call-update) | async-done | bytes 13631504 | tf_op jit(solution)/shard_map/all_gather | solution.py:195
  119.9 6.8 %shard_map.87.refs_0_ = bf16[128,768]{1,0:T(8,128)(2,1)} custom-call(s32[1]{0:T(128)} %bitcast.1.pos_ref, bf16[128,1536]{1,0:T(8,128)(2,1)} %q_ref.3, bf16[16,3328,128]{2,1,0:T(8,128)(2,1)} %bitcast.25), custom_call_target="tpu_custom_call" | custom-call | tf_op jit(solution)/shard_map/pallas_call | solution.py:75
  126.7 1.5 collective-permute-start
  128.1 6.8 %shard_map.86.refs_1_ = bf16[128,768]{1,0:T(8,128)(2,1)} custom-call(s32[1]{0:T(128)} %bitcast.1.pos_ref, bf16[128,1536]{1,0:T(8,128)(2,1)} %q_ref.3, bf16[16,3328,128]{2,1,0:T(8,128)(2,1)} %bitcast.26), custom_call_target="tpu_custom_call" | custom-call | tf_op jit(solution)/shard_map/pallas_call | solution.py:75
  134.9 0.0 collective-permute-done.refs_0_
  134.9 0.0 copy-start.8
  134.9 0.6 collective-permute-start.1
  135.5 4.8 %shard_map.88.refs_4_ = f32[128,1536]{1,0:T(8,128)} custom-call(s32[1]{0:T(128)} %bitcast.10.sel_ref, bf16[128,768]{1,0:T(8,128)(2,1)} %shard_map.87.refs_0_, bf16[128,768]{1,0:T(8,128)(2,1)} %shard_map.86.refs_1_, bf16[16,3328,128]{2,1,0:T(8,128)(2,1)} %bitcast.27, bf16[16,3328,128]{2,1,0:T(8,128)(2,1)} %bitcast.28), custom_call_target="tpu_custom_call" | custom-call | tf_op jit(solution)/shard_map/pallas_call | solution.py:143
  140.3 0.0 copy-done.8
  140.3 1.6 collective-permute-done.1.refs_1_
  142.0 0.0 copy-start.9
  142.0 0.7 copy-done.9
  142.6 0.0 copy-start.10
  142.6 0.0 copy-start.11
  142.6 0.0 copy-start.4
  142.6 5.1 %shard_map.89 = bf16[128,1536]{1,0:T(8,128)(2,1)} custom-call(s32[1]{0:T(128)} %bitcast.sel_ref, bf16[128,768]{1,0:T(8,128)(2,1)} %copy-done.8, bf16[128,768]{1,0:T(8,128)(2,1)} %copy-done.9, bf16[16,3328,128]{2,1,0:T(8,128)(2,1)} %bitcast.29, bf16[16,3328,128]{2,1,0:T(8,128)(2,1)} %bitcast.30, f32[128,1536]{1,0:T(8,128)} %shard_map.88.refs_4_, ...), custom_call_target="tpu_custom_call" | custom-call | tf_op jit(solution)/shard_map/pallas_call | solution.py:143
  147.7 0.0 copy-start.3
  147.7 1.3 fusion.5
  149.0 0.6 collective-permute-start.2
  149.7 0.0 copy-done.10
  149.7 0.0 copy-done.11
  149.7 0.1 fusion.18
  149.7 1.5 collective-permute-start.3
  151.2 1.4 collective-permute-done.2
  152.7 0.0 copy-done.4
  152.7 2.1 fusion.6
  154.8 0.0 copy-start.5
  154.8 5.0 %collective-permute-done.3 = bf16[128,1536]{1,0:T(8,128)(2,1)S(1)} collective-permute-done((bf16[128,1536]{1,0:T(8,128)(2,1)}, bf16[128,1536]{1,0:T(8,128)(2,1)S(1)}, u32[]{:S(2)}, u32[]{:S(2)}) %collective-permute-start.3) | collective-permute-done | bytes 393248 | tf_op jit(solution)/shard_map/ppermute | solution.py:238
  159.8 0.0 copy-start.6
  159.8 0.7 copy-done.6
  160.6 0.0 copy-done.3
  160.6 1.9 fusion
  162.4 0.0 copy-start.7
  162.4 0.0 all-gather.4.cloned.1.call-update
  162.5 0.0 copy-done.5
  162.5 4.0 %fusion.8 = f32[128,1536]{1,0:T(8,128)S(1)} fusion(bf16[1536,1536]{0,1:T(8,128)(2,1)} %get-tuple-element.12, bf16[128,1536]{1,0:T(8,128)(2,1)S(1)} %copy-done.5, f32[1536]{0:T(1024)S(1)} %get-tuple-element.24, f32[128]{0:T(128)S(1)} %rsqrt_bitcast_fusion), kind=kOutput, calls=%fused_computation.15 | convolution fusion | flops 604766208 | bytes 5904896 | tf_op jit(solution)/shard_map/dot_general | solution.py:249
  166.5 0.0 copy-start.1
  166.5 0.0 copy-done.7
  166.5 5.1 %convolution_add_fusion.q_ref = f32[128,1536]{1,0:T(8,128)} fusion(f32[128,1536]{1,0:T(8,128)S(1)} %fusion.8, bf16[1536,1536]{0,1:T(8,128)(2,1)} %get-tuple-element.13, bf16[128,1536]{1,0:T(8,128)(2,1)S(1)} %copy-done.7, f32[1536]{0:T(1024)S(1)} %get-tuple-element.25, f32[128]{0:T(128)S(1)} %rsqrt_bitcast_fusion), kind=kOutput, calls=%fused_computation | convolution fusion | flops 604962816 | bytes 6691328 | tf_op jit(solution)/shard_map/dot_general | solution.py:252
  171.6 39.5 %all-gather.4.cloned.1.call-done.kv_ref = bf16[2048,1024]{1,0:T(8,128)(2,1)} async-done(((bf16[128,1024]{1,0:T(8,128)(2,1)}), bf16[2048,1024]{1,0:T(8,128)(2,1)}) %all-gather.4.cloned.1.call-update) | async-done | bytes 4194320 | tf_op jit(solution)/shard_map/all_gather | solution.py:248
  211.2 13.2 %shard_map.90 = bf16[128,1536]{1,0:T(8,128)(2,1)} custom-call(s32[1]{0:T(128)} %bitcast.1.pos_ref, f32[128,1536]{1,0:T(8,128)} %convolution_add_fusion.q_ref, bf16[2048,1024]{1,0:T(8,128)(2,1)} %all-gather.4.cloned.1.call-done.kv_ref), custom_call_target="tpu_custom_call" | custom-call | tf_op jit(solution)/shard_map/pallas_call | solution.py:75
  224.4 0.0 copy-done.1
  (2 shorter events, 0.1 us)
Async XLA Ops:
  7.2 1.8 copy-start
  7.2 112.7 %all-gather.6.cloned.1.call-start = ((), (), s32[]{:S(2)}) async-start(), calls=%async_computation.1 | async-start | bytes 14483456 | tf_op jit(solution)/shard_map/all_gather | solution.py:195
  10.0 201.2 %all-gather.4.cloned.1.call-start = ((), (), s32[]{:S(2)}) async-start(), calls=%async_computation | async-start | bytes 4456448 | tf_op jit(solution)/shard_map/all_gather | solution.py:248
  44.9 7.8 %copy-start.2 = (bf16[3072,4,3,128]{0,3,2,1:T(8,128)(2,1)S(1)}, bf16[3072,4,3,128]{0,3,2,1:T(8,128)(2,1)}, u32[]{:S(2)}) copy-start(bf16[3072,4,3,128]{0,3,2,1:T(8,128)(2,1)} %slice.9) | copy-start | bytes 28311556
  126.7 8.2 %collective-permute-start = (bf16[128,768]{1,0:T(8,128)(2,1)}, bf16[128,768]{1,0:T(8,128)(2,1)S(1)}, u32[]{:S(2)}, u32[]{:S(2)}) collective-permute-start(bf16[128,768]{1,0:T(8,128)(2,1)} %shard_map.87.refs_0_), channel_id=1, source_target_pairs={{0,1},{1,0},{2,3},{3,2},{4,5},{5,4},{6,7},{7,6},{8,9},{9,8},{10,11... | collective-permute-start | bytes 589832 | tf_op jit(solution)/shard_map/ppermute | solution.py:213
  134.9 5.4 %copy-start.8 = (bf16[128,768]{1,0:T(8,128)(2,1)}, bf16[128,768]{1,0:T(8,128)(2,1)S(1)}, u32[]{:S(2)}) copy-start(bf16[128,768]{1,0:T(8,128)(2,1)S(1)} %collective-permute-done.refs_0_) | copy-start | bytes 589828
  134.9 7.1 %collective-permute-start.1 = (bf16[128,768]{1,0:T(8,128)(2,1)}, bf16[128,768]{1,0:T(8,128)(2,1)S(1)}, u32[]{:S(2)}, u32[]{:S(2)}) collective-permute-start(bf16[128,768]{1,0:T(8,128)(2,1)} %shard_map.86.refs_1_), channel_id=1, source_target_pairs={{0,1},{1,0},{2,3},{3,2},{4,5},{5,4},{6,7},{7,6},{8,9},{9,8},{10,11... | collective-permute-start | bytes 589832 | tf_op jit(solution)/shard_map/ppermute | solution.py:215
  142.0 0.7 copy-start.9
  142.6 7.0 %copy-start.10 = (f32[3072]{0:T(1024)S(1)}, f32[3072]{0:T(1024)}, u32[]{:S(2)}) copy-start(f32[3072]{0:T(1024)} %param.12) | copy-start | bytes 36868
  142.6 7.0 %copy-start.11 = (f32[3072]{0:T(1024)S(1)}, f32[3072]{0:T(1024)}, u32[]{:S(2)}) copy-start(f32[3072]{0:T(1024)} %param.11) | copy-start | bytes 36868
  142.6 10.0 %copy-start.4 = (bf16[1536,1024]{0,1:T(8,128)(2,1)S(1)}, bf16[1536,1024]{0,1:T(8,128)(2,1)}, u32[]{:S(2)}) copy-start(bf16[1536,1024]{0,1:T(8,128)(2,1)} %get-tuple-element.14) | copy-start | bytes 9437188
  147.7 12.8 %copy-start.3 = (bf16[1536,1024]{0,1:T(8,128)(2,1)S(1)}, bf16[1536,1024]{0,1:T(8,128)(2,1)}, u32[]{:S(2)}) copy-start(bf16[1536,1024]{0,1:T(8,128)(2,1)} %get-tuple-element.15) | copy-start | bytes 9437188
  149.0 3.6 %collective-permute-start.2 = (f32[128,1]{0,1:T(1,128)S(1)}, f32[128,1]{0,1:T(1,128)S(1)}, u32[]{:S(2)}, u32[]{:S(2)}) collective-permute-start(f32[128,1]{0,1:T(1,128)S(1)} %bitcast.38), channel_id=1, source_target_pairs={{0,1},{1,0},{2,3},{3,2},{4,5},{5,4},{6,7},{7,6},{8,9},{9,8},{10,11... | collective-permute-start | bytes 1544 | tf_op jit(solution)/shard_map/ppermute | solution.py:237
  149.7 10.1 %collective-permute-start.3 = (bf16[128,1536]{1,0:T(8,128)(2,1)}, bf16[128,1536]{1,0:T(8,128)(2,1)S(1)}, u32[]{:S(2)}, u32[]{:S(2)}) collective-permute-start(bf16[128,1536]{1,0:T(8,128)(2,1)} %shard_map.89), channel_id=1, source_target_pairs={{0,1},{1,0},{2,3},{3,2},{4,5},{5,4},{6,7},{7,6},{8,9},{9,8},{10,11... | collective-permute-start | bytes 1179656 | tf_op jit(solution)/shard_map/ppermute | solution.py:238
  154.8 7.6 %copy-start.5 = (bf16[128,1536]{1,0:T(8,128)(2,1)S(1)}, bf16[128,1536]{1,0:T(8,128)(2,1)}, u32[]{:S(2)}) copy-start(bf16[128,1536]{1,0:T(8,128)(2,1)} %shard_map.89) | copy-start | bytes 1179652
  159.8 0.7 copy-start.6
  162.4 4.1 %copy-start.7 = (bf16[128,1536]{1,0:T(8,128)(2,1)S(1)}, bf16[128,1536]{1,0:T(8,128)(2,1)}, u32[]{:S(2)}) copy-start(bf16[128,1536]{1,0:T(8,128)(2,1)} %copy-done.6) | copy-start | bytes 1179652
  166.5 57.9 %copy-start.1 = (bf16[128,1024]{1,0:T(8,128)(2,1)S(1)}, bf16[128,1024]{1,0:T(8,128)(2,1)}, u32[]{:S(2)}) copy-start(bf16[128,1024]{1,0:T(8,128)(2,1)} %param.9) | copy-start | bytes 786436
Sparse Core Ops, SparseCore 0:
  10.3 109.5 all-gather.5
  162.6 48.5 all-gather.3

commit v15 on v12

--- a/solution.py
+++ b/solution.py
@@ -40,12 +40,14 @@
         value = kv_ref[:, HD:]
     score_scale = 1.0 / math.sqrt(HD)
     contract = (((1,), (1,)), ((), ()))
+    if exact:
+        doubled = jnp.concatenate([key, key], axis=1)
     for head in range(q_ref.shape[1] // HD):
         query = q_ref[:, head * HD:(head + 1) * HD]
         if exact:
             q_hi, q_lo = _split(query.astype(jnp.float32))
-            scores = lax.dot_general(q_hi, key, contract, preferred_element_type=jnp.float32)
-            scores = scores + lax.dot_general(q_lo, key, contract, preferred_element_type=jnp.float32)
+            both = jnp.concatenate([q_hi, q_lo], axis=1)
+            scores = lax.dot_general(both, doubled, contract, preferred_element_type=jnp.float32)
         else:
             scores = lax.dot_general(query, key, contract, preferred_element_type=jnp.float32)
         masked = scores * score_scale + bias_ref[...]

time: 227 us -> 228 us (level)
  no operation moved by 1% of the time
where the time goes in v15:
time: 228 us; the launch traced here: 227 us
  waiting for transfers between devices  109 us (48%)
  local copies, waits for them, and re-layouts  50.8 us (22%)
  Pallas kernels  32.5 us (14%)
  between operations  14.1 us (6%)
  matrix products  13.2 us (6%)
  starting transfers between devices  5.11 us (2%)
    all_gather x1, waiting for transfers between devices, body(): slab = lax.all_gather(packed[None], 'seq', axis=0, tiled=True)  62.4 us
    all_gather x1, waiting for transfers between devices, body(): lax.all_gather(shared.astype(jnp.bfloat16), 'seq', axis=0, tiled=True)  39.5 us
    unnamed x25, local copies, waits for them, and re-layouts  23.5 us
    pallas_call x3, Pallas kernels, attend(): pl.pallas_call(kernel, out_shape=jax.ShapeDtypeStruct((rows, count * qblo...  22.6 us
    pallas_call x2, Pallas kernels, project_half(): pl.pallas_call(functools.partial(_half_kernel, weight_rows=weight_rows, p...  9.89 us
    slice x1, local copies, waits for them, and re-layouts, body(): col_layout[:, :, :QPK].reshape(cross_weight.shape[0], groups * QPK * HD)  8.23 us
    dynamic_slice x1, local copies, waits for them, and re-layouts, body(): lax.dynamic_slice_in_dim(weight_kv, at, feats, 0)  6.6 us
    slice x1, local copies, waits for them, and re-layouts, body(): col_layout[:, :, QPK:].reshape(cross_weight.shape[0], groups * 2 * HD)  5.87 us
  transfers between devices with their start and end apart: 6, of which 6 were waited for; matrix products, arithmetic and copies ran while one was open for 25% of the time, Pallas kernels for 5%

profile of v15, /device:TPU:0, one launch (start us, length us, event | category | flops | bytes accessed | tf_op | source)
XLA Modules:
  0.0 226.9 jit_solution(4072390081527637113)
XLA Ops:
  7.2 0.0 copy-start
  7.2 0.0 all-gather.6.cloned.1.call-start
  7.2 1.5 reshape.40
  8.8 0.2 copy.13
  8.9 0.0 copy-done
  9.0 1.0 pad_maximum_fusion
  10.0 0.0 all-gather.6.cloned.1.call-update
  10.0 0.0 all-gather.4.cloned.1.call-start
  10.0 20.8 %copy.15 = bf16[3072,2560]{0,1:T(8,128)(2,1)} copy(bf16[3072,2560]{1,0:T(8,128)(2,1)} %param.13) | data formatting | bytes 31457280 | tf_op args[6]
  30.9 8.2 %slice.9 = bf16[3072,4,3,128]{0,3,2,1:T(8,128)(2,1)} slice(bf16[3072,4,5,128]{0,3,2,1:T(8,128)(2,1)} %bitcast.31), slice={[0:3072], [0:4], [0:3], [0:128]} | slice | bytes 18874368 | tf_op jit(solution)/shard_map/slice | solution.py:197
  39.1 5.9 %slice.8 = bf16[3072,4,2,128]{0,3,2,1:T(8,128)(2,1)} slice(bf16[3072,4,5,128]{0,3,2,1:T(8,128)(2,1)} %bitcast.32), slice={[0:3072], [0:4], [3:5], [0:128]} | slice | bytes 12582912 | tf_op jit(solution)/shard_map/slice | solution.py:196
  44.9 0.0 copy-start.2
  45.0 6.6 %constant_dynamic-slice_fusion.2 = (bf16[1536,1024]{0,1:T(8,128)(2,1)}, bf16[1536,1024]{0,1:T(8,128)(2,1)}) fusion(bf16[3072,1024]{0,1:T(8,128)(2,1)} %bitcast.34, s32[]{:T(128)S(6)} %select_n.5, s32[]{:T(128)S(6)} %select_n.4), kind=kLoop, calls=%fused_computation.27 | loop fusion | bytes 12582920 | tf_op jit(solution)/shard_map/dynamic_slice | solution.py:202
  51.6 1.2 copy-done.2
  52.8 4.8 %constant_dynamic-slice_fusion = (bf16[1536,1536]{0,1:T(8,128)(2,1)}, bf16[1536,1536]{0,1:T(8,128)(2,1)}) fusion(bf16[3072,1536]{0,1:T(8,128)(2,1)S(1)} %bitcast.33, s32[]{:T(128)S(6)} %select_n.5, s32[]{:T(128)S(6)} %select_n.4), kind=kLoop, calls=%fused_computation.25 | loop fusion | bytes 18874376 | tf_op jit(solution)/shard_map/dynamic_slice | solution.py:203
  57.5 62.4 %all-gather.6.cloned.1.call-done = bf16[53248,128]{1,0:T(8,128)(2,1)} async-done(((bf16[3328,128]{1,0:T(8,128)(2,1)}), bf16[53248,128]{1,0:T(8,128)(2,1)}) %all-gather.6.cloned.1.call-update) | async-done | bytes 13631504 | tf_op jit(solution)/shard_map/all_gather | solution.py:194
  119.9 5.6 %shard_map.87.refs_0_ = bf16[128,768]{1,0:T(8,128)(2,1)} custom-call(s32[1]{0:T(128)} %bitcast.1.pos_ref, bf16[128,1536]{1,0:T(8,128)(2,1)} %q_ref.3, bf16[16,3328,128]{2,1,0:T(8,128)(2,1)} %bitcast.25), custom_call_target="tpu_custom_call" | custom-call | tf_op jit(solution)/shard_map/pallas_call | solution.py:74
  125.5 1.5 collective-permute-start
  127.0 5.6 %shard_map.86.refs_1_ = bf16[128,768]{1,0:T(8,128)(2,1)} custom-call(s32[1]{0:T(128)} %bitcast.1.pos_ref, bf16[128,1536]{1,0:T(8,128)(2,1)} %q_ref.3, bf16[16,3328,128]{2,1,0:T(8,128)(2,1)} %bitcast.26), custom_call_target="tpu_custom_call" | custom-call | tf_op jit(solution)/shard_map/pallas_call | solution.py:74
  132.6 0.2 collective-permute-done.refs_0_
  132.8 0.0 copy-start.8
  132.8 1.5 collective-permute-start.1
  134.3 4.8 %shard_map.88.refs_4_ = f32[128,1536]{1,0:T(8,128)} custom-call(s32[1]{0:T(128)} %bitcast.10.sel_ref, bf16[128,768]{1,0:T(8,128)(2,1)} %shard_map.87.refs_0_, bf16[128,768]{1,0:T(8,128)(2,1)} %shard_map.86.refs_1_, bf16[16,3328,128]{2,1,0:T(8,128)(2,1)} %bitcast.27, bf16[16,3328,128]{2,1,0:T(8,128)(2,1)} %bitcast.28), custom_call_target="tpu_custom_call" | custom-call | tf_op jit(solution)/shard_map/pallas_call | solution.py:142
  139.1 0.0 copy-done.8
  139.1 0.6 collective-permute-done.1.refs_1_
  139.6 0.0 copy-start.9
  139.7 0.7 copy-done.9
  140.3 0.0 copy-start.10
  140.3 0.0 copy-start.11
  140.3 0.0 copy-start.4
  140.3 5.1 %shard_map.89 = bf16[128,1536]{1,0:T(8,128)(2,1)} custom-call(s32[1]{0:T(128)} %bitcast.sel_ref, bf16[128,768]{1,0:T(8,128)(2,1)} %copy-done.8, bf16[128,768]{1,0:T(8,128)(2,1)} %copy-done.9, bf16[16,3328,128]{2,1,0:T(8,128)(2,1)} %bitcast.29, bf16[16,3328,128]{2,1,0:T(8,128)(2,1)} %bitcast.30, f32[128,1536]{1,0:T(8,128)} %shard_map.88.refs_4_, ...), custom_call_target="tpu_custom_call" | custom-call | tf_op jit(solution)/shard_map/pallas_call | solution.py:142
  145.4 0.0 copy-start.3
  145.4 1.3 fusion.5
  146.7 1.1 collective-permute-start.2
  147.8 0.0 copy-done.10
  147.8 0.0 copy-done.11
  147.8 0.1 fusion.18
  147.9 1.0 collective-permute-start.3
  148.9 1.4 collective-permute-done.2
  150.4 0.0 copy-done.4
  150.4 2.1 fusion.6
  152.5 0.0 copy-start.5
  152.5 4.9 %collective-permute-done.3 = bf16[128,1536]{1,0:T(8,128)(2,1)S(1)} collective-permute-done((bf16[128,1536]{1,0:T(8,128)(2,1)}, bf16[128,1536]{1,0:T(8,128)(2,1)S(1)}, u32[]{:S(2)}, u32[]{:S(2)}) %collective-permute-start.3) | collective-permute-done | bytes 393248 | tf_op jit(solution)/shard_map/ppermute | solution.py:237
  157.4 0.0 copy-start.6
  157.4 0.7 copy-done.6
  158.2 0.0 copy-done.3
  158.2 1.9 fusion
  160.0 0.0 copy-start.7
  160.0 0.0 all-gather.4.cloned.1.call-update
  160.1 0.0 copy-done.5
  160.1 4.0 %fusion.8 = f32[128,1536]{1,0:T(8,128)S(1)} fusion(bf16[1536,1536]{0,1:T(8,128)(2,1)} %get-tuple-element.12, bf16[128,1536]{1,0:T(8,128)(2,1)S(1)} %copy-done.5, f32[1536]{0:T(1024)S(1)} %get-tuple-element.24, f32[128]{0:T(128)S(1)} %rsqrt_bitcast_fusion), kind=kOutput, calls=%fused_computation.15 | convolution fusion | flops 604766208 | bytes 5904896 | tf_op jit(solution)/shard_map/dot_general | solution.py:248
  164.1 0.0 copy-start.1
  164.1 0.0 copy-done.7
  164.1 5.1 %convolution_add_fusion.q_ref = f32[128,1536]{1,0:T(8,128)} fusion(f32[128,1536]{1,0:T(8,128)S(1)} %fusion.8, bf16[1536,1536]{0,1:T(8,128)(2,1)} %get-tuple-element.13, bf16[128,1536]{1,0:T(8,128)(2,1)S(1)} %copy-done.7, f32[1536]{0:T(1024)S(1)} %get-tuple-element.25, f32[128]{0:T(128)S(1)} %rsqrt_bitcast_fusion), kind=kOutput, calls=%fused_computation | convolution fusion | flops 604962816 | bytes 6691328 | tf_op jit(solution)/shard_map/dot_general | solution.py:251
  169.2 39.5 %all-gather.4.cloned.1.call-done.kv_ref = bf16[2048,1024]{1,0:T(8,128)(2,1)} async-done(((bf16[128,1024]{1,0:T(8,128)(2,1)}), bf16[2048,1024]{1,0:T(8,128)(2,1)}) %all-gather.4.cloned.1.call-update) | async-done | bytes 4194320 | tf_op jit(solution)/shard_map/all_gather | solution.py:247
  208.7 11.4 %shard_map.90 = bf16[128,1536]{1,0:T(8,128)(2,1)} custom-call(s32[1]{0:T(128)} %bitcast.1.pos_ref, f32[128,1536]{1,0:T(8,128)} %convolution_add_fusion.q_ref, bf16[2048,1024]{1,0:T(8,128)(2,1)} %all-gather.4.cloned.1.call-done.kv_ref), custom_call_target="tpu_custom_call" | custom-call | tf_op jit(solution)/shard_map/pallas_call | solution.py:74
  220.1 0.0 copy-done.1
  (2 shorter events, 0.1 us)
Async XLA Ops:
  7.2 1.8 copy-start
  7.2 112.7 %all-gather.6.cloned.1.call-start = ((), (), s32[]{:S(2)}) async-start(), calls=%async_computation.1 | async-start | bytes 14483456 | tf_op jit(solution)/shard_map/all_gather | solution.py:194
  10.0 198.7 %all-gather.4.cloned.1.call-start = ((), (), s32[]{:S(2)}) async-start(), calls=%async_computation | async-start | bytes 4456448 | tf_op jit(solution)/shard_map/all_gather | solution.py:247
  44.9 7.8 %copy-start.2 = (bf16[3072,4,3,128]{0,3,2,1:T(8,128)(2,1)S(1)}, bf16[3072,4,3,128]{0,3,2,1:T(8,128)(2,1)}, u32[]{:S(2)}) copy-start(bf16[3072,4,3,128]{0,3,2,1:T(8,128)(2,1)} %slice.9) | copy-start | bytes 28311556
  125.5 7.3 %collective-permute-start = (bf16[128,768]{1,0:T(8,128)(2,1)}, bf16[128,768]{1,0:T(8,128)(2,1)S(1)}, u32[]{:S(2)}, u32[]{:S(2)}) collective-permute-start(bf16[128,768]{1,0:T(8,128)(2,1)} %shard_map.87.refs_0_), channel_id=1, source_target_pairs={{0,1},{1,0},{2,3},{3,2},{4,5},{5,4},{6,7},{7,6},{8,9},{9,8},{10,11... | collective-permute-start | bytes 589832 | tf_op jit(solution)/shard_map/ppermute | solution.py:212
  132.8 6.3 %copy-start.8 = (bf16[128,768]{1,0:T(8,128)(2,1)}, bf16[128,768]{1,0:T(8,128)(2,1)S(1)}, u32[]{:S(2)}) copy-start(bf16[128,768]{1,0:T(8,128)(2,1)S(1)} %collective-permute-done.refs_0_) | copy-start | bytes 589828
  132.8 6.9 %collective-permute-start.1 = (bf16[128,768]{1,0:T(8,128)(2,1)}, bf16[128,768]{1,0:T(8,128)(2,1)S(1)}, u32[]{:S(2)}, u32[]{:S(2)}) collective-permute-start(bf16[128,768]{1,0:T(8,128)(2,1)} %shard_map.86.refs_1_), channel_id=1, source_target_pairs={{0,1},{1,0},{2,3},{3,2},{4,5},{5,4},{6,7},{7,6},{8,9},{9,8},{10,11... | collective-permute-start | bytes 589832 | tf_op jit(solution)/shard_map/ppermute | solution.py:214
  139.6 0.7 copy-start.9
  140.3 7.5 %copy-start.10 = (f32[3072]{0:T(1024)S(1)}, f32[3072]{0:T(1024)}, u32[]{:S(2)}) copy-start(f32[3072]{0:T(1024)} %param.12) | copy-start | bytes 36868
  140.3 7.5 %copy-start.11 = (f32[3072]{0:T(1024)S(1)}, f32[3072]{0:T(1024)}, u32[]{:S(2)}) copy-start(f32[3072]{0:T(1024)} %param.11) | copy-start | bytes 36868
  140.3 10.0 %copy-start.4 = (bf16[1536,1024]{0,1:T(8,128)(2,1)S(1)}, bf16[1536,1024]{0,1:T(8,128)(2,1)}, u32[]{:S(2)}) copy-start(bf16[1536,1024]{0,1:T(8,128)(2,1)} %get-tuple-element.14) | copy-start | bytes 9437188
  145.4 12.7 %copy-start.3 = (bf16[1536,1024]{0,1:T(8,128)(2,1)S(1)}, bf16[1536,1024]{0,1:T(8,128)(2,1)}, u32[]{:S(2)}) copy-start(bf16[1536,1024]{0,1:T(8,128)(2,1)} %get-tuple-element.15) | copy-start | bytes 9437188
  146.7 3.6 %collective-permute-start.2 = (f32[128,1]{0,1:T(1,128)S(1)}, f32[128,1]{0,1:T(1,128)S(1)}, u32[]{:S(2)}, u32[]{:S(2)}) collective-permute-start(f32[128,1]{0,1:T(1,128)S(1)} %bitcast.38), channel_id=1, source_target_pairs={{0,1},{1,0},{2,3},{3,2},{4,5},{5,4},{6,7},{7,6},{8,9},{9,8},{10,11... | collective-permute-start | bytes 1544 | tf_op jit(solution)/shard_map/ppermute | solution.py:236
  147.9 9.5 %collective-permute-start.3 = (bf16[128,1536]{1,0:T(8,128)(2,1)}, bf16[128,1536]{1,0:T(8,128)(2,1)S(1)}, u32[]{:S(2)}, u32[]{:S(2)}) collective-permute-start(bf16[128,1536]{1,0:T(8,128)(2,1)} %shard_map.89), channel_id=1, source_target_pairs={{0,1},{1,0},{2,3},{3,2},{4,5},{5,4},{6,7},{7,6},{8,9},{9,8},{10,11... | collective-permute-start | bytes 1179656 | tf_op jit(solution)/shard_map/ppermute | solution.py:237
  152.5 7.5 %copy-start.5 = (bf16[128,1536]{1,0:T(8,128)(2,1)S(1)}, bf16[128,1536]{1,0:T(8,128)(2,1)}, u32[]{:S(2)}) copy-start(bf16[128,1536]{1,0:T(8,128)(2,1)} %shard_map.89) | copy-start | bytes 1179652
  157.4 0.7 copy-start.6
  160.0 4.1 %copy-start.7 = (bf16[128,1536]{1,0:T(8,128)(2,1)S(1)}, bf16[128,1536]{1,0:T(8,128)(2,1)}, u32[]{:S(2)}) copy-start(bf16[128,1536]{1,0:T(8,128)(2,1)} %copy-done.6) | copy-start | bytes 1179652
  164.1 56.0 %copy-start.1 = (bf16[128,1024]{1,0:T(8,128)(2,1)S(1)}, bf16[128,1024]{1,0:T(8,128)(2,1)}, u32[]{:S(2)}) copy-start(bf16[128,1024]{1,0:T(8,128)(2,1)} %param.9) | copy-start | bytes 786436
Sparse Core Ops, SparseCore 0:
  10.3 109.5 all-gather.5
  160.2 48.4 all-gather.3

commit v16 on v12

--- a/solution.py
+++ b/solution.py
@@ -154,6 +154,27 @@
     )(which, *attended, *([slab] * count), *bases)
 
 
+def _pack_kernel(w_ref, kv_ref, o_ref):
+    w_rows = w_ref.shape[0]
+    kv_rows = kv_ref.shape[0]
+    w_blocks = w_ref.shape[1] // HD
+    for c in range(w_blocks):
+        o_ref[c * w_rows:(c + 1) * w_rows, :] = w_ref[:, c * HD:(c + 1) * HD]
+    start = w_blocks * w_rows
+    kv_start = o_ref.shape[0] - (kv_ref.shape[1] // HD) * kv_rows
+    if kv_start > start:
+        o_ref[start:kv_start, :] = jnp.zeros((kv_start - start, HD), o_ref.dtype)
+    for c in range(kv_ref.shape[1] // HD):
+        o_ref[kv_start + c * kv_rows:kv_start + (c + 1) * kv_rows, :] = kv_ref[:, c * HD:(c + 1) * HD]
+
+
+def pack(weight, pairs, total_rows):
+    return pl.pallas_call(
+        _pack_kernel,
+        out_shape=jax.ShapeDtypeStruct((total_rows, HD), weight.dtype),
+    )(weight, pairs)
+
+
 def to_slab(x):
     rows, cols = x.shape
     return x.reshape(rows, cols // HD, HD).transpose(1, 0, 2).reshape(-1, HD)
@@ -188,7 +209,9 @@
         pad = (-weight_part.shape[0]) % (2 * tok_rows)
         weight_part = jnp.pad(weight_part, ((0, pad), (0, 0)))
         offset = weight_part.shape[0] // (2 * tok_rows)
-        packed = jnp.concatenate([weight_part, to_slab(self_keys_values)], axis=0)
+        packed = pack(
+            self_out_weight, self_keys_values, weight_part.shape[0] + self_keys_values.size // HD
+        )
         slab = lax.all_gather(packed[None], "seq", axis=0, tiled=True)
         col_layout = cross_weight.reshape(cross_weight.shape[0], groups, QPK + 2, HD)
         weight_kv = col_layout[:, :, QPK:].reshape(cross_weight.shape[0], groups * 2 * HD)

time: 227 us -> 228 us (level)
    unnamed x25 -> x21, local copies, waits for them, and re-layouts: 23.5 us -> 23 us
where the time goes in v16:
time: 228 us; the launch traced here: 227 us
  waiting for transfers between devices  110 us (48%)
  local copies, waits for them, and re-layouts  49.3 us (22%)
  Pallas kernels  34 us (15%)
  between operations  14.1 us (6%)
  matrix products  13.1 us (6%)
  starting transfers between devices  5.12 us (2%)
    all_gather x1, waiting for transfers between devices, body(): slab = lax.all_gather(packed[None], 'seq', axis=0, tiled=True)  63.5 us
    all_gather x1, waiting for transfers between devices, body(): lax.all_gather(shared.astype(jnp.bfloat16), 'seq', axis=0, tiled=True)  39.5 us
    unnamed x21, local copies, waits for them, and re-layouts  23 us
    pallas_call x3, Pallas kernels, attend(): pl.pallas_call(kernel, out_shape=jax.ShapeDtypeStruct((rows, count * qblo...  22 us
    pallas_call x2, Pallas kernels, project_half(): pl.pallas_call(functools.partial(_half_kernel, weight_rows=weight_rows, p...  9.87 us
    slice x1, local copies, waits for them, and re-layouts, body(): col_layout[:, :, :QPK].reshape(cross_weight.shape[0], groups * QPK * HD)  8.23 us
    dynamic_slice x1, local copies, waits for them, and re-layouts, body(): lax.dynamic_slice_in_dim(weight_kv, at, feats, 0)  6.62 us
    slice x1, local copies, waits for them, and re-layouts, body(): col_layout[:, :, QPK:].reshape(cross_weight.shape[0], groups * 2 * HD)  5.86 us
  transfers between devices with their start and end apart: 6, of which 6 were waited for; matrix products, arithmetic and copies ran while one was open for 25% of the time, Pallas kernels for 5%

profile of v16, /device:TPU:0, one launch (start us, length us, event | category | flops | bytes accessed | tf_op | source)
XLA Modules:
  0.0 227.0 jit_solution(5762895428942255086)
XLA Ops:
  7.2 0.0 all-gather.6.cloned.1.call-start
  7.2 2.2 shard_map.86
  9.4 0.0 all-gather.6.cloned.1.call-update
  9.4 0.0 all-gather.4.cloned.1.call-start
  9.5 20.3 %copy.9 = bf16[3072,2560]{0,1:T(8,128)(2,1)} copy(bf16[3072,2560]{1,0:T(8,128)(2,1)} %param.13) | data formatting | bytes 31457280 | tf_op args[6]
  29.8 8.2 %slice.9 = bf16[3072,4,3,128]{0,3,2,1:T(8,128)(2,1)} slice(bf16[3072,4,5,128]{0,3,2,1:T(8,128)(2,1)} %bitcast.21), slice={[0:3072], [0:4], [0:3], [0:128]} | slice | bytes 18874368 | tf_op jit(solution)/shard_map/slice | solution.py:218
  38.0 5.9 %slice.8 = bf16[3072,4,2,128]{0,3,2,1:T(8,128)(2,1)} slice(bf16[3072,4,5,128]{0,3,2,1:T(8,128)(2,1)} %bitcast.22), slice={[0:3072], [0:4], [3:5], [0:128]} | slice | bytes 12582912 | tf_op jit(solution)/shard_map/slice | solution.py:217
  43.9 0.0 copy-start
  43.9 6.6 %constant_dynamic-slice_fusion.2 = (bf16[1536,1024]{0,1:T(8,128)(2,1)}, bf16[1536,1024]{0,1:T(8,128)(2,1)}) fusion(bf16[3072,1024]{0,1:T(8,128)(2,1)} %bitcast.24, s32[]{:T(128)S(6)} %select_n.5, s32[]{:T(128)S(6)} %select_n.4), kind=kLoop, calls=%fused_computation.25 | loop fusion | bytes 12582920 | tf_op jit(solution)/shard_map/dynamic_slice | solution.py:223
  50.5 1.2 copy-done
  51.7 4.7 %constant_dynamic-slice_fusion = (bf16[1536,1536]{0,1:T(8,128)(2,1)}, bf16[1536,1536]{0,1:T(8,128)(2,1)}) fusion(bf16[3072,1536]{0,1:T(8,128)(2,1)S(1)} %bitcast.23, s32[]{:T(128)S(6)} %select_n.5, s32[]{:T(128)S(6)} %select_n.4), kind=kLoop, calls=%fused_computation.23 | loop fusion | bytes 18874376 | tf_op jit(solution)/shard_map/dynamic_slice | solution.py:224
  56.4 63.5 %all-gather.6.cloned.1.call-done = bf16[53248,128]{1,0:T(8,128)(2,1)} async-done(((bf16[3328,128]{1,0:T(8,128)(2,1)}), bf16[53248,128]{1,0:T(8,128)(2,1)}) %all-gather.6.cloned.1.call-update) | async-done | bytes 13631504 | tf_op jit(solution)/shard_map/all_gather | solution.py:215
  119.9 5.6 %shard_map.88.refs_0_ = bf16[128,768]{1,0:T(8,128)(2,1)} custom-call(s32[1]{0:T(128)} %bitcast.1.pos_ref, bf16[128,1536]{1,0:T(8,128)(2,1)} %q_ref.3, bf16[16,3328,128]{2,1,0:T(8,128)(2,1)} %bitcast.15), custom_call_target="tpu_custom_call" | custom-call | tf_op jit(solution)/shard_map/pallas_call | solution.py:72
  125.5 1.5 collective-permute-start
  127.0 5.6 %shard_map.87.refs_1_ = bf16[128,768]{1,0:T(8,128)(2,1)} custom-call(s32[1]{0:T(128)} %bitcast.1.pos_ref, bf16[128,1536]{1,0:T(8,128)(2,1)} %q_ref.3, bf16[16,3328,128]{2,1,0:T(8,128)(2,1)} %bitcast.16), custom_call_target="tpu_custom_call" | custom-call | tf_op jit(solution)/shard_map/pallas_call | solution.py:72
  132.6 0.2 collective-permute-done.refs_0_
  132.8 0.0 copy-start.6
  132.8 1.5 collective-permute-start.1
  134.2 4.8 %shard_map.89.refs_4_ = f32[128,1536]{1,0:T(8,128)} custom-call(s32[1]{0:T(128)} %bitcast.6.sel_ref, bf16[128,768]{1,0:T(8,128)(2,1)} %shard_map.88.refs_0_, bf16[128,768]{1,0:T(8,128)(2,1)} %shard_map.87.refs_1_, bf16[16,3328,128]{2,1,0:T(8,128)(2,1)} %bitcast.17, bf16[16,3328,128]{2,1,0:T(8,128)(2,1)} %bitcast.18), custom_call_target="tpu_custom_call" | custom-call | tf_op jit(solution)/shard_map/pallas_call | solution.py:140
  139.1 0.0 copy-done.6
  139.1 0.6 collective-permute-done.1.refs_1_
  139.6 0.0 copy-start.7
  139.6 0.7 copy-done.7
  140.3 0.0 copy-start.2
  140.3 5.1 %shard_map.90 = bf16[128,1536]{1,0:T(8,128)(2,1)} custom-call(s32[1]{0:T(128)} %bitcast.sel_ref, bf16[128,768]{1,0:T(8,128)(2,1)} %copy-done.6, bf16[128,768]{1,0:T(8,128)(2,1)} %copy-done.7, bf16[16,3328,128]{2,1,0:T(8,128)(2,1)} %bitcast.19, bf16[16,3328,128]{2,1,0:T(8,128)(2,1)} %bitcast.20, f32[128,1536]{1,0:T(8,128)} %shard_map.89.refs_4_, ...), custom_call_target="tpu_custom_call" | custom-call | tf_op jit(solution)/shard_map/pallas_call | solution.py:140
  145.4 0.0 copy-start.1
  145.4 0.0 copy-start.3
  145.4 1.3 fusion.5
  146.7 1.1 collective-permute-start.2
  147.8 0.9 fusion.18
  148.6 1.0 collective-permute-start.3
  149.7 0.7 collective-permute-done.2
  150.3 0.0 copy-start.8
  150.3 0.0 copy-done.2
  150.3 2.1 fusion.6
  152.5 5.7 %collective-permute-done.3 = bf16[128,1536]{1,0:T(8,128)(2,1)S(1)} collective-permute-done((bf16[128,1536]{1,0:T(8,128)(2,1)}, bf16[128,1536]{1,0:T(8,128)(2,1)S(1)}, u32[]{:S(2)}, u32[]{:S(2)}) %collective-permute-start.3) | collective-permute-done | bytes 393248 | tf_op jit(solution)/shard_map/ppermute | solution.py:258
  158.2 0.0 copy-start.4
  158.2 0.0 copy-done.8
  158.2 0.7 copy-done.4
  158.9 0.0 copy-done.1
  158.9 1.9 fusion
  160.8 0.0 copy-start.5
  160.8 0.0 copy-start.9
  160.8 0.0 all-gather.4.cloned.1.call-update
  160.8 0.0 copy-done.3
  160.8 4.0 %fusion.8 = f32[128,1536]{1,0:T(8,128)S(1)} fusion(bf16[1536,1536]{0,1:T(8,128)(2,1)} %get-tuple-element.12, bf16[128,1536]{1,0:T(8,128)(2,1)S(1)} %copy-done.3, f32[1536]{0:T(1024)S(1)} %get-tuple-element.24, f32[128]{0:T(128)} %copy-done.8), kind=kOutput, calls=%fused_computation.14 | convolution fusion | flops 604766208 | bytes 5904896 | tf_op jit(solution)/shard_map/dot_general | solution.py:269
  164.9 0.0 copy-done.5
  164.9 0.0 copy-done.9
  164.9 5.1 %convolution_add_fusion.q_ref = f32[128,1536]{1,0:T(8,128)} fusion(f32[128,1536]{1,0:T(8,128)S(1)} %fusion.8, bf16[1536,1536]{0,1:T(8,128)(2,1)} %get-tuple-element.13, bf16[128,1536]{1,0:T(8,128)(2,1)S(1)} %copy-done.5, f32[1536]{0:T(1024)S(1)} %get-tuple-element.25, f32[128]{0:T(128)S(1)} %copy-done.9), kind=kOutput, calls=%fused_computation | convolution fusion | flops 604962816 | bytes 6691328 | tf_op jit(solution)/shard_map/dot_general | solution.py:272
  169.9 39.5 %all-gather.4.cloned.1.call-done.kv_ref = bf16[2048,1024]{1,0:T(8,128)(2,1)} async-done(((bf16[128,1024]{1,0:T(8,128)(2,1)}), bf16[2048,1024]{1,0:T(8,128)(2,1)}) %all-gather.4.cloned.1.call-update) | async-done | bytes 4194320 | tf_op jit(solution)/shard_map/all_gather | solution.py:268
  209.4 10.8 %shard_map.91 = bf16[128,1536]{1,0:T(8,128)(2,1)} custom-call(s32[1]{0:T(128)} %bitcast.1.pos_ref, f32[128,1536]{1,0:T(8,128)} %convolution_add_fusion.q_ref, bf16[2048,1024]{1,0:T(8,128)(2,1)} %all-gather.4.cloned.1.call-done.kv_ref), custom_call_target="tpu_custom_call" | custom-call | tf_op jit(solution)/shard_map/pallas_call | solution.py:72
  (1 shorter events, 0.0 us)
Async XLA Ops:
  7.2 112.7 %all-gather.6.cloned.1.call-start = ((), (), s32[]{:S(2)}) async-start(), calls=%async_computation.1 | async-start | bytes 14483456 | tf_op jit(solution)/shard_map/all_gather | solution.py:215
  9.4 200.0 %all-gather.4.cloned.1.call-start = ((), (), s32[]{:S(2)}) async-start(), calls=%async_computation | async-start | bytes 4456448 | tf_op jit(solution)/shard_map/all_gather | solution.py:268
  43.9 7.8 %copy-start = (bf16[3072,4,3,128]{0,3,2,1:T(8,128)(2,1)S(1)}, bf16[3072,4,3,128]{0,3,2,1:T(8,128)(2,1)}, u32[]{:S(2)}) copy-start(bf16[3072,4,3,128]{0,3,2,1:T(8,128)(2,1)} %slice.9) | copy-start | bytes 28311556
  125.5 7.3 %collective-permute-start = (bf16[128,768]{1,0:T(8,128)(2,1)}, bf16[128,768]{1,0:T(8,128)(2,1)S(1)}, u32[]{:S(2)}, u32[]{:S(2)}) collective-permute-start(bf16[128,768]{1,0:T(8,128)(2,1)} %shard_map.88.refs_0_), channel_id=1, source_target_pairs={{0,1},{1,0},{2,3},{3,2},{4,5},{5,4},{6,7},{7,6},{8,9},{9,8},{10,11... | collective-permute-start | bytes 589832 | tf_op jit(solution)/shard_map/ppermute | solution.py:233
  132.8 6.3 %copy-start.6 = (bf16[128,768]{1,0:T(8,128)(2,1)}, bf16[128,768]{1,0:T(8,128)(2,1)S(1)}, u32[]{:S(2)}) copy-start(bf16[128,768]{1,0:T(8,128)(2,1)S(1)} %collective-permute-done.refs_0_) | copy-start | bytes 589828
  132.8 6.9 %collective-permute-start.1 = (bf16[128,768]{1,0:T(8,128)(2,1)}, bf16[128,768]{1,0:T(8,128)(2,1)S(1)}, u32[]{:S(2)}, u32[]{:S(2)}) collective-permute-start(bf16[128,768]{1,0:T(8,128)(2,1)} %shard_map.87.refs_1_), channel_id=1, source_target_pairs={{0,1},{1,0},{2,3},{3,2},{4,5},{5,4},{6,7},{7,6},{8,9},{9,8},{10,11... | collective-permute-start | bytes 589832 | tf_op jit(solution)/shard_map/ppermute | solution.py:235
  139.6 0.7 copy-start.7
  140.3 10.0 %copy-start.2 = (bf16[1536,1024]{0,1:T(8,128)(2,1)S(1)}, bf16[1536,1024]{0,1:T(8,128)(2,1)}, u32[]{:S(2)}) copy-start(bf16[1536,1024]{0,1:T(8,128)(2,1)} %get-tuple-element.14) | copy-start | bytes 9437188
  145.4 13.5 %copy-start.1 = (bf16[1536,1024]{0,1:T(8,128)(2,1)S(1)}, bf16[1536,1024]{0,1:T(8,128)(2,1)}, u32[]{:S(2)}) copy-start(bf16[1536,1024]{0,1:T(8,128)(2,1)} %get-tuple-element.15) | copy-start | bytes 9437188
  145.4 15.4 %copy-start.3 = (bf16[128,1536]{1,0:T(8,128)(2,1)S(1)}, bf16[128,1536]{1,0:T(8,128)(2,1)}, u32[]{:S(2)}) copy-start(bf16[128,1536]{1,0:T(8,128)(2,1)} %shard_map.90) | copy-start | bytes 1179652
  146.7 3.6 %collective-permute-start.2 = (f32[128,1]{0,1:T(1,128)S(1)}, f32[128,1]{0,1:T(1,128)S(1)}, u32[]{:S(2)}, u32[]{:S(2)}) collective-permute-start(f32[128,1]{0,1:T(1,128)S(1)} %bitcast.25), channel_id=1, source_target_pairs={{0,1},{1,0},{2,3},{3,2},{4,5},{5,4},{6,7},{7,6},{8,9},{9,8},{10,11... | collective-permute-start | bytes 1544 | tf_op jit(solution)/shard_map/ppermute | solution.py:257
  148.6 9.5 %collective-permute-start.3 = (bf16[128,1536]{1,0:T(8,128)(2,1)}, bf16[128,1536]{1,0:T(8,128)(2,1)S(1)}, u32[]{:S(2)}, u32[]{:S(2)}) collective-permute-start(bf16[128,1536]{1,0:T(8,128)(2,1)} %shard_map.90), channel_id=1, source_target_pairs={{0,1},{1,0},{2,3},{3,2},{4,5},{5,4},{6,7},{7,6},{8,9},{9,8},{10,11... | collective-permute-start | bytes 1179656 | tf_op jit(solution)/shard_map/ppermute | solution.py:258
  150.3 7.9 %copy-start.8 = (f32[128]{0:T(128)}, f32[128]{0:T(128)S(1)}, u32[]{:S(2)}) copy-start(f32[128]{0:T(128)S(1)} %rsqrt_bitcast_fusion) | copy-start | bytes 1540
  158.2 0.7 copy-start.4
  160.8 4.1 %copy-start.5 = (bf16[128,1536]{1,0:T(8,128)(2,1)S(1)}, bf16[128,1536]{1,0:T(8,128)(2,1)}, u32[]{:S(2)}) copy-start(bf16[128,1536]{1,0:T(8,128)(2,1)} %copy-done.4) | copy-start | bytes 1179652
  160.8 4.1 %copy-start.9 = (f32[128]{0:T(128)S(1)}, f32[128]{0:T(128)}, u32[]{:S(2)}) copy-start(f32[128]{0:T(128)} %copy-done.8) | copy-start | bytes 1540
Sparse Core Ops, SparseCore 0:
  10.3 109.5 all-gather.5
  160.9 48.4 all-gather.3

commit v17 on v12

--- a/solution.py
+++ b/solution.py
@@ -96,7 +96,7 @@
 def project(attended, slab, residual, weight_rows):
     rows, width = residual.shape
     blocks = width // HD
-    per_step = next(n for n in (4, 3, 2, 1) if blocks % n == 0)
+    per_step = next(n for n in (6, 4, 3, 2, 1) if blocks % n == 0)
     return pl.pallas_call(
         functools.partial(_project_kernel, weight_rows=weight_rows),
         out_shape=jax.ShapeDtypeStruct((rows, width), jnp.bfloat16),
@@ -130,7 +130,7 @@
 def project_half(which, attended, slab, bases, weight_rows, out_dtype, width):
     rows = attended[0].shape[0]
     blocks = width // HD
-    per_step = next(n for n in (4, 3, 2, 1) if blocks % n == 0)
+    per_step = next(n for n in (6, 4, 3, 2, 1) if blocks % n == 0)
     devices = attended[0].shape[1] // weight_rows
     count = len(attended)
 

time: 227 us -> 226 us (level)
  transfers between devices with their start and end apart: 6 -> 6, of which waited for: 6 -> 6; matrix products, arithmetic and copies ran while one was open for 25% -> 26% of each run, Pallas kernels for 5% -> 4%
where the time goes in v17:
time: 226 us
  waiting for transfers between devices  110 us (49%)
  local copies, waits for them, and re-layouts  50.8 us (22%)
  Pallas kernels  30.4 us (13%)
  between operations  14.1 us (6%)
  matrix products  13.2 us (6%)
  starting transfers between devices  5.11 us (2%)
  other arithmetic  2.28 us (1%)
    all_gather x1, waiting for transfers between devices, body(): slab = lax.all_gather(packed[None], 'seq', axis=0, tiled=True)  62.4 us
    all_gather x1, waiting for transfers between devices, body(): lax.all_gather(shared.astype(jnp.bfloat16), 'seq', axis=0, tiled=True)  39.5 us
    unnamed x25, local copies, waits for them, and re-layouts  23.5 us
    pallas_call x3, Pallas kernels, attend(): pl.pallas_call(kernel, out_shape=jax.ShapeDtypeStruct((rows, count * qblo...  22 us
    pallas_call x2, Pallas kernels, project_half(): pl.pallas_call(functools.partial(_half_kernel, weight_rows=weight_rows, p...  8.44 us
    slice x1, local copies, waits for them, and re-layouts, body(): col_layout[:, :, :QPK].reshape(cross_weight.shape[0], groups * QPK * HD)  8.23 us
    dynamic_slice x1, local copies, waits for them, and re-layouts, body(): lax.dynamic_slice_in_dim(weight_kv, at, feats, 0)  6.6 us
    slice x1, local copies, waits for them, and re-layouts, body(): col_layout[:, :, QPK:].reshape(cross_weight.shape[0], groups * 2 * HD)  5.87 us
  transfers between devices with their start and end apart: 6, of which 6 were waited for; matrix products, arithmetic and copies ran while one was open for 26% of the time, Pallas kernels for 4%

profile of v17, /device:TPU:0, one launch (start us, length us, event | category | flops | bytes accessed | tf_op | source)
XLA Modules:
  0.0 225.6 jit_solution(15125738733988321986)
XLA Ops:
  7.2 0.0 copy-start
  7.2 0.0 all-gather.6.cloned.1.call-start
  7.2 1.5 reshape.40
  8.8 0.2 copy.13
  8.9 0.0 copy-done
  9.0 1.0 pad_maximum_fusion
  10.0 0.0 all-gather.6.cloned.1.call-update
  10.0 0.0 all-gather.4.cloned.1.call-start
  10.0 20.8 %copy.15 = bf16[3072,2560]{0,1:T(8,128)(2,1)} copy(bf16[3072,2560]{1,0:T(8,128)(2,1)} %param.13) | data formatting | bytes 31457280 | tf_op args[6]
  30.9 8.2 %slice.9 = bf16[3072,4,3,128]{0,3,2,1:T(8,128)(2,1)} slice(bf16[3072,4,5,128]{0,3,2,1:T(8,128)(2,1)} %bitcast.31), slice={[0:3072], [0:4], [0:3], [0:128]} | slice | bytes 18874368 | tf_op jit(solution)/shard_map/slice | solution.py:195
  39.1 5.9 %slice.8 = bf16[3072,4,2,128]{0,3,2,1:T(8,128)(2,1)} slice(bf16[3072,4,5,128]{0,3,2,1:T(8,128)(2,1)} %bitcast.32), slice={[0:3072], [0:4], [3:5], [0:128]} | slice | bytes 12582912 | tf_op jit(solution)/shard_map/slice | solution.py:194
  44.9 0.0 copy-start.2
  45.0 6.6 %constant_dynamic-slice_fusion.2 = (bf16[1536,1024]{0,1:T(8,128)(2,1)}, bf16[1536,1024]{0,1:T(8,128)(2,1)}) fusion(bf16[3072,1024]{0,1:T(8,128)(2,1)} %bitcast.34, s32[]{:T(128)S(6)} %select_n.5, s32[]{:T(128)S(6)} %select_n.4), kind=kLoop, calls=%fused_computation.27 | loop fusion | bytes 12582920 | tf_op jit(solution)/shard_map/dynamic_slice | solution.py:200
  51.6 1.2 copy-done.2
  52.8 4.8 %constant_dynamic-slice_fusion = (bf16[1536,1536]{0,1:T(8,128)(2,1)}, bf16[1536,1536]{0,1:T(8,128)(2,1)}) fusion(bf16[3072,1536]{0,1:T(8,128)(2,1)S(1)} %bitcast.33, s32[]{:T(128)S(6)} %select_n.5, s32[]{:T(128)S(6)} %select_n.4), kind=kLoop, calls=%fused_computation.25 | loop fusion | bytes 18874376 | tf_op jit(solution)/shard_map/dynamic_slice | solution.py:201
  57.5 62.4 %all-gather.6.cloned.1.call-done = bf16[53248,128]{1,0:T(8,128)(2,1)} async-done(((bf16[3328,128]{1,0:T(8,128)(2,1)}), bf16[53248,128]{1,0:T(8,128)(2,1)}) %all-gather.6.cloned.1.call-update) | async-done | bytes 13631504 | tf_op jit(solution)/shard_map/all_gather | solution.py:192
  119.9 5.6 %shard_map.87.refs_0_ = bf16[128,768]{1,0:T(8,128)(2,1)} custom-call(s32[1]{0:T(128)} %bitcast.1.pos_ref, bf16[128,1536]{1,0:T(8,128)(2,1)} %q_ref.3, bf16[16,3328,128]{2,1,0:T(8,128)(2,1)} %bitcast.25), custom_call_target="tpu_custom_call" | custom-call | tf_op jit(solution)/shard_map/pallas_call | solution.py:72
  125.5 1.5 collective-permute-start
  127.0 5.6 %shard_map.86.refs_1_ = bf16[128,768]{1,0:T(8,128)(2,1)} custom-call(s32[1]{0:T(128)} %bitcast.1.pos_ref, bf16[128,1536]{1,0:T(8,128)(2,1)} %q_ref.3, bf16[16,3328,128]{2,1,0:T(8,128)(2,1)} %bitcast.26), custom_call_target="tpu_custom_call" | custom-call | tf_op jit(solution)/shard_map/pallas_call | solution.py:72
  132.6 0.2 collective-permute-done.refs_0_
  132.8 0.0 copy-start.8
  132.8 1.5 collective-permute-start.1
  134.3 4.1 %shard_map.88.refs_4_ = f32[128,1536]{1,0:T(8,128)} custom-call(s32[1]{0:T(128)} %bitcast.10.sel_ref, bf16[128,768]{1,0:T(8,128)(2,1)} %shard_map.87.refs_0_, bf16[128,768]{1,0:T(8,128)(2,1)} %shard_map.86.refs_1_, bf16[16,3328,128]{2,1,0:T(8,128)(2,1)} %bitcast.27, bf16[16,3328,128]{2,1,0:T(8,128)(2,1)} %bitcast.28), custom_call_target="tpu_custom_call" | custom-call | tf_op jit(solution)/shard_map/pallas_call | solution.py:140
  138.3 0.0 copy-done.8
  138.3 1.3 collective-permute-done.1.refs_1_
  139.6 0.0 copy-start.9
  139.7 0.7 copy-done.9
  140.3 0.0 copy-start.10
  140.3 0.0 copy-start.11
  140.3 0.0 copy-start.4
  140.3 4.4 %shard_map.89 = bf16[128,1536]{1,0:T(8,128)(2,1)} custom-call(s32[1]{0:T(128)} %bitcast.sel_ref, bf16[128,768]{1,0:T(8,128)(2,1)} %copy-done.8, bf16[128,768]{1,0:T(8,128)(2,1)} %copy-done.9, bf16[16,3328,128]{2,1,0:T(8,128)(2,1)} %bitcast.29, bf16[16,3328,128]{2,1,0:T(8,128)(2,1)} %bitcast.30, f32[128,1536]{1,0:T(8,128)} %shard_map.88.refs_4_, ...), custom_call_target="tpu_custom_call" | custom-call | tf_op jit(solution)/shard_map/pallas_call | solution.py:140
  144.7 0.0 copy-start.3
  144.7 1.3 fusion.5
  146.0 1.1 collective-permute-start.2
  147.1 0.0 copy-done.10
  147.1 0.0 copy-done.11
  147.1 0.1 fusion.18
  147.2 1.0 collective-permute-start.3
  148.2 1.4 collective-permute-done.2
  149.7 0.0 copy-done.4
  149.7 2.1 fusion.6
  151.8 0.0 copy-start.5
  151.8 4.9 %collective-permute-done.3 = bf16[128,1536]{1,0:T(8,128)(2,1)S(1)} collective-permute-done((bf16[128,1536]{1,0:T(8,128)(2,1)}, bf16[128,1536]{1,0:T(8,128)(2,1)S(1)}, u32[]{:S(2)}, u32[]{:S(2)}) %collective-permute-start.3) | collective-permute-done | bytes 393248 | tf_op jit(solution)/shard_map/ppermute | solution.py:235
  156.7 0.0 copy-start.6
  156.7 0.7 copy-done.6
  157.5 0.0 copy-done.3
  157.5 1.9 fusion
  159.3 0.0 copy-start.7
  159.3 0.0 all-gather.4.cloned.1.call-update
  159.4 0.0 copy-done.5
  159.4 4.0 %fusion.8 = f32[128,1536]{1,0:T(8,128)S(1)} fusion(bf16[1536,1536]{0,1:T(8,128)(2,1)} %get-tuple-element.12, bf16[128,1536]{1,0:T(8,128)(2,1)S(1)} %copy-done.5, f32[1536]{0:T(1024)S(1)} %get-tuple-element.24, f32[128]{0:T(128)S(1)} %rsqrt_bitcast_fusion), kind=kOutput, calls=%fused_computation.15 | convolution fusion | flops 604766208 | bytes 5904896 | tf_op jit(solution)/shard_map/dot_general | solution.py:246
  163.4 0.0 copy-start.1
  163.4 0.0 copy-done.7
  163.4 5.1 %convolution_add_fusion.q_ref = f32[128,1536]{1,0:T(8,128)} fusion(f32[128,1536]{1,0:T(8,128)S(1)} %fusion.8, bf16[1536,1536]{0,1:T(8,128)(2,1)} %get-tuple-element.13, bf16[128,1536]{1,0:T(8,128)(2,1)S(1)} %copy-done.7, f32[1536]{0:T(1024)S(1)} %get-tuple-element.25, f32[128]{0:T(128)S(1)} %rsqrt_bitcast_fusion), kind=kOutput, calls=%fused_computation | convolution fusion | flops 604962816 | bytes 6691328 | tf_op jit(solution)/shard_map/dot_general | solution.py:249
  168.5 39.5 %all-gather.4.cloned.1.call-done.kv_ref = bf16[2048,1024]{1,0:T(8,128)(2,1)} async-done(((bf16[128,1024]{1,0:T(8,128)(2,1)}), bf16[2048,1024]{1,0:T(8,128)(2,1)}) %all-gather.4.cloned.1.call-update) | async-done | bytes 4194320 | tf_op jit(solution)/shard_map/all_gather | solution.py:245
  208.0 10.8 %shard_map.90 = bf16[128,1536]{1,0:T(8,128)(2,1)} custom-call(s32[1]{0:T(128)} %bitcast.1.pos_ref, f32[128,1536]{1,0:T(8,128)} %convolution_add_fusion.q_ref, bf16[2048,1024]{1,0:T(8,128)(2,1)} %all-gather.4.cloned.1.call-done.kv_ref), custom_call_target="tpu_custom_call" | custom-call | tf_op jit(solution)/shard_map/pallas_call | solution.py:72
  218.8 0.0 copy-done.1
  (2 shorter events, 0.1 us)
Async XLA Ops:
  7.2 1.8 copy-start
  7.2 112.7 %all-gather.6.cloned.1.call-start = ((), (), s32[]{:S(2)}) async-start(), calls=%async_computation.1 | async-start | bytes 14483456 | tf_op jit(solution)/shard_map/all_gather | solution.py:192
  10.0 198.0 %all-gather.4.cloned.1.call-start = ((), (), s32[]{:S(2)}) async-start(), calls=%async_computation | async-start | bytes 4456448 | tf_op jit(solution)/shard_map/all_gather | solution.py:245
  44.9 7.8 %copy-start.2 = (bf16[3072,4,3,128]{0,3,2,1:T(8,128)(2,1)S(1)}, bf16[3072,4,3,128]{0,3,2,1:T(8,128)(2,1)}, u32[]{:S(2)}) copy-start(bf16[3072,4,3,128]{0,3,2,1:T(8,128)(2,1)} %slice.9) | copy-start | bytes 28311556
  125.5 7.3 %collective-permute-start = (bf16[128,768]{1,0:T(8,128)(2,1)}, bf16[128,768]{1,0:T(8,128)(2,1)S(1)}, u32[]{:S(2)}, u32[]{:S(2)}) collective-permute-start(bf16[128,768]{1,0:T(8,128)(2,1)} %shard_map.87.refs_0_), channel_id=1, source_target_pairs={{0,1},{1,0},{2,3},{3,2},{4,5},{5,4},{6,7},{7,6},{8,9},{9,8},{10,11... | collective-permute-start | bytes 589832 | tf_op jit(solution)/shard_map/ppermute | solution.py:210
  132.8 5.5 %copy-start.8 = (bf16[128,768]{1,0:T(8,128)(2,1)}, bf16[128,768]{1,0:T(8,128)(2,1)S(1)}, u32[]{:S(2)}) copy-start(bf16[128,768]{1,0:T(8,128)(2,1)S(1)} %collective-permute-done.refs_0_) | copy-start | bytes 589828
  132.8 6.9 %collective-permute-start.1 = (bf16[128,768]{1,0:T(8,128)(2,1)}, bf16[128,768]{1,0:T(8,128)(2,1)S(1)}, u32[]{:S(2)}, u32[]{:S(2)}) collective-permute-start(bf16[128,768]{1,0:T(8,128)(2,1)} %shard_map.86.refs_1_), channel_id=1, source_target_pairs={{0,1},{1,0},{2,3},{3,2},{4,5},{5,4},{6,7},{7,6},{8,9},{9,8},{10,11... | collective-permute-start | bytes 589832 | tf_op jit(solution)/shard_map/ppermute | solution.py:212
  139.6 0.7 copy-start.9
  140.3 6.8 %copy-start.10 = (f32[3072]{0:T(1024)S(1)}, f32[3072]{0:T(1024)}, u32[]{:S(2)}) copy-start(f32[3072]{0:T(1024)} %param.12) | copy-start | bytes 36868
  140.3 6.8 %copy-start.11 = (f32[3072]{0:T(1024)S(1)}, f32[3072]{0:T(1024)}, u32[]{:S(2)}) copy-start(f32[3072]{0:T(1024)} %param.11) | copy-start | bytes 36868
  140.3 9.3 %copy-start.4 = (bf16[1536,1024]{0,1:T(8,128)(2,1)S(1)}, bf16[1536,1024]{0,1:T(8,128)(2,1)}, u32[]{:S(2)}) copy-start(bf16[1536,1024]{0,1:T(8,128)(2,1)} %get-tuple-element.14) | copy-start | bytes 9437188
  144.7 12.7 %copy-start.3 = (bf16[1536,1024]{0,1:T(8,128)(2,1)S(1)}, bf16[1536,1024]{0,1:T(8,128)(2,1)}, u32[]{:S(2)}) copy-start(bf16[1536,1024]{0,1:T(8,128)(2,1)} %get-tuple-element.15) | copy-start | bytes 9437188
  146.0 3.6 %collective-permute-start.2 = (f32[128,1]{0,1:T(1,128)S(1)}, f32[128,1]{0,1:T(1,128)S(1)}, u32[]{:S(2)}, u32[]{:S(2)}) collective-permute-start(f32[128,1]{0,1:T(1,128)S(1)} %bitcast.38), channel_id=1, source_target_pairs={{0,1},{1,0},{2,3},{3,2},{4,5},{5,4},{6,7},{7,6},{8,9},{9,8},{10,11... | collective-permute-start | bytes 1544 | tf_op jit(solution)/shard_map/ppermute | solution.py:234
  147.2 9.5 %collective-permute-start.3 = (bf16[128,1536]{1,0:T(8,128)(2,1)}, bf16[128,1536]{1,0:T(8,128)(2,1)S(1)}, u32[]{:S(2)}, u32[]{:S(2)}) collective-permute-start(bf16[128,1536]{1,0:T(8,128)(2,1)} %shard_map.89), channel_id=1, source_target_pairs={{0,1},{1,0},{2,3},{3,2},{4,5},{5,4},{6,7},{7,6},{8,9},{9,8},{10,11... | collective-permute-start | bytes 1179656 | tf_op jit(solution)/shard_map/ppermute | solution.py:235
  151.8 7.5 %copy-start.5 = (bf16[128,1536]{1,0:T(8,128)(2,1)S(1)}, bf16[128,1536]{1,0:T(8,128)(2,1)}, u32[]{:S(2)}) copy-start(bf16[128,1536]{1,0:T(8,128)(2,1)} %shard_map.89) | copy-start | bytes 1179652
  156.7 0.7 copy-start.6
  159.3 4.1 %copy-start.7 = (bf16[128,1536]{1,0:T(8,128)(2,1)S(1)}, bf16[128,1536]{1,0:T(8,128)(2,1)}, u32[]{:S(2)}) copy-start(bf16[128,1536]{1,0:T(8,128)(2,1)} %copy-done.6) | copy-start | bytes 1179652
  163.4 55.3 %copy-start.1 = (bf16[128,1024]{1,0:T(8,128)(2,1)S(1)}, bf16[128,1024]{1,0:T(8,128)(2,1)}, u32[]{:S(2)}) copy-start(bf16[128,1024]{1,0:T(8,128)(2,1)} %param.9) | copy-start | bytes 786436
Sparse Core Ops, SparseCore 0:
  10.3 109.5 all-gather.5
  159.5 48.4 all-gather.3

commit v18 on v17

--- a/solution.py
+++ b/solution.py
@@ -96,7 +96,7 @@
 def project(attended, slab, residual, weight_rows):
     rows, width = residual.shape
     blocks = width // HD
-    per_step = next(n for n in (6, 4, 3, 2, 1) if blocks % n == 0)
+    per_step = next(n for n in (12, 6, 4, 3, 2, 1) if blocks % n == 0)
     return pl.pallas_call(
         functools.partial(_project_kernel, weight_rows=weight_rows),
         out_shape=jax.ShapeDtypeStruct((rows, width), jnp.bfloat16),
@@ -130,7 +130,7 @@
 def project_half(which, attended, slab, bases, weight_rows, out_dtype, width):
     rows = attended[0].shape[0]
     blocks = width // HD
-    per_step = next(n for n in (6, 4, 3, 2, 1) if blocks % n == 0)
+    per_step = next(n for n in (12, 6, 4, 3, 2, 1) if blocks % n == 0)
     devices = attended[0].shape[1] // weight_rows
     count = len(attended)
 

time: 226 us -> 227 us (level)
  transfers between devices with their start and end apart: 6 -> 6, of which waited for: 6 -> 6; matrix products, arithmetic and copies ran while one was open for 26% -> 25% of each run, Pallas kernels for 4% -> 5%
where the time goes in v18:
time: 227 us; the launch traced here: 226 us
  waiting for transfers between devices  109 us (48%)
  local copies, waits for them, and re-layouts  50.8 us (22%)
  Pallas kernels  32 us (14%)
  between operations  14.1 us (6%)
  matrix products  13.2 us (6%)
  starting transfers between devices  5.12 us (2%)
  other arithmetic  2.28 us (1%)
    all_gather x1, waiting for transfers between devices, body(): slab = lax.all_gather(packed[None], 'seq', axis=0, tiled=True)  62.4 us
    all_gather x1, waiting for transfers between devices, body(): lax.all_gather(shared.astype(jnp.bfloat16), 'seq', axis=0, tiled=True)  39.4 us
    unnamed x25, local copies, waits for them, and re-layouts  23.5 us
    pallas_call x3, Pallas kernels, attend(): pl.pallas_call(kernel, out_shape=jax.ShapeDtypeStruct((rows, count * qblo...  22 us
    pallas_call x2, Pallas kernels, project_half(): pl.pallas_call(functools.partial(_half_kernel, weight_rows=weight_rows, p...  10 us
    slice x1, local copies, waits for them, and re-layouts, body(): col_layout[:, :, :QPK].reshape(cross_weight.shape[0], groups * QPK * HD)  8.23 us
    dynamic_slice x1, local copies, waits for them, and re-layouts, body(): lax.dynamic_slice_in_dim(weight_kv, at, feats, 0)  6.6 us
    slice x1, local copies, waits for them, and re-layouts, body(): col_layout[:, :, QPK:].reshape(cross_weight.shape[0], groups * 2 * HD)  5.87 us
  transfers between devices with their start and end apart: 6, of which 6 were waited for; matrix products, arithmetic and copies ran while one was open for 25% of the time, Pallas kernels for 5%

profile of v18, /device:TPU:0, one launch (start us, length us, event | category | flops | bytes accessed | tf_op | source)
XLA Modules:
  0.0 226.4 jit_solution(5449705740228676782)
XLA Ops:
  7.2 0.0 copy-start
  7.2 0.0 all-gather.6.cloned.1.call-start
  7.2 1.5 reshape.40
  8.8 0.2 copy.13
  8.9 0.0 copy-done
  9.0 1.0 pad_maximum_fusion
  10.0 0.0 all-gather.6.cloned.1.call-update
  10.0 0.0 all-gather.4.cloned.1.call-start
  10.0 20.8 %copy.15 = bf16[3072,2560]{0,1:T(8,128)(2,1)} copy(bf16[3072,2560]{1,0:T(8,128)(2,1)} %param.13) | data formatting | bytes 31457280 | tf_op args[6]
  30.9 8.2 %slice.9 = bf16[3072,4,3,128]{0,3,2,1:T(8,128)(2,1)} slice(bf16[3072,4,5,128]{0,3,2,1:T(8,128)(2,1)} %bitcast.31), slice={[0:3072], [0:4], [0:3], [0:128]} | slice | bytes 18874368 | tf_op jit(solution)/shard_map/slice | solution.py:195
  39.1 5.9 %slice.8 = bf16[3072,4,2,128]{0,3,2,1:T(8,128)(2,1)} slice(bf16[3072,4,5,128]{0,3,2,1:T(8,128)(2,1)} %bitcast.32), slice={[0:3072], [0:4], [3:5], [0:128]} | slice | bytes 12582912 | tf_op jit(solution)/shard_map/slice | solution.py:194
  44.9 0.0 copy-start.2
  45.0 6.6 %constant_dynamic-slice_fusion.2 = (bf16[1536,1024]{0,1:T(8,128)(2,1)}, bf16[1536,1024]{0,1:T(8,128)(2,1)}) fusion(bf16[3072,1024]{0,1:T(8,128)(2,1)} %bitcast.34, s32[]{:T(128)S(6)} %select_n.5, s32[]{:T(128)S(6)} %select_n.4), kind=kLoop, calls=%fused_computation.27 | loop fusion | bytes 12582920 | tf_op jit(solution)/shard_map/dynamic_slice | solution.py:200
  51.6 1.2 copy-done.2
  52.8 4.8 %constant_dynamic-slice_fusion = (bf16[1536,1536]{0,1:T(8,128)(2,1)}, bf16[1536,1536]{0,1:T(8,128)(2,1)}) fusion(bf16[3072,1536]{0,1:T(8,128)(2,1)S(1)} %bitcast.33, s32[]{:T(128)S(6)} %select_n.5, s32[]{:T(128)S(6)} %select_n.4), kind=kLoop, calls=%fused_computation.25 | loop fusion | bytes 18874376 | tf_op jit(solution)/shard_map/dynamic_slice | solution.py:201
  57.5 62.4 %all-gather.6.cloned.1.call-done = bf16[53248,128]{1,0:T(8,128)(2,1)} async-done(((bf16[3328,128]{1,0:T(8,128)(2,1)}), bf16[53248,128]{1,0:T(8,128)(2,1)}) %all-gather.6.cloned.1.call-update) | async-done | bytes 13631504 | tf_op jit(solution)/shard_map/all_gather | solution.py:192
  119.9 5.6 %shard_map.87.refs_0_ = bf16[128,768]{1,0:T(8,128)(2,1)} custom-call(s32[1]{0:T(128)} %bitcast.1.pos_ref, bf16[128,1536]{1,0:T(8,128)(2,1)} %q_ref.3, bf16[16,3328,128]{2,1,0:T(8,128)(2,1)} %bitcast.25), custom_call_target="tpu_custom_call" | custom-call | tf_op jit(solution)/shard_map/pallas_call | solution.py:72
  125.5 1.5 collective-permute-start
  127.0 5.6 %shard_map.86.refs_1_ = bf16[128,768]{1,0:T(8,128)(2,1)} custom-call(s32[1]{0:T(128)} %bitcast.1.pos_ref, bf16[128,1536]{1,0:T(8,128)(2,1)} %q_ref.3, bf16[16,3328,128]{2,1,0:T(8,128)(2,1)} %bitcast.26), custom_call_target="tpu_custom_call" | custom-call | tf_op jit(solution)/shard_map/pallas_call | solution.py:72
  132.6 0.2 collective-permute-done.refs_0_
  132.8 0.0 copy-start.8
  132.8 1.5 collective-permute-start.1
  134.3 4.9 %shard_map.88.refs_4_ = f32[128,1536]{1,0:T(8,128)} custom-call(s32[1]{0:T(128)} %bitcast.10.sel_ref, bf16[128,768]{1,0:T(8,128)(2,1)} %shard_map.87.refs_0_, bf16[128,768]{1,0:T(8,128)(2,1)} %shard_map.86.refs_1_, bf16[16,3328,128]{2,1,0:T(8,128)(2,1)} %bitcast.27, bf16[16,3328,128]{2,1,0:T(8,128)(2,1)} %bitcast.28), custom_call_target="tpu_custom_call" | custom-call | tf_op jit(solution)/shard_map/pallas_call | solution.py:140
  139.2 0.0 copy-done.8
  139.2 0.5 collective-permute-done.1.refs_1_
  139.7 0.0 copy-start.9
  139.7 0.7 copy-done.9
  140.3 0.0 copy-start.10
  140.3 0.0 copy-start.11
  140.3 0.0 copy-start.4
  140.3 5.1 %shard_map.89 = bf16[128,1536]{1,0:T(8,128)(2,1)} custom-call(s32[1]{0:T(128)} %bitcast.sel_ref, bf16[128,768]{1,0:T(8,128)(2,1)} %copy-done.8, bf16[128,768]{1,0:T(8,128)(2,1)} %copy-done.9, bf16[16,3328,128]{2,1,0:T(8,128)(2,1)} %bitcast.29, bf16[16,3328,128]{2,1,0:T(8,128)(2,1)} %bitcast.30, f32[128,1536]{1,0:T(8,128)} %shard_map.88.refs_4_, ...), custom_call_target="tpu_custom_call" | custom-call | tf_op jit(solution)/shard_map/pallas_call | solution.py:140
  145.4 0.0 copy-start.3
  145.4 1.3 fusion.5
  146.8 1.1 collective-permute-start.2
  147.8 0.0 copy-done.10
  147.8 0.0 copy-done.11
  147.8 0.1 fusion.18
  147.9 1.0 collective-permute-start.3
  148.9 1.4 collective-permute-done.2
  150.4 0.0 copy-done.4
  150.4 2.1 fusion.6
  152.5 0.0 copy-start.5
  152.6 5.0 %collective-permute-done.3 = bf16[128,1536]{1,0:T(8,128)(2,1)S(1)} collective-permute-done((bf16[128,1536]{1,0:T(8,128)(2,1)}, bf16[128,1536]{1,0:T(8,128)(2,1)S(1)}, u32[]{:S(2)}, u32[]{:S(2)}) %collective-permute-start.3) | collective-permute-done | bytes 393248 | tf_op jit(solution)/shard_map/ppermute | solution.py:235
  157.5 0.0 copy-start.6
  157.5 0.7 copy-done.6
  158.3 0.0 copy-done.3
  158.3 1.9 fusion
  160.1 0.0 copy-start.7
  160.1 0.0 all-gather.4.cloned.1.call-update
  160.2 0.0 copy-done.5
  160.2 4.0 %fusion.8 = f32[128,1536]{1,0:T(8,128)S(1)} fusion(bf16[1536,1536]{0,1:T(8,128)(2,1)} %get-tuple-element.12, bf16[128,1536]{1,0:T(8,128)(2,1)S(1)} %copy-done.5, f32[1536]{0:T(1024)S(1)} %get-tuple-element.24, f32[128]{0:T(128)S(1)} %rsqrt_bitcast_fusion), kind=kOutput, calls=%fused_computation.15 | convolution fusion | flops 604766208 | bytes 5904896 | tf_op jit(solution)/shard_map/dot_general | solution.py:246
  164.2 0.0 copy-start.1
  164.2 0.0 copy-done.7
  164.2 5.1 %convolution_add_fusion.q_ref = f32[128,1536]{1,0:T(8,128)} fusion(f32[128,1536]{1,0:T(8,128)S(1)} %fusion.8, bf16[1536,1536]{0,1:T(8,128)(2,1)} %get-tuple-element.13, bf16[128,1536]{1,0:T(8,128)(2,1)S(1)} %copy-done.7, f32[1536]{0:T(1024)S(1)} %get-tuple-element.25, f32[128]{0:T(128)S(1)} %rsqrt_bitcast_fusion), kind=kOutput, calls=%fused_computation | convolution fusion | flops 604962816 | bytes 6691328 | tf_op jit(solution)/shard_map/dot_general | solution.py:249
  169.4 39.4 %all-gather.4.cloned.1.call-done.kv_ref = bf16[2048,1024]{1,0:T(8,128)(2,1)} async-done(((bf16[128,1024]{1,0:T(8,128)(2,1)}), bf16[2048,1024]{1,0:T(8,128)(2,1)}) %all-gather.4.cloned.1.call-update) | async-done | bytes 4194320 | tf_op jit(solution)/shard_map/all_gather | solution.py:245
  208.8 10.8 %shard_map.90 = bf16[128,1536]{1,0:T(8,128)(2,1)} custom-call(s32[1]{0:T(128)} %bitcast.1.pos_ref, f32[128,1536]{1,0:T(8,128)} %convolution_add_fusion.q_ref, bf16[2048,1024]{1,0:T(8,128)(2,1)} %all-gather.4.cloned.1.call-done.kv_ref), custom_call_target="tpu_custom_call" | custom-call | tf_op jit(solution)/shard_map/pallas_call | solution.py:72
  219.5 0.0 copy-done.1
  (2 shorter events, 0.1 us)
Async XLA Ops:
  7.2 1.8 copy-start
  7.2 112.7 %all-gather.6.cloned.1.call-start = ((), (), s32[]{:S(2)}) async-start(), calls=%async_computation.1 | async-start | bytes 14483456 | tf_op jit(solution)/shard_map/all_gather | solution.py:192
  10.0 198.8 %all-gather.4.cloned.1.call-start = ((), (), s32[]{:S(2)}) async-start(), calls=%async_computation | async-start | bytes 4456448 | tf_op jit(solution)/shard_map/all_gather | solution.py:245
  44.9 7.8 %copy-start.2 = (bf16[3072,4,3,128]{0,3,2,1:T(8,128)(2,1)S(1)}, bf16[3072,4,3,128]{0,3,2,1:T(8,128)(2,1)}, u32[]{:S(2)}) copy-start(bf16[3072,4,3,128]{0,3,2,1:T(8,128)(2,1)} %slice.9) | copy-start | bytes 28311556
  125.5 7.3 %collective-permute-start = (bf16[128,768]{1,0:T(8,128)(2,1)}, bf16[128,768]{1,0:T(8,128)(2,1)S(1)}, u32[]{:S(2)}, u32[]{:S(2)}) collective-permute-start(bf16[128,768]{1,0:T(8,128)(2,1)} %shard_map.87.refs_0_), channel_id=1, source_target_pairs={{0,1},{1,0},{2,3},{3,2},{4,5},{5,4},{6,7},{7,6},{8,9},{9,8},{10,11... | collective-permute-start | bytes 589832 | tf_op jit(solution)/shard_map/ppermute | solution.py:210
  132.8 6.4 %copy-start.8 = (bf16[128,768]{1,0:T(8,128)(2,1)}, bf16[128,768]{1,0:T(8,128)(2,1)S(1)}, u32[]{:S(2)}) copy-start(bf16[128,768]{1,0:T(8,128)(2,1)S(1)} %collective-permute-done.refs_0_) | copy-start | bytes 589828
  132.8 6.9 %collective-permute-start.1 = (bf16[128,768]{1,0:T(8,128)(2,1)}, bf16[128,768]{1,0:T(8,128)(2,1)S(1)}, u32[]{:S(2)}, u32[]{:S(2)}) collective-permute-start(bf16[128,768]{1,0:T(8,128)(2,1)} %shard_map.86.refs_1_), channel_id=1, source_target_pairs={{0,1},{1,0},{2,3},{3,2},{4,5},{5,4},{6,7},{7,6},{8,9},{9,8},{10,11... | collective-permute-start | bytes 589832 | tf_op jit(solution)/shard_map/ppermute | solution.py:212
  139.7 0.7 copy-start.9
  140.3 7.5 %copy-start.10 = (f32[3072]{0:T(1024)S(1)}, f32[3072]{0:T(1024)}, u32[]{:S(2)}) copy-start(f32[3072]{0:T(1024)} %param.12) | copy-start | bytes 36868
  140.3 7.5 %copy-start.11 = (f32[3072]{0:T(1024)S(1)}, f32[3072]{0:T(1024)}, u32[]{:S(2)}) copy-start(f32[3072]{0:T(1024)} %param.11) | copy-start | bytes 36868
  140.3 10.1 %copy-start.4 = (bf16[1536,1024]{0,1:T(8,128)(2,1)S(1)}, bf16[1536,1024]{0,1:T(8,128)(2,1)}, u32[]{:S(2)}) copy-start(bf16[1536,1024]{0,1:T(8,128)(2,1)} %get-tuple-element.14) | copy-start | bytes 9437188
  145.4 12.8 %copy-start.3 = (bf16[1536,1024]{0,1:T(8,128)(2,1)S(1)}, bf16[1536,1024]{0,1:T(8,128)(2,1)}, u32[]{:S(2)}) copy-start(bf16[1536,1024]{0,1:T(8,128)(2,1)} %get-tuple-element.15) | copy-start | bytes 9437188
  146.8 3.6 %collective-permute-start.2 = (f32[128,1]{0,1:T(1,128)S(1)}, f32[128,1]{0,1:T(1,128)S(1)}, u32[]{:S(2)}, u32[]{:S(2)}) collective-permute-start(f32[128,1]{0,1:T(1,128)S(1)} %bitcast.38), channel_id=1, source_target_pairs={{0,1},{1,0},{2,3},{3,2},{4,5},{5,4},{6,7},{7,6},{8,9},{9,8},{10,11... | collective-permute-start | bytes 1544 | tf_op jit(solution)/shard_map/ppermute | solution.py:234
  147.9 9.6 %collective-permute-start.3 = (bf16[128,1536]{1,0:T(8,128)(2,1)}, bf16[128,1536]{1,0:T(8,128)(2,1)S(1)}, u32[]{:S(2)}, u32[]{:S(2)}) collective-permute-start(bf16[128,1536]{1,0:T(8,128)(2,1)} %shard_map.89), channel_id=1, source_target_pairs={{0,1},{1,0},{2,3},{3,2},{4,5},{5,4},{6,7},{7,6},{8,9},{9,8},{10,11... | collective-permute-start | bytes 1179656 | tf_op jit(solution)/shard_map/ppermute | solution.py:235
  152.5 7.6 %copy-start.5 = (bf16[128,1536]{1,0:T(8,128)(2,1)S(1)}, bf16[128,1536]{1,0:T(8,128)(2,1)}, u32[]{:S(2)}) copy-start(bf16[128,1536]{1,0:T(8,128)(2,1)} %shard_map.89) | copy-start | bytes 1179652
  157.5 0.7 copy-start.6
  160.1 4.1 %copy-start.7 = (bf16[128,1536]{1,0:T(8,128)(2,1)S(1)}, bf16[128,1536]{1,0:T(8,128)(2,1)}, u32[]{:S(2)}) copy-start(bf16[128,1536]{1,0:T(8,128)(2,1)} %copy-done.6) | copy-start | bytes 1179652
  164.2 55.3 %copy-start.1 = (bf16[128,1024]{1,0:T(8,128)(2,1)S(1)}, bf16[128,1024]{1,0:T(8,128)(2,1)}, u32[]{:S(2)}) copy-start(bf16[128,1024]{1,0:T(8,128)(2,1)} %param.9) | copy-start | bytes 786436
Sparse Core Ops, SparseCore 0:
  10.3 109.5 all-gather.5
  160.3 48.4 all-gather.3
